TPU v7x, 256 devices: a whole 4x4x8 slice. The times are simulated.
256 devices in a mesh: dp: 64 (over y, z_lo, x), tensor: 4 (over z_hi, core).
Axes of the slice: x: 4, y: 4, z: 8 (z_hi: 2, z_lo: 4; z = z_hi * 4 + z_lo), core: 2. Of those that a mesh axis runs over, the one named last changes fastest.
Arguments:
- tokens: bfloat16 [16384, 8192], P('dp', 'tensor'), may hold values from -160 to 160
- weights: bfloat16 [3, 512, 32, 256], P(None, None, 'tensor'), may hold values from -0.25 to 0.25
- cotangent: bfloat16 [16384, 8192], P('dp', 'tensor'), may hold values from -6 to 6
Outputs:
- mixed: bfloat16 [16384, 8192], P('dp', 'tensor')
- token_grads: bfloat16 [16384, 8192], P('dp', 'tensor')
- weight_grads: float32 [3, 512, 32, 256], P(None, 'dp', 'tensor')
All inputs are finite; a program needn't handle non-finite values.
Results may differ from a plain program's by a relative error of at most 0.0014.
The roundings to bfloat16 on the way count: a program that leaves them out, or rounds other values in their place, can miss the bound.
Values may be sent and summed in bfloat16 or wider, within the bound.
No kernel may reach another device: no remote copies, remote signals or barrier semaphores. Data moves between devices by JAX's collectives and lax.ppermute only.
A program may use at most 128 MiB of HBM per device.

v0:
```python
import math

import jax
import jax.numpy as jnp
from jax import lax
from jax.sharding import PartitionSpec as P

D = 8192
BLK = 256
FACTORS = 3


root_half = 0.7071067811865476
pdf_scale = 0.3989422804014327
epsilon = 1e-06


def swapped(x, axis, stride):
    return lax.ppermute(x, axis, [(i, i ^ 1 << stride) for i in range(lax.axis_size(axis))])


def gelu_value(value):
    return value * (0.5 * (1.0 + lax.erf(value * root_half)))


def gelu_slope(value):
    return (
        0.5 * (1.0 + lax.erf(value * root_half)) + value * jnp.exp(-0.5 * value * value) * pdf_scale
    )


def local_partner(blocks, stride):
    tok_rows, block_count, width = blocks.shape
    folded = blocks.reshape(tok_rows, block_count // (2 * stride), 2, stride, width)
    return jnp.flip(folded, axis=2).reshape(tok_rows, block_count, width)


def apply_factor(hidden, partner, layer_weights):
    preact = jnp.einsum(
        "tbc,cbd->tbd", hidden, layer_weights[:BLK], preferred_element_type=jnp.float32
    )
    return preact + jnp.einsum(
        "tbc,cbd->tbd", partner, layer_weights[BLK:], preferred_element_type=jnp.float32
    )


def shards(tokens, weights, cotangent):
    tok_rows, local_width = tokens.shape
    blocks_dev = local_width // BLK
    block_bits = (D // BLK).bit_length() - 1
    device_bits = blocks_dev.bit_length() - 1
    data_size = lax.axis_size("dp")
    grad_scale = 1.0 / math.sqrt(tok_rows * data_size)
    tokens_f32 = tokens.astype(jnp.float32)
    square_sum = lax.psum(jnp.sum(tokens_f32 * tokens_f32, axis=1), "tensor")
    inv_rms = lax.rsqrt(square_sum / D + epsilon)[:, None]
    normed = tokens_f32 * inv_rms
    hidden = normed.astype(jnp.bfloat16).reshape(tok_rows, blocks_dev, BLK)
    stored_inputs = []
    stored_preact = []
    preact = None
    for factor in range(FACTORS):
        bit_index = block_bits - FACTORS + factor
        stride = 1 << bit_index
        if stride < blocks_dev:
            partner = local_partner(hidden, stride)
        else:
            partner = swapped(hidden, "tensor", bit_index - device_bits)
        preact = apply_factor(hidden, partner, weights[factor])
        stored_inputs.append((hidden, partner))
        stored_preact.append(preact)
        if factor < FACTORS - 1:
            hidden = gelu_value(preact).astype(jnp.bfloat16)
    mixed = (tokens_f32 + preact.reshape(tok_rows, local_width)).astype(jnp.bfloat16)
    grad_pre = cotangent.reshape(tok_rows, blocks_dev, BLK)
    grad_terms = []
    grad_hidden = None
    for factor in reversed(range(FACTORS)):
        bit_index = block_bits - FACTORS + factor
        stride = 1 << bit_index
        kept_hidden, kept_partner = stored_inputs[factor]
        joined = jnp.concatenate([kept_hidden, kept_partner], axis=2)
        grad_terms.append(
            jnp.einsum("tbc,tbd->cbd", joined, grad_pre, preferred_element_type=jnp.float32)
            * grad_scale
        )
        layer_weights = weights[factor]
        near_term = jnp.einsum(
            "tbd,cbd->tbc", grad_pre, layer_weights[:BLK], preferred_element_type=jnp.float32
        )
        far_term = jnp.einsum(
            "tbd,cbd->tbc", grad_pre, layer_weights[BLK:], preferred_element_type=jnp.float32
        )
        if stride < blocks_dev:
            arrived = local_partner(far_term, stride)
        else:
            arrived = swapped(far_term, "tensor", bit_index - device_bits)
        grad_hidden = near_term + arrived
        if factor > 0:
            previous = stored_preact[factor - 1]
            grad_pre = (grad_hidden * gelu_slope(previous)).astype(jnp.bfloat16)
    flat = grad_hidden.reshape(tok_rows, local_width)
    inner_sum = lax.psum(jnp.sum(flat * normed, axis=1), "tensor")
    token_grads = (
        cotangent.astype(jnp.float32) + inv_rms * (flat - normed * (inner_sum / D)[:, None])
    ).astype(jnp.bfloat16)
    weight_grads = lax.psum_scatter(
        jnp.stack(grad_terms[::-1]), "dp", scatter_dimension=1, tiled=True
    )
    return (mixed, token_grads, weight_grads)


def solution(mesh):
    return jax.shard_map(
        shards,
        mesh=mesh,
        in_specs=(P("dp", "tensor"), P(None, None, "tensor", None), P("dp", "tensor")),
        out_specs=(P("dp", "tensor"), P("dp", "tensor"), P(None, "dp", "tensor", None)),
        check_vma=False,
    )
```

profile of v0, /device:TPU:2, one launch (start us, length us, event | category | flops | bytes accessed | tf_op | source)
XLA Modules:
  0.0 632.7 jit_solution(5617616283579790947)
XLA Ops:
  7.2 0.0 reduce-scatter.2.cloned.1.call-start
  7.2 5.2 fusion.67
  12.4 0.8 copy.136
  13.2 0.4 copy-done.1
  13.7 1.8 convolution_bitcast_fusion.1
  15.5 7.2 %collective-permute-start.2 = (f32[256,8,256]{0,2,1:T(8,128)}, f32[256,8,256]{0,2,1:T(8,128)}, u32[]{:S(2)}, u32[]{:S(2)}) collective-permute-start(f32[256,8,256]{0,2,1:T(8,128)} %convolution_bitcast_fusion.1), channel_id=1, source_target_pairs={{0,2},{1,3},{2,0},{3,1},{4,6},{5,7},{6,4},{7,5},{8,10},{9,11},{10,... | collective-permute-start | bytes 6291464 | tf_op jit(solution)/shard_map/ppermute | solution.py:19
  22.7 0.0 copy-done.21
  22.7 0.5 copy.75
  23.2 0.3 fusion.8
  23.5 96.6 %psum.14 = f32[256]{0:T(256)S(1)} all-reduce(f32[256]{0:T(256)S(1)} %fusion.8), channel_id=1, replica_groups=mesh['dp'=64,'tensor'=4] {'tensor'}, use_global_device_ids=true, to_apply=%region_1.0 | all-reduce | flops 256 | bytes 2048 | tf_op jit(solution)/shard_map/psum | solution.py:55
  120.2 0.2 fusion.2
  120.4 1.3 copy.78
  121.7 1.3 rev.8
  123.0 2.8 copy.134
  125.8 2.4 copy.133
  128.2 0.0 copy-done.6
  128.2 1.8 fusion.57
  130.0 2.0 fusion.38
  132.1 0.0 collective-permute-start
  132.1 2.9 copy.135
  134.9 2.4 copy.132
  137.3 2.4 copy.131
  139.8 1.7 fusion.51
  141.5 0.0 copy-start.2
  141.5 0.0 collective-permute-done
  141.6 0.0 copy-done.8
  141.6 2.0 fusion.34
  143.6 0.0 collective-permute-done.2
  143.6 0.0 copy-done.2
  143.6 0.0 copy-done.18
  143.6 2.6 fusion.15
  146.2 0.0 copy-start.16
  146.2 1.9 convolution_bitcast_fusion
  148.1 0.1 collective-permute-start.3
  148.2 0.0 collective-permute-start.1
  148.3 1.3 copy.104
  149.6 2.7 multiply_bitcast_fusion.1
  152.3 0.0 copy-start.19
  152.3 47.6 %collective-permute-done.1 = bf16[256,8,256]{0,2,1:T(8,128)(2,1)} collective-permute-done((bf16[256,8,256]{0,2,1:T(8,128)(2,1)S(1)}, bf16[256,8,256]{0,2,1:T(8,128)(2,1)}, u32[]{:S(2)}, u32[]{:S(2)}) %collective-permute-start.1) | collective-permute-done | bytes 1048608 | tf_op jit(solution)/shard_map/ppermute | solution.py:19
  199.9 3.9 multiply_bitcast_fusion
  203.9 0.0 collective-permute-done.3
  203.9 2.7 fusion.21
  206.6 0.0 copy-start.9
  206.6 1.0 copy-done.9
  207.6 2.7 multiply_bitcast_fusion.2
  210.3 10.0 %pad_maximum_fusion = f32[3,512,8,256]{1,3,2,0:T(8,128)} fusion(f32[1,512,8,256]{1,3,2,0:T(8,128)} %multiply_bitcast_fusion, f32[1,512,8,256]{1,3,2,0:T(8,128)S(1)} %multiply_bitcast_fusion.1, f32[1,512,8,256]{1,3,2,0:T(8,128)} %multiply_bitcast_fusion.2), kind=kLoop, calls=%fused_computation | loop fusion | flops 6291456 | bytes 25165824 | tf_op jit(solution)/shard_map/stack | solution.py:108
  220.3 12.8 %copy.108 = f32[3,512,8,256]{3,2,0,1:T(8,128)} copy(f32[3,512,8,256]{1,3,2,0:T(8,128)} %pad_maximum_fusion) | data formatting | bytes 25165824 | tf_op jit(solution)/shard_map/stack | solution.py:108
  233.1 0.0 reduce-scatter.2.cloned.1.call-update
  233.1 1.2 copy-done.4
  234.3 1.3 copy.88
  235.6 1.7 fusion.45
  237.4 0.0 copy-start.10
  237.4 3.2 convolution_add_fusion
  240.6 0.5 fusion.55
  241.1 1.8 copy.103
  242.9 3.1 rev.9
  246.0 2.7 bitcast_add_fusion
  248.7 0.3 fusion.3
  249.1 9.7 %psum.15 = f32[256]{0:T(256)S(1)} all-reduce(f32[256]{0:T(256)S(1)} %fusion.3), channel_id=1, replica_groups=mesh['dp'=64,'tensor'=4] {'tensor'}, use_global_device_ids=true, to_apply=%region_3.4 | all-reduce | flops 256 | bytes 2048 | tf_op jit(solution)/shard_map/psum | solution.py:103
  258.7 4.1 fusion.7
  262.8 2.4 copy.110
  265.2 1.4 copy.109
  266.6 357.6 %reduce-scatter.2.cloned.1.call-done = f32[3,8,8,256]{3,2,0,1:T(8,128)} async-done(((f32[3,512,8,256]{3,2,0,1:T(8,128)}), f32[3,8,8,256]{3,2,0,1:T(8,128)}) %reduce-scatter.2.cloned.1.call-update) | async-done | bytes 196624 | tf_op jit(solution)/shard_map/reduce_scatter | solution.py:107
  624.2 1.6 copy.111
  (33 shorter events, 0.1 us)
Async XLA Ops:
  7.2 617.1 %reduce-scatter.2.cloned.1.call-start = ((), (), s32[]{:S(2)}) async-start(), calls=%async_computation.1 | async-start | bytes 12779520 | tf_op jit(solution)/shard_map/reduce_scatter | solution.py:107
  12.4 1.2 copy-start.1
  13.2 2.3 copy-start.11
  13.7 9.0 %copy-start.21 = (bf16[256,2048]{1,0:T(8,128)(2,1)S(1)}, bf16[256,2048]{1,0:T(8,128)(2,1)}, u32[]{:S(2)}) copy-start(bf16[256,2048]{1,0:T(8,128)(2,1)} %param.3) | copy-start | bytes 3145732
  15.5 128.1 %collective-permute-start.2 = (f32[256,8,256]{0,2,1:T(8,128)}, f32[256,8,256]{0,2,1:T(8,128)}, u32[]{:S(2)}, u32[]{:S(2)}) collective-permute-start(f32[256,8,256]{0,2,1:T(8,128)} %convolution_bitcast_fusion.1), channel_id=1, source_target_pairs={{0,2},{1,3},{2,0},{3,1},{4,6},{5,7},{6,4},{7,5},{8,10},{9,11},{10,... | collective-permute-start | bytes 6291464 | tf_op jit(solution)/shard_map/ppermute | solution.py:19
  123.0 5.2 copy-start.6
  128.2 1.8 copy-start.5
  132.1 7.7 %copy-start = (bf16[256,8,256]{0,2,1:T(8,128)(2,1)}, bf16[256,8,256]{0,2,1:T(8,128)(2,1)S(1)}, u32[]{:S(2)}) copy-start(bf16[256,8,256]{0,2,1:T(8,128)(2,1)S(1)} %get-tuple-element.20) | copy-start | bytes 3145732
  132.1 9.5 %collective-permute-start = (bf16[256,8,256]{0,2,1:T(8,128)(2,1)S(1)}, bf16[256,8,256]{0,2,1:T(8,128)(2,1)}, u32[]{:S(2)}, u32[]{:S(2)}) collective-permute-start(bf16[256,8,256]{0,2,1:T(8,128)(2,1)S(1)} %get-tuple-element.20), channel_id=1, source_target_pairs={{0,1},{1,0},{2,3},{3,2},{4,5},{5,4},{6,7},{7,6},{8,9},{9,8},{10,11... | collective-permute-start | bytes 3145736 | tf_op jit(solution)/shard_map/ppermute | solution.py:19
  139.8 1.8 copy-start.8
  141.5 2.1 copy-start.2
  141.5 2.1 copy-start.18
  146.2 1.9 copy-start.16
  148.1 55.7 %collective-permute-start.3 = (f32[256,8,256]{0,2,1:T(8,128)}, f32[256,8,256]{0,2,1:T(8,128)}, u32[]{:S(2)}, u32[]{:S(2)}) collective-permute-start(f32[256,8,256]{0,2,1:T(8,128)} %convolution_bitcast_fusion), channel_id=1, source_target_pairs={{0,1},{1,0},{2,3},{3,2},{4,5},{5,4},{6,7},{7,6},{8,9},{9,8},{10,11... | collective-permute-start | bytes 6291464 | tf_op jit(solution)/shard_map/ppermute | solution.py:19
  148.2 51.7 %collective-permute-start.1 = (bf16[256,8,256]{0,2,1:T(8,128)(2,1)S(1)}, bf16[256,8,256]{0,2,1:T(8,128)(2,1)}, u32[]{:S(2)}, u32[]{:S(2)}) collective-permute-start(bf16[256,8,256]{0,2,1:T(8,128)(2,1)S(1)} %get-tuple-element.22), channel_id=1, source_target_pairs={{0,2},{1,3},{2,0},{3,1},{4,6},{5,7},{6,4},{7,5},{8,10},{9,11},{10,... | collective-permute-start | bytes 3145736 | tf_op jit(solution)/shard_map/ppermute | solution.py:19
  149.6 50.3 %copy-start.3 = (bf16[256,2048]{1,0:T(8,128)(2,1)S(1)}, bf16[256,2048]{1,0:T(8,128)(2,1)}, u32[]{:S(2)}) copy-start(bf16[256,2048]{1,0:T(8,128)(2,1)} %param.5) | copy-start | bytes 3145732
  152.3 51.6 %copy-start.17 = (bf16[256,8,256]{0,2,1:T(8,128)(2,1)S(1)}, bf16[256,8,256]{0,2,1:T(8,128)(2,1)}, u32[]{:S(2)}) copy-start(bf16[256,8,256]{0,2,1:T(8,128)(2,1)} %copy-done.16) | copy-start | bytes 3145732
  152.3 51.6 %copy-start.19 = (bf16[1,256,8,256]{1,3,2,0:T(8,128)(2,1)S(1)}, bf16[1,256,8,256]{1,3,2,0:T(8,128)(2,1)}, u32[]{:S(2)}) copy-start(bf16[1,256,8,256]{1,3,2,0:T(8,128)(2,1)} %copy.132) | copy-start | bytes 3145732
  152.3 51.6 %copy-start.20 = (f32[8,256,256]{1,2,0:T(8,128)S(1)}, f32[8,256,256]{1,2,0:T(8,128)}, u32[]{:S(2)}) copy-start(f32[8,256,256]{1,2,0:T(8,128)} %get-tuple-element.21) | copy-start | bytes 6291460
  203.9 3.7 copy-start.7
  203.9 3.7 copy-start.14
  206.6 1.0 copy-start.9
  233.1 1.2 copy-start.4
  235.6 1.8 copy-start.12
  237.4 3.2 copy-start.10
  237.4 3.2 copy-start.13
  262.8 2.4 copy-start.15
Sparse Core Ops, SparseCore 0:
  233.3 390.9 reduce-scatter.1
where the time goes:
time: 639 us; the launch traced here: 633 us
  waiting for transfers between devices  405 us (63%)
  blocking collectives  106 us (17%)
  local copies, waits for them, and re-layouts  50.4 us (8%)
  matrix products  34.1 us (5%)
  other arithmetic  15 us (2%)
  between operations  14.3 us (2%)
  starting transfers between devices  7.35 us (1%)
    reduce_scatter x1, waiting for transfers between devices, shards(): lax.psum_scatter(jnp.stack(grad_terms[::-1]), 'dp', scatter_dimension=1,...  358 us
    psum x1, blocking collectives, shards(): square_sum = lax.psum(jnp.sum(tokens_f32 * tokens_f32, axis=1), 'tensor')  96.6 us
    ppermute x4, waiting for transfers between devices, swapped(): lax.ppermute(x, axis, [(i, i ^ 1 << stride) for i in range(lax.axis_size(...  47.6 us
    unnamed x55, local copies, waits for them, and re-layouts  23.6 us
    another operation x1, local copies, waits for them, and re-layouts, shards(): jnp.stack(grad_terms[::-1])  12.8 us
  transfers between devices with their start and end apart: 5, of which 2 were waited for; matrix products, arithmetic and copies ran while one was open for 9% of the time, Pallas kernels for 0%

commit v1 on v0

--- a/solution.py
+++ b/solution.py
@@ -3,7 +3,7 @@
 import jax
 import jax.numpy as jnp
 from jax import lax
-from jax.sharding import PartitionSpec as P
+from jax.sharding import Mesh, PartitionSpec as P
 
 D = 8192
 BLK = 256
@@ -17,6 +17,26 @@
 
 def swapped(x, axis, stride):
     return lax.ppermute(x, axis, [(i, i ^ 1 << stride) for i in range(lax.axis_size(axis))])
+
+
+def tensor_sum(x):
+    for bit in range(lax.axis_size("tensor").bit_length() - 1):
+        x = x + swapped(x, "tensor", bit)
+    return x
+
+
+def staged_scatter(grads):
+    factors, rows = grads.shape[:2]
+    ny, nz, nx = (lax.axis_size(a) for a in ("dy", "dz", "dx"))
+    rest = grads.shape[2:]
+    share = rows // (ny * nz * nx)
+    g = grads.reshape((factors, ny, nz, nx, share) + rest)
+    g = jnp.transpose(g, (3, 1, 2, 0) + tuple(range(4, g.ndim)))
+    lanes = rest[-1]
+    for axis, size in (("dx", nx), ("dy", ny), ("dz", nz)):
+        g = g.reshape(size, -1, lanes)
+        g = lax.psum_scatter(g, axis, scatter_dimension=0, tiled=True)
+    return g.reshape((factors, share) + rest)
 
 
 def gelu_value(value):
@@ -49,10 +69,10 @@
     blocks_dev = local_width // BLK
     block_bits = (D // BLK).bit_length() - 1
     device_bits = blocks_dev.bit_length() - 1
-    data_size = lax.axis_size("dp")
+    data_size = lax.axis_size(("dy", "dz", "dx"))
     grad_scale = 1.0 / math.sqrt(tok_rows * data_size)
     tokens_f32 = tokens.astype(jnp.float32)
-    square_sum = lax.psum(jnp.sum(tokens_f32 * tokens_f32, axis=1), "tensor")
+    square_sum = tensor_sum(jnp.sum(tokens_f32 * tokens_f32, axis=1))
     inv_rms = lax.rsqrt(square_sum / D + epsilon)[:, None]
     normed = tokens_f32 * inv_rms
     hidden = normed.astype(jnp.bfloat16).reshape(tok_rows, blocks_dev, BLK)
@@ -100,21 +120,24 @@
             previous = stored_preact[factor - 1]
             grad_pre = (grad_hidden * gelu_slope(previous)).astype(jnp.bfloat16)
     flat = grad_hidden.reshape(tok_rows, local_width)
-    inner_sum = lax.psum(jnp.sum(flat * normed, axis=1), "tensor")
+    inner_sum = tensor_sum(jnp.sum(flat * normed, axis=1))
     token_grads = (
         cotangent.astype(jnp.float32) + inv_rms * (flat - normed * (inner_sum / D)[:, None])
     ).astype(jnp.bfloat16)
-    weight_grads = lax.psum_scatter(
-        jnp.stack(grad_terms[::-1]), "dp", scatter_dimension=1, tiled=True
-    )
+    weight_grads = staged_scatter(jnp.stack(grad_terms[::-1]))
     return (mixed, token_grads, weight_grads)
 
 
 def solution(mesh):
+    ny, nz, nx = 4, 4, 4
+    fine = Mesh(
+        mesh.devices.reshape(ny, nz, nx, mesh.shape["tensor"]), ("dy", "dz", "dx", "tensor")
+    )
+    dp = ("dy", "dz", "dx")
     return jax.shard_map(
         shards,
-        mesh=mesh,
-        in_specs=(P("dp", "tensor"), P(None, None, "tensor", None), P("dp", "tensor")),
-        out_specs=(P("dp", "tensor"), P("dp", "tensor"), P(None, "dp", "tensor", None)),
+        mesh=fine,
+        in_specs=(P(dp, "tensor"), P(None, None, "tensor", None), P(dp, "tensor")),
+        out_specs=(P(dp, "tensor"), P(dp, "tensor"), P(None, dp, "tensor", None)),
         check_vma=False,
     )

time: 639 us -> 416 us (0.65)
  waiting for transfers between devices: 405 us -> 278 us
  blocking collectives: 106 us -> 0 us
  local copies, waits for them, and re-layouts: 50.4 us -> 60.5 us
  starting transfers between devices: 7.35 us -> 13.8 us
    reduce_scatter x1 -> x3, waiting for transfers between devices: 358 us -> 163 us  [staged_scatter(): g = lax.psum_scatter(g, axis, scatter_dimension=0, tiled=True)]
    psum x2 -> x0, blocking collectives: 106 us -> none  [the longest x1 96.6 us: shards(): square_sum = lax.psum(jnp.sum(tokens_f32 * tokens_f32, axis=1), 'tensor')]
    ppermute x4 -> x8, waiting for transfers between devices: 47.6 us -> 115 us  [swapped(): lax.ppermute(x, axis, [(i, i ^ 1 << stride) for i in range(lax.axis_size(...]
    transpose x0 -> x1, other arithmetic: none -> 11.4 us  [staged_scatter(): g = jnp.transpose(g, (3, 1, 2, 0) + tuple(range(4, g.ndim)))]
    transpose x0 -> x1, local copies, waits for them, and re-layouts: none -> 11.3 us  [staged_scatter(): g = jnp.transpose(g, (3, 1, 2, 0) + tuple(range(4, g.ndim)))]
    mul x0 -> x2, local copies, waits for them, and re-layouts: none -> 11.1 us  [shards(): jnp.einsum('tbc,tbd->cbd', joined, grad_pre, preferred_element_type=jnp.f...]
    another operation x1 -> x0, other arithmetic: 10 us -> none  [shards(): jnp.stack(grad_terms[::-1])]
    another operation x1, local copies, waits for them, and re-layouts: 12.8 us -> 5.31 us  [shards(): weight_grads = staged_scatter(jnp.stack(grad_terms[::-1]))]
  transfers between devices with their start and end apart: 5 -> 11, of which waited for: 2 -> 6; matrix products, arithmetic and copies ran while one was open for 9% -> 17% of each run, Pallas kernels for 0% -> 0%
where the time goes in v1:
time: 416 us
  waiting for transfers between devices  278 us (67%)
  local copies, waits for them, and re-layouts  60.5 us (15%)
  matrix products  35.6 us (9%)
  other arithmetic  14.2 us (3%)
  between operations  14.1 us (3%)
  starting transfers between devices  13.8 us (3%)
    reduce_scatter x3, waiting for transfers between devices, staged_scatter(): g = lax.psum_scatter(g, axis, scatter_dimension=0, tiled=True)  163 us
    ppermute x8, waiting for transfers between devices, swapped(): lax.ppermute(x, axis, [(i, i ^ 1 << stride) for i in range(lax.axis_size(...  115 us
    unnamed x52, local copies, waits for them, and re-layouts  19.8 us
    ppermute x8, starting transfers between devices, swapped(): lax.ppermute(x, axis, [(i, i ^ 1 << stride) for i in range(lax.axis_size(...  13.7 us
    transpose x1, other arithmetic, staged_scatter(): g = jnp.transpose(g, (3, 1, 2, 0) + tuple(range(4, g.ndim)))  11.4 us
    transpose x1, local copies, waits for them, and re-layouts, staged_scatter(): g = jnp.transpose(g, (3, 1, 2, 0) + tuple(range(4, g.ndim)))  11.3 us
    mul x2, local copies, waits for them, and re-layouts, shards(): jnp.einsum('tbc,tbd->cbd', joined, grad_pre, preferred_element_type=jnp.f...  11.1 us
    dot_general x3, matrix products, shards(): jnp.einsum('tbc,tbd->cbd', joined, grad_pre, preferred_element_type=jnp.f...  9.17 us
  transfers between devices with their start and end apart: 11, of which 6 were waited for; matrix products, arithmetic and copies ran while one was open for 17% of the time, Pallas kernels for 0%

profile of v1, /device:TPU:2, one launch (start us, length us, event | category | flops | bytes accessed | tf_op | source)
XLA Modules:
  0.0 415.7 jit_solution(14833172735338622358)
XLA Ops:
  7.2 0.0 reduce-scatter.4.cloned.1.call-start
  7.2 1.5 copy.38
  8.7 0.3 fusion.8
  9.0 0.1 collective-permute-start
  9.1 5.5 %fusion.67 = (bf16[1,256,8,256]{3,2,1,0:T(8,128)(2,1)}, bf16[1,256,8,256]{3,2,1,0:T(8,128)(2,1)}, bf16[1,256,8,256]{3,2,1,0:T(8,128)(2,1)}, bf16[1,256,8,256]{3,...) fusion(bf16[3,512,8,256]{3,2,1,0:T(8,128)(2,1)} %param.4), kind=kLoop, calls=%fused_computation.88 | loop fusion | bytes 12582912 | tf_op jit(solution)/shard_map/slice | solution.py:63
  14.6 1.7 copy.99
  16.4 7.3 %collective-permute-start.1 = (f32[256]{0:T(256)S(1)}, f32[256]{0:T(256)S(1)}, u32[]{:S(2)}, u32[]{:S(2)}) collective-permute-start(f32[256]{0:T(256)S(1)} %add.71), channel_id=1, source_target_pairs={{0,2},{1,3},{2,0},{3,1},{4,6},{5,7},{6,4},{7,5},{8,10},{9,11},{10,... | collective-permute-start | bytes 3080 | tf_op jit(solution)/shard_map/ppermute | solution.py:19
  23.7 1.8 convolution_bitcast_fusion.1
  25.5 0.0 collective-permute-start.4
  25.5 2.5 copy.97
  28.0 1.6 copy.96
  29.6 0.2 fusion.2
  29.8 1.3 copy.41
  31.1 1.3 rev.8
  32.4 2.1 fusion.57
  34.5 2.0 fusion.38
  36.5 0.2 collective-permute-start.2
  36.8 2.6 copy.95
  39.3 2.4 copy.98
  41.8 2.4 copy.94
  44.2 1.7 fusion.51
  45.9 0.0 copy-start.3
  45.9 0.0 copy-start.18
  45.9 0.0 collective-permute-done.2
  46.0 2.0 fusion.34
  48.0 74.2 %collective-permute-done.4 = f32[256,8,256]{0,2,1:T(8,128)} collective-permute-done((f32[256,8,256]{0,2,1:T(8,128)}, f32[256,8,256]{0,2,1:T(8,128)}, u32[]{:S(2)}, u32[]{:S(2)}) %collective-permute-start.4) | collective-permute-done | bytes 2097184 | tf_op jit(solution)/shard_map/ppermute | solution.py:19
  122.2 2.6 fusion.15
  124.8 1.9 convolution_bitcast_fusion
  126.7 0.0 collective-permute-start.3
  126.7 1.3 copy.67
  128.0 4.6 %multiply_bitcast_fusion = f32[512,8,256]{0,2,1:T(8,128)} fusion(bf16[256,8,256]{0,2,1:T(8,128)(2,1)} %copy-done.16, bf16[256,8,256]{0,2,1:T(8,128)(2,1)} %collective-permute-done.2, bf16[256,8,256]{0,2,1:T(8,128)(2,1)} %copy-done.1), kind=kOutput, calls=%fused_computation.1 | convolution fusion | flops 542113792 | bytes 7340032 | tf_op jit(solution)/shard_map/tbc,tbd->cbd/dot_general | solution.py:104
  132.6 5.5 %copy.70 = f32[512,8,256]{2,1,0:T(8,128)} copy(f32[512,8,256]{0,2,1:T(8,128)} %multiply_bitcast_fusion) | data formatting | bytes 8388608 | tf_op jit(solution)/shard_map/mul | solution.py:104
  138.1 40.6 %collective-permute-done.3 = bf16[256,8,256]{0,2,1:T(8,128)(2,1)} collective-permute-done((bf16[256,8,256]{0,2,1:T(8,128)(2,1)S(1)}, bf16[256,8,256]{0,2,1:T(8,128)(2,1)}, u32[]{:S(2)}, u32[]{:S(2)}) %collective-permute-start.3) | collective-permute-done | bytes 1048608 | tf_op jit(solution)/shard_map/ppermute | solution.py:19
  178.6 1.9 convolution_multiply_fusion
  180.6 0.0 copy-start.19
  180.6 5.3 %copy.72 = f32[1,4,4,4,8,8,256]{6,5,4,3,2,1,0:T(8,128)} copy(f32[1,4,4,4,8,8,256]{6,4,3,2,1,5,0:T(8,128)S(1)} %bitcast.133) | data formatting | bytes 8388608 | tf_op jit(solution)/shard_map/stack | solution.py:127
  186.0 2.7 fusion.21
  188.7 0.0 copy-start.9
  188.7 2.7 multiply_bitcast_fusion.1
  191.4 5.5 %copy.68 = f32[512,8,256]{2,1,0:T(8,128)} copy(f32[512,8,256]{0,2,1:T(8,128)} %multiply_bitcast_fusion.1) | data formatting | bytes 8388608 | tf_op jit(solution)/shard_map/mul | solution.py:104
  196.9 11.4 %maximum_bitcast_fusion = f32[4,4,4,3,8,8,256]{6,5,4,0,2,1,3:T(8,128)} fusion(f32[1,4,4,4,8,8,256]{6,5,4,3,2,1,0:T(8,128)} %copy.72, f32[1,4,4,4,8,8,256]{6,5,4,3,2,1,0:T(8,128)} %bitcast.137, f32[1,4,4,4,8,8,256]{6,5,4,3,2,1,0:T(8,128)} %bitcast.138), kind=kLoop, calls=%fused_computation | loop fusion | flops 6291456 | bytes 25165824 | tf_op jit(solution)/shard_map/transpose | solution.py:34
  208.3 11.3 %copy.73 = f32[4,4,4,3,8,8,256]{6,5,4,3,2,1,0:T(8,128)} copy(f32[4,4,4,3,8,8,256]{6,5,4,0,2,1,3:T(8,128)} %maximum_bitcast_fusion) | data formatting | bytes 25165824 | tf_op jit(solution)/shard_map/transpose | solution.py:34
  219.6 0.0 reduce-scatter.4.cloned.1.call-update
  219.6 0.0 reduce-scatter.6.cloned.1.call-start
  219.7 113.6 %reduce-scatter.4.cloned.1.call-done = f32[1,3072,256]{2,1,0:T(8,128)} async-done(((f32[4,3072,256]{2,1,0:T(8,128)}), f32[1,3072,256]{2,1,0:T(8,128)}) %reduce-scatter.4.cloned.1.call-update) | async-done | bytes 3145744 | tf_op jit(solution)/shard_map/reduce_scatter | solution.py:38
  333.3 0.0 reduce-scatter.6.cloned.1.call-update
  333.3 0.0 reduce-scatter.8.cloned.1.call-start
  333.4 1.3 copy.51
  334.7 3.1 fusion.55
  337.8 1.9 copy.66
  339.7 1.6 rev.9
  341.3 2.7 bitcast_add_fusion
  344.0 0.3 fusion.3
  344.4 0.3 collective-permute-start.6
  344.7 33.0 %reduce-scatter.6.cloned.1.call-done = f32[1,768,256]{2,1,0:T(8,128)} async-done(((f32[4,768,256]{2,1,0:T(8,128)}), f32[1,768,256]{2,1,0:T(8,128)}) %reduce-scatter.6.cloned.1.call-update) | async-done | bytes 786448 | tf_op jit(solution)/shard_map/reduce_scatter | solution.py:38
  377.7 0.0 reduce-scatter.8.cloned.1.call-update
  377.7 2.1 fusion.45
  379.8 5.8 %collective-permute-start.7 = (f32[256]{0:T(256)S(1)}, f32[256]{0:T(256)S(1)}, u32[]{:S(2)}, u32[]{:S(2)}) collective-permute-start(f32[256]{0:T(256)S(1)} %add.89), channel_id=1, source_target_pairs={{0,2},{1,3},{2,0},{3,1},{4,6},{5,7},{6,4},{7,5},{8,10},{9,11},{10,... | collective-permute-start | bytes 3080 | tf_op jit(solution)/shard_map/ppermute | solution.py:19
  385.7 1.7 convolution_add_fusion
  387.3 0.1 collective-permute-done.7
  387.4 1.9 fusion.7
  389.3 2.4 copy.74
  391.7 1.4 copy.75
  393.1 16.1 %reduce-scatter.8.cloned.1.call-done = f32[1,192,256]{2,1,0:T(8,128)} async-done(((f32[4,192,256]{2,1,0:T(8,128)}), f32[1,192,256]{2,1,0:T(8,128)}) %reduce-scatter.8.cloned.1.call-update) | async-done | bytes 196624 | tf_op jit(solution)/shard_map/reduce_scatter | solution.py:38
  (47 shorter events, 0.1 us)
Async XLA Ops:
  7.2 326.1 %reduce-scatter.4.cloned.1.call-start = ((), (), s32[]{:S(2)}) async-start(), calls=%async_computation.3 | async-start | bytes 15728640 | tf_op jit(solution)/shard_map/reduce_scatter | solution.py:38
  9.0 7.4 %collective-permute-start = (f32[256]{0:T(256)S(1)}, f32[256]{0:T(256)S(1)}, u32[]{:S(2)}, u32[]{:S(2)}) collective-permute-start(f32[256]{0:T(256)S(1)} %fusion.8), channel_id=1, source_target_pairs={{0,1},{1,0},{2,3},{3,2},{4,5},{5,4},{6,7},{7,6},{8,9},{9,8},{10,11... | collective-permute-start | bytes 3080 | tf_op jit(solution)/shard_map/ppermute | solution.py:19
  14.6 9.0 %copy-start.2 = (bf16[256,2048]{1,0:T(8,128)(2,1)S(1)}, bf16[256,2048]{1,0:T(8,128)(2,1)}, u32[]{:S(2)}) copy-start(bf16[256,2048]{1,0:T(8,128)(2,1)} %param.5) | copy-start | bytes 3145732
  16.4 9.1 %copy-start.10 = (bf16[1,256,8,256]{1,3,2,0:T(8,128)(2,1)}, bf16[1,256,8,256]{1,3,2,0:T(8,128)(2,1)S(1)}, u32[]{:S(2)}) copy-start(bf16[1,256,8,256]{1,3,2,0:T(8,128)(2,1)S(1)} %copy.99) | copy-start | bytes 3145732
  16.4 13.2 %collective-permute-start.1 = (f32[256]{0:T(256)S(1)}, f32[256]{0:T(256)S(1)}, u32[]{:S(2)}, u32[]{:S(2)}) collective-permute-start(f32[256]{0:T(256)S(1)} %add.71), channel_id=1, source_target_pairs={{0,2},{1,3},{2,0},{3,1},{4,6},{5,7},{6,4},{7,5},{8,10},{9,11},{10,... | collective-permute-start | bytes 3080 | tf_op jit(solution)/shard_map/ppermute | solution.py:19
  25.5 2.5 copy-start.13
  25.5 96.7 %collective-permute-start.4 = (f32[256,8,256]{0,2,1:T(8,128)}, f32[256,8,256]{0,2,1:T(8,128)}, u32[]{:S(2)}, u32[]{:S(2)}) collective-permute-start(f32[256,8,256]{0,2,1:T(8,128)} %convolution_bitcast_fusion.1), channel_id=1, source_target_pairs={{0,2},{1,3},{2,0},{3,1},{4,6},{5,7},{6,4},{7,5},{8,10},{9,11},{10,... | collective-permute-start | bytes 6291464 | tf_op jit(solution)/shard_map/ppermute | solution.py:19
  32.4 2.1 copy-start.6
  32.4 2.1 copy-start.5
  36.5 7.6 %copy-start.1 = (bf16[256,8,256]{0,2,1:T(8,128)(2,1)}, bf16[256,8,256]{0,2,1:T(8,128)(2,1)S(1)}, u32[]{:S(2)}) copy-start(bf16[256,8,256]{0,2,1:T(8,128)(2,1)S(1)} %get-tuple-element.14) | copy-start | bytes 3145732
  36.5 9.4 %collective-permute-start.2 = (bf16[256,8,256]{0,2,1:T(8,128)(2,1)S(1)}, bf16[256,8,256]{0,2,1:T(8,128)(2,1)}, u32[]{:S(2)}, u32[]{:S(2)}) collective-permute-start(bf16[256,8,256]{0,2,1:T(8,128)(2,1)S(1)} %get-tuple-element.14), channel_id=1, source_target_pairs={{0,1},{1,0},{2,3},{3,2},{4,5},{5,4},{6,7},{7,6},{8,9},{9,8},{10,11... | collective-permute-start | bytes 3145736 | tf_op jit(solution)/shard_map/ppermute | solution.py:19
  44.2 1.8 copy-start.8
  45.9 76.3 %copy-start.3 = (bf16[256,2048]{1,0:T(8,128)(2,1)S(1)}, bf16[256,2048]{1,0:T(8,128)(2,1)}, u32[]{:S(2)}) copy-start(bf16[256,2048]{1,0:T(8,128)(2,1)} %param.5) | copy-start | bytes 3145732
  45.9 76.3 %copy-start.18 = (bf16[1,256,8,256]{1,3,2,0:T(8,128)(2,1)S(1)}, bf16[1,256,8,256]{1,3,2,0:T(8,128)(2,1)}, u32[]{:S(2)}) copy-start(bf16[1,256,8,256]{1,3,2,0:T(8,128)(2,1)} %copy.94) | copy-start | bytes 3145732
  48.0 130.6 %copy-start = (bf16[256,8,256]{0,2,1:T(8,128)(2,1)}, bf16[256,8,256]{0,2,1:T(8,128)(2,1)S(1)}, u32[]{:S(2)}) copy-start(bf16[256,8,256]{0,2,1:T(8,128)(2,1)S(1)} %get-tuple-element.16) | copy-start | bytes 3145732
  124.8 1.9 copy-start.16
  126.7 59.3 %collective-permute-start.5 = (f32[256,8,256]{0,2,1:T(8,128)}, f32[256,8,256]{0,2,1:T(8,128)}, u32[]{:S(2)}, u32[]{:S(2)}) collective-permute-start(f32[256,8,256]{0,2,1:T(8,128)} %convolution_bitcast_fusion), channel_id=1, source_target_pairs={{0,1},{1,0},{2,3},{3,2},{4,5},{5,4},{6,7},{7,6},{8,9},{9,8},{10,11... | collective-permute-start | bytes 6291464 | tf_op jit(solution)/shard_map/ppermute | solution.py:19
  126.7 52.0 %collective-permute-start.3 = (bf16[256,8,256]{0,2,1:T(8,128)(2,1)S(1)}, bf16[256,8,256]{0,2,1:T(8,128)(2,1)}, u32[]{:S(2)}, u32[]{:S(2)}) collective-permute-start(bf16[256,8,256]{0,2,1:T(8,128)(2,1)S(1)} %get-tuple-element.16), channel_id=1, source_target_pairs={{0,2},{1,3},{2,0},{3,1},{4,6},{5,7},{6,4},{7,5},{8,10},{9,11},{10,... | collective-permute-start | bytes 3145736 | tf_op jit(solution)/shard_map/ppermute | solution.py:19
  132.6 46.1 %copy-start.4 = (bf16[256,2048]{1,0:T(8,128)(2,1)S(1)}, bf16[256,2048]{1,0:T(8,128)(2,1)}, u32[]{:S(2)}) copy-start(bf16[256,2048]{1,0:T(8,128)(2,1)} %param.5) | copy-start | bytes 3145732
  180.6 5.4 %copy-start.17 = (bf16[256,8,256]{0,2,1:T(8,128)(2,1)S(1)}, bf16[256,8,256]{0,2,1:T(8,128)(2,1)}, u32[]{:S(2)}) copy-start(bf16[256,8,256]{0,2,1:T(8,128)(2,1)} %copy-done.16) | copy-start | bytes 3145732
  180.6 5.3 %copy-start.19 = (bf16[1,256,8,256]{1,3,2,0:T(8,128)(2,1)S(1)}, bf16[1,256,8,256]{1,3,2,0:T(8,128)(2,1)}, u32[]{:S(2)}) copy-start(bf16[1,256,8,256]{1,3,2,0:T(8,128)(2,1)} %copy.95) | copy-start | bytes 3145732
  180.6 5.3 %copy-start.20 = (f32[8,256,256]{1,2,0:T(8,128)S(1)}, f32[8,256,256]{1,2,0:T(8,128)}, u32[]{:S(2)}) copy-start(f32[8,256,256]{1,2,0:T(8,128)} %get-tuple-element.15) | copy-start | bytes 6291460
  186.0 2.7 copy-start.7
  186.0 2.7 copy-start.14
  188.7 146.0 %copy-start.9 = (bf16[256,8,256]{0,2,1:T(8,128)(2,1)}, bf16[256,8,256]{0,2,1:T(8,128)(2,1)S(1)}, u32[]{:S(2)}) copy-start(bf16[256,8,256]{0,2,1:T(8,128)(2,1)S(1)} %fusion.21) | copy-start | bytes 3145732
  219.6 158.1 %reduce-scatter.6.cloned.1.call-start = ((), (), s32[]{:S(2)}) async-start(), calls=%async_computation.4 | async-start | bytes 3932160 | tf_op jit(solution)/shard_map/reduce_scatter | solution.py:38
  333.3 75.9 %reduce-scatter.8.cloned.1.call-start = ((), (), s32[]{:S(2)}) async-start(), calls=%async_computation.5 | async-start | bytes 983040 | tf_op jit(solution)/shard_map/reduce_scatter | solution.py:38
  344.4 35.4 %collective-permute-start.6 = (f32[256]{0:T(256)S(1)}, f32[256]{0:T(256)S(1)}, u32[]{:S(2)}, u32[]{:S(2)}) collective-permute-start(f32[256]{0:T(256)S(1)} %fusion.3), channel_id=1, source_target_pairs={{0,1},{1,0},{2,3},{3,2},{4,5},{5,4},{6,7},{7,6},{8,9},{9,8},{10,11... | collective-permute-start | bytes 3080 | tf_op jit(solution)/shard_map/ppermute | solution.py:19
  377.7 7.9 %copy-start.11 = (bf16[1,256,8,256]{1,3,2,0:T(8,128)(2,1)S(1)}, bf16[1,256,8,256]{1,3,2,0:T(8,128)(2,1)}, u32[]{:S(2)}) copy-start(bf16[1,256,8,256]{1,3,2,0:T(8,128)(2,1)} %copy-done.10) | copy-start | bytes 3145732
  379.8 7.6 %copy-start.12 = (bf16[256,2048]{0,1:T(8,128)(2,1)S(1)}, bf16[256,2048]{0,1:T(8,128)(2,1)}, u32[]{:S(2)}) copy-start(bf16[256,2048]{0,1:T(8,128)(2,1)} %copy.51) | copy-start | bytes 3145732
  379.8 7.6 %collective-permute-start.7 = (f32[256]{0:T(256)S(1)}, f32[256]{0:T(256)S(1)}, u32[]{:S(2)}, u32[]{:S(2)}) collective-permute-start(f32[256]{0:T(256)S(1)} %add.89), channel_id=1, source_target_pairs={{0,2},{1,3},{2,0},{3,1},{4,6},{5,7},{6,4},{7,5},{8,10},{9,11},{10,... | collective-permute-start | bytes 3080 | tf_op jit(solution)/shard_map/ppermute | solution.py:19
  389.3 2.4 copy-start.15
Sparse Core Ops, SparseCore 0:
  219.7 113.5 reduce-scatter.3
  335.8 41.8 reduce-scatter.5
  380.8 28.3 reduce-scatter.7

commit v2 on v1

--- a/solution.py
+++ b/solution.py
@@ -25,18 +25,34 @@
     return x
 
 
-def staged_scatter(grads):
-    factors, rows = grads.shape[:2]
+def scatter_first(grads):
+    rows = grads.shape[0]
     ny, nz, nx = (lax.axis_size(a) for a in ("dy", "dz", "dx"))
-    rest = grads.shape[2:]
+    rest = grads.shape[1:]
     share = rows // (ny * nz * nx)
-    g = grads.reshape((factors, ny, nz, nx, share) + rest)
-    g = jnp.transpose(g, (3, 1, 2, 0) + tuple(range(4, g.ndim)))
-    lanes = rest[-1]
-    for axis, size in (("dx", nx), ("dy", ny), ("dz", nz)):
-        g = g.reshape(size, -1, lanes)
+    g = grads.reshape((ny, nz, nx, share) + rest)
+    g = jnp.moveaxis(g, 2, 0).reshape(nx, -1, rest[-1])
+    g = lax.psum_scatter(g, "dx", scatter_dimension=0, tiled=True)
+    return g.reshape((ny, nz, share) + rest)
+
+
+def scatter_rest(parts):
+    ny, nz, share = parts[0].shape[:3]
+    rest = parts[0].shape[3:]
+    g = jnp.stack(parts, axis=2)
+    for axis, size in (("dy", ny), ("dz", nz)):
+        g = g.reshape(size, -1, rest[-1])
         g = lax.psum_scatter(g, axis, scatter_dimension=0, tiled=True)
-    return g.reshape((factors, share) + rest)
+    return g.reshape((len(parts), share) + rest)
+
+
+def partner_rows(rows):
+    pieces = lax.axis_size(("dy", "dx"))
+    piece = rows.shape[0] // pieces
+    mine = lax.axis_index("dy") * lax.axis_size("dx") + lax.axis_index("dx")
+    part = lax.dynamic_slice_in_dim(rows, mine * piece, piece, axis=0)
+    part = swapped(part, "tensor", 1)
+    return lax.all_gather(part, ("dy", "dx"), axis=0, tiled=True)
 
 
 def gelu_value(value):
@@ -101,20 +117,30 @@
         kept_hidden, kept_partner = stored_inputs[factor]
         joined = jnp.concatenate([kept_hidden, kept_partner], axis=2)
         grad_terms.append(
-            jnp.einsum("tbc,tbd->cbd", joined, grad_pre, preferred_element_type=jnp.float32)
-            * grad_scale
+            scatter_first(
+                jnp.einsum("tbc,tbd->cbd", joined, grad_pre, preferred_element_type=jnp.float32)
+                * grad_scale
+            )
         )
         layer_weights = weights[factor]
         near_term = jnp.einsum(
             "tbd,cbd->tbc", grad_pre, layer_weights[:BLK], preferred_element_type=jnp.float32
         )
-        far_term = jnp.einsum(
-            "tbd,cbd->tbc", grad_pre, layer_weights[BLK:], preferred_element_type=jnp.float32
-        )
+        if stride < blocks_dev or factor < FACTORS - 1 or bit_index - device_bits != 1:
+            far_term = jnp.einsum(
+                "tbd,cbd->tbc", grad_pre, layer_weights[BLK:], preferred_element_type=jnp.float32
+            )
         if stride < blocks_dev:
             arrived = local_partner(far_term, stride)
+        elif factor < FACTORS - 1 or bit_index - device_bits != 1:
+            arrived = swapped(far_term, "tensor", bit_index - device_bits)
         else:
-            arrived = swapped(far_term, "tensor", bit_index - device_bits)
+            arrived = jnp.einsum(
+                "tbd,cbd->tbc",
+                swapped(grad_pre, "tensor", 1),
+                partner_rows(layer_weights[BLK:]),
+                preferred_element_type=jnp.float32,
+            )
         grad_hidden = near_term + arrived
         if factor > 0:
             previous = stored_preact[factor - 1]
@@ -124,7 +150,7 @@
     token_grads = (
         cotangent.astype(jnp.float32) + inv_rms * (flat - normed * (inner_sum / D)[:, None])
     ).astype(jnp.bfloat16)
-    weight_grads = staged_scatter(jnp.stack(grad_terms[::-1]))
+    weight_grads = scatter_rest(grad_terms[::-1])
     return (mixed, token_grads, weight_grads)
 
 

time: 416 us -> 350 us (0.84)
  waiting for transfers between devices: 278 us -> 197 us
  starting transfers between devices: 13.8 us -> 23.6 us
  other arithmetic: 14.2 us -> 6.33 us
  local copies, waits for them, and re-layouts: 60.5 us -> 66.4 us
  matrix products: 35.6 us -> 41.2 us
    ppermute x8 -> x9, waiting for transfers between devices: 115 us -> 46.3 us  [swapped(): lax.ppermute(x, axis, [(i, i ^ 1 << stride) for i in range(lax.axis_size(...]
    reduce_scatter x3 -> x5, waiting for transfers between devices: 163 us -> 148 us  [the longest x3 102 us: scatter_first(): g = lax.psum_scatter(g, 'dx', scatter_dimension=0, tiled=True)]
    transpose x1 -> x0, other arithmetic: 11.4 us -> none  [staged_scatter(): g = jnp.transpose(g, (3, 1, 2, 0) + tuple(range(4, g.ndim)))]
    ppermute x8 -> x9, starting transfers between devices: 13.7 us -> 23.3 us  [swapped(): lax.ppermute(x, axis, [(i, i ^ 1 << stride) for i in range(lax.axis_size(...]
    reshape x0 -> x2, local copies, waits for them, and re-layouts: none -> 5.77 us  [the longest x1 4.45 us: scatter_first(): g = grads.reshape((ny, nz, nx, share) + rest)]
    another operation x1 -> x0, local copies, waits for them, and re-layouts: 5.31 us -> none  [shards(): weight_grads = staged_scatter(jnp.stack(grad_terms[::-1]))]
    unnamed x52 -> x42, local copies, waits for them, and re-layouts: 19.8 us -> 21.9 us
    transpose x1 -> x2, local copies, waits for them, and re-layouts: 11.3 us -> 9.37 us  [scatter_first(): g = jnp.moveaxis(g, 2, 0).reshape(nx, -1, rest[-1])]
  transfers between devices with their start and end apart: 11 -> 15, of which waited for: 6 -> 10; matrix products, arithmetic and copies ran while one was open for 17% -> 25% of each run, Pallas kernels for 0% -> 0%
where the time goes in v2:
time: 350 us; the launch traced here: 349 us
  waiting for transfers between devices  197 us (56%)
  local copies, waits for them, and re-layouts  66.4 us (19%)
  matrix products  41.2 us (12%)
  starting transfers between devices  23.6 us (7%)
  between operations  14.4 us (4%)
  other arithmetic  6.33 us (2%)
    reduce_scatter x3, waiting for transfers between devices, scatter_first(): g = lax.psum_scatter(g, 'dx', scatter_dimension=0, tiled=True)  102 us
    ppermute x9, waiting for transfers between devices, swapped(): lax.ppermute(x, axis, [(i, i ^ 1 << stride) for i in range(lax.axis_size(...  46.3 us
    reduce_scatter x2, waiting for transfers between devices, scatter_rest(): g = lax.psum_scatter(g, axis, scatter_dimension=0, tiled=True)  45.3 us
    ppermute x9, starting transfers between devices, swapped(): lax.ppermute(x, axis, [(i, i ^ 1 << stride) for i in range(lax.axis_size(...  23.3 us
    unnamed x42, local copies, waits for them, and re-layouts  21.9 us
    mul x2, local copies, waits for them, and re-layouts, shards(): jnp.einsum('tbc,tbd->cbd', joined, grad_pre, preferred_element_type=jnp.f...  11 us
    dot_general x3, matrix products, shards(): jnp.einsum('tbd,cbd->tbc', grad_pre, layer_weights[:BLK], preferred_eleme...  9.69 us
    transpose x2, local copies, waits for them, and re-layouts, scatter_first(): g = jnp.moveaxis(g, 2, 0).reshape(nx, -1, rest[-1])  9.37 us
  transfers between devices with their start and end apart: 15, of which 10 were waited for; matrix products, arithmetic and copies ran while one was open for 25% of the time, Pallas kernels for 0%

profile of v2, /device:TPU:2, one launch (start us, length us, event | category | flops | bytes accessed | tf_op | source)
XLA Modules:
  0.0 349.3 jit_solution(8253859826115204523)
XLA Ops:
  7.2 1.5 copy.74
  8.7 0.3 fusion.8
  9.0 0.1 collective-permute-start
  9.1 5.2 %fusion.58 = (bf16[1,256,8,256]{3,2,1,0:T(8,128)(2,1)}, bf16[1,256,8,256]{3,2,1,0:T(8,128)(2,1)}, bf16[1,256,8,256]{3,2,1,0:T(8,128)(2,1)}, bf16[1,256,8,256]{3,...) fusion(bf16[3,512,8,256]{3,2,1,0:T(8,128)(2,1)} %param.4), kind=kLoop, calls=%fused_computation.80 | loop fusion | bytes 12582912 | tf_op jit(solution)/shard_map/slice | solution.py:79
  14.3 1.6 copy.144
  16.0 7.3 %collective-permute-start.1 = (f32[256]{0:T(256)S(1)}, f32[256]{0:T(256)S(1)}, u32[]{:S(2)}, u32[]{:S(2)}) collective-permute-start(f32[256]{0:T(256)S(1)} %add.84), channel_id=1, source_target_pairs={{0,2},{1,3},{2,0},{3,1},{4,6},{5,7},{6,4},{7,5},{8,10},{9,11},{10,... | collective-permute-start | bytes 3080 | tf_op jit(solution)/shard_map/ppermute | solution.py:19
  23.3 1.0 dynamic-slice_bitcast_fusion
  24.3 1.2 copy.92
  25.5 0.1 collective-permute-start.4
  25.6 2.4 copy.142
  28.0 0.8 copy.141
  28.8 0.2 fusion.2
  29.0 1.3 copy.77
  30.3 2.3 rev.8
  32.6 1.8 collective-permute-done.4
  34.4 0.6 copy-done.15
  35.1 2.0 fusion.51
  37.1 2.3 fusion.38
  39.4 1.5 copy.87
  40.9 1.3 copy.93
  42.2 4.1 %collective-permute-start.5 = (bf16[256,8,256]{2,0,1:T(8,128)(2,1)}, bf16[256,8,256]{2,0,1:T(8,128)(2,1)}, u32[]{:S(2)}, u32[]{:S(2)}) collective-permute-start(bf16[256,8,256]{2,0,1:T(8,128)(2,1)} %copy.93), channel_id=1, source_target_pairs={{0,2},{1,3},{2,0},{3,1},{4,6},{5,7},{6,4},{7,5},{8,10},{9,11},{10,... | collective-permute-start | bytes 3145736 | tf_op jit(solution)/shard_map/ppermute | solution.py:19
  46.4 2.5 copy.140
  48.8 2.4 copy.143
  51.3 2.4 copy.139
  53.7 3.1 fusion.40
  56.8 1.8 fusion.47
  58.6 3.5 %fusion.34 = (bf16[256,8,256]{0,2,1:T(8,128)(2,1)}, f32[8,256,256]{1,2,0:T(8,128)}) fusion(f32[8,256,256]{1,2,0:T(8,128)S(1)} %fusion.47, bf16[256,8,256]{0,2,1:T(8,128)(2,1)} %collective-permute-done.2, bf16[1,256,8,256]{1,3,2,0:T(8,128)(2,1)S(1)} %copy-done.6), kind=kOutput, calls=%fused_computation.47 | convolution fusion | flops 271581184 | bytes 7340032 | tf_op jit(solution)/shard_map/tbc,cbd->tbd/dot_general | solution.py:78
  62.1 17.8 %collective-permute-done.5 = bf16[256,8,256]{2,0,1:T(8,128)(2,1)} collective-permute-done((bf16[256,8,256]{2,0,1:T(8,128)(2,1)}, bf16[256,8,256]{2,0,1:T(8,128)(2,1)}, u32[]{:S(2)}, u32[]{:S(2)}) %collective-permute-start.5) | collective-permute-done | bytes 1048608 | tf_op jit(solution)/shard_map/ppermute | solution.py:19
  79.9 3.2 all-gather.2.cloned.1.call-done
  83.1 4.0 %fusion.15 = bf16[256,8,256]{0,2,1:T(8,128)(2,1)S(1)} fusion(f32[8,256,256]{1,2,0:T(8,128)} %get-tuple-element.20, f32[8,256,256]{2,1,0:T(8,128)} %fusion.40, bf16[256,8,256]{2,0,1:T(8,128)(2,1)} %all-gather.2.cloned.1.call-done, bf16[256,8,256]{2,0,1:T(8,128)(2,1)} %collective-permute-done.5), kind=kOutput, calls=%fused_computation.24 | convolution fusion | flops 274202624 | bytes 7340032 | tf_op jit(solution)/shard_map/tbd,cbd->tbc/dot_general | solution.py:138
  87.1 1.1 copy-done.13
  88.2 4.2 %multiply_bitcast_fusion = f32[512,8,256]{0,2,1:T(8,128)} fusion(bf16[256,8,256]{0,2,1:T(8,128)(2,1)S(1)} %fusion.15, bf16[256,8,256]{0,2,1:T(8,128)(2,1)} %collective-permute-done.2, bf16[256,8,256]{0,2,1:T(8,128)(2,1)} %get-tuple-element.17), kind=kOutput, calls=%fused_computation | convolution fusion | flops 542113792 | bytes 7340032 | tf_op jit(solution)/shard_map/tbc,tbd->cbd/dot_general | solution.py:121
  92.4 5.5 %copy.109 = f32[512,8,256]{2,1,0:T(8,128)} copy(f32[512,8,256]{0,2,1:T(8,128)} %multiply_bitcast_fusion) | data formatting | bytes 8388608 | tf_op jit(solution)/shard_map/mul | solution.py:121
  97.9 4.6 %copy.110 = f32[4,4,4,8,8,256]{5,4,3,2,1,0:T(8,128)} copy(f32[4,4,4,8,8,256]{5,4,3,0,2,1:T(8,128)} %bitcast.148) | data formatting | bytes 8388608 | tf_op jit(solution)/shard_map/transpose | solution.py:34
  102.6 5.8 %collective-permute-start.3 = (bf16[256,8,256]{0,2,1:T(8,128)(2,1)}, bf16[256,8,256]{0,2,1:T(8,128)(2,1)S(1)}, u32[]{:S(2)}, u32[]{:S(2)}) collective-permute-start(bf16[256,8,256]{0,2,1:T(8,128)(2,1)} %get-tuple-element.19), channel_id=1, source_target_pairs={{0,2},{1,3},{2,0},{3,1},{4,6},{5,7},{6,4},{7,5},{8,10},{9,11},{10,... | collective-permute-start | bytes 3145736 | tf_op jit(solution)/shard_map/ppermute | solution.py:19
  108.4 22.2 %collective-permute-done.3 = bf16[256,8,256]{0,2,1:T(8,128)(2,1)S(1)} collective-permute-done((bf16[256,8,256]{0,2,1:T(8,128)(2,1)}, bf16[256,8,256]{0,2,1:T(8,128)(2,1)S(1)}, u32[]{:S(2)}, u32[]{:S(2)}) %collective-permute-start.3) | collective-permute-done | bytes 1048608 | tf_op jit(solution)/shard_map/ppermute | solution.py:19
  130.7 2.3 convolution_multiply_fusion
  133.0 4.5 %copy.112 = f32[4,4,4,8,8,256]{5,4,3,1,0,2:T(8,128)} copy(f32[4,4,4,8,8,256]{5,3,2,1,0,4:T(8,128)S(1)} %bitcast.141) | data formatting | bytes 8388608 | tf_op jit(solution)/shard_map/reshape | solution.py:33
  137.6 3.3 convolution_bitcast_fusion
  140.9 1.3 copy.105
  142.2 3.2 collective-permute-done.6
  145.4 4.2 %fusion.21 = bf16[256,8,256]{0,2,1:T(8,128)(2,1)S(1)} fusion(f32[256,8,256]{0,2,1:T(8,128)} %collective-permute-done.6, f32[8,256,256]{1,2,0:T(8,128)} %get-tuple-element.18, bf16[256,8,256]{0,2,1:T(8,128)(2,1)} %copy-done.13, bf16[1,256,8,256]{1,3,2,0:T(8,128)(2,1)} %copy.140), kind=kOutput, calls=%fused_computation.30 | convolution fusion | flops 274202624 | bytes 7340032 | tf_op jit(solution)/shard_map/tbd,cbd->tbc/dot_general | solution.py:126
  149.6 2.7 multiply_bitcast_fusion.1
  152.3 5.5 %copy.106 = f32[512,8,256]{2,1,0:T(8,128)} copy(f32[512,8,256]{0,2,1:T(8,128)} %multiply_bitcast_fusion.1) | data formatting | bytes 8388608 | tf_op jit(solution)/shard_map/mul | solution.py:121
  157.8 4.8 %copy.107 = f32[4,4,4,8,8,256]{5,4,3,2,1,0:T(8,128)} copy(f32[4,4,4,8,8,256]{5,4,3,0,2,1:T(8,128)} %bitcast.149) | data formatting | bytes 8388608 | tf_op jit(solution)/shard_map/transpose | solution.py:34
  162.7 50.9 %reduce-scatter.10.cloned.1.call-done = f32[1,1024,256]{2,1,0:T(8,128)} async-done(((f32[4,1024,256]{2,1,0:T(8,128)}), f32[1,1024,256]{2,1,0:T(8,128)}) %reduce-scatter.10.cloned.1.call-update) | async-done | bytes 1048592 | tf_op jit(solution)/shard_map/reduce_scatter | solution.py:35
  213.5 51.5 %reduce-scatter.6.cloned.1.call-done = f32[1,1024,256]{2,1,0:T(8,128)} async-done(((f32[4,1024,256]{2,1,0:T(8,128)}), f32[1,1024,256]{2,1,0:T(8,128)}) %reduce-scatter.6.cloned.1.call-update) | async-done | bytes 1048592 | tf_op jit(solution)/shard_map/reduce_scatter | solution.py:35
  265.1 3.8 %pad_maximum_fusion = f32[4,4,3,8,8,256]{5,4,3,2,1,0:T(8,128)} fusion(f32[4,4,1,8,8,256]{5,4,3,2,1,0:T(8,128)} %bitcast.155, f32[4,4,1,8,8,256]{5,4,3,2,1,0:T(8,128)} %bitcast.154, f32[4,4,1,8,8,256]{5,4,3,2,1,0:T(8,128)} %bitcast.156), kind=kLoop, calls=%fused_computation.2 | loop fusion | flops 1572864 | bytes 6291456 | tf_op jit(solution)/shard_map/stack | solution.py:42
  269.0 3.1 fusion.49
  272.1 2.9 copy.104
  275.0 3.2 rev.9
  278.2 2.4 bitcast_add_fusion
  280.6 1.4 copy-done
  282.0 0.4 fusion.3
  282.3 0.1 collective-permute-start.7
  282.4 28.5 %reduce-scatter.12.cloned.1.call-done = f32[1,768,256]{2,1,0:T(8,128)} async-done(((f32[4,768,256]{2,1,0:T(8,128)}), f32[1,768,256]{2,1,0:T(8,128)}) %reduce-scatter.12.cloned.1.call-update) | async-done | bytes 786448 | tf_op jit(solution)/shard_map/reduce_scatter | solution.py:45
  310.9 1.8 fusion.42
  312.8 5.8 %collective-permute-start.8 = (f32[256]{0:T(256)S(1)}, f32[256]{0:T(256)S(1)}, u32[]{:S(2)}, u32[]{:S(2)}) collective-permute-start(f32[256]{0:T(256)S(1)} %add.105), channel_id=1, source_target_pairs={{0,2},{1,3},{2,0},{3,1},{4,6},{5,7},{6,4},{7,5},{8,10},{9,11},{10,... | collective-permute-start | bytes 3080 | tf_op jit(solution)/shard_map/ppermute | solution.py:19
  318.6 0.4 convolution_add_fusion
  319.1 1.3 collective-permute-done.8
  320.4 1.6 fusion.7
  321.9 2.3 copy.116
  324.2 1.4 copy.117
  325.6 16.8 %reduce-scatter.14.cloned.1.call-done = f32[1,192,256]{2,1,0:T(8,128)} async-done(((f32[4,192,256]{2,1,0:T(8,128)}), f32[1,192,256]{2,1,0:T(8,128)}) %reduce-scatter.14.cloned.1.call-update) | async-done | bytes 196624 | tf_op jit(solution)/shard_map/reduce_scatter | solution.py:45
  (52 shorter events, 0.5 us)
Async XLA Ops:
  7.2 76.0 %all-gather.2.cloned.1.call-start = ((), (), s32[]{:S(2)}) async-start(), calls=%async_computation.5 | async-start | bytes 1114112 | tf_op jit(solution)/shard_map/all_gather | solution.py:55
  9.0 7.0 %collective-permute-start = (f32[256]{0:T(256)S(1)}, f32[256]{0:T(256)S(1)}, u32[]{:S(2)}, u32[]{:S(2)}) collective-permute-start(f32[256]{0:T(256)S(1)} %fusion.8), channel_id=1, source_target_pairs={{0,1},{1,0},{2,3},{3,2},{4,5},{5,4},{6,7},{7,6},{8,9},{9,8},{10,11... | collective-permute-start | bytes 3080 | tf_op jit(solution)/shard_map/ppermute | solution.py:19
  15.9 12.0 %copy-start.8 = (bf16[1,256,8,256]{1,3,2,0:T(8,128)(2,1)}, bf16[1,256,8,256]{1,3,2,0:T(8,128)(2,1)S(1)}, u32[]{:S(2)}) copy-start(bf16[1,256,8,256]{1,3,2,0:T(8,128)(2,1)S(1)} %copy.144) | copy-start | bytes 3145732
  16.0 12.8 %collective-permute-start.1 = (f32[256]{0:T(256)S(1)}, f32[256]{0:T(256)S(1)}, u32[]{:S(2)}, u32[]{:S(2)}) collective-permute-start(f32[256]{0:T(256)S(1)} %add.84), channel_id=1, source_target_pairs={{0,2},{1,3},{2,0},{3,1},{4,6},{5,7},{6,4},{7,5},{8,10},{9,11},{10,... | collective-permute-start | bytes 3080 | tf_op jit(solution)/shard_map/ppermute | solution.py:19
  25.5 8.9 %collective-permute-start.4 = (bf16[16,8,256]{2,0,1:T(8,128)(2,1)S(1)}, bf16[16,8,256]{2,0,1:T(8,128)(2,1)S(1)}, u32[]{:S(2)}, u32[]{:S(2)}) collective-permute-start(bf16[16,8,256]{2,0,1:T(8,128)(2,1)S(1)} %copy.92), channel_id=1, source_target_pairs={{0,2},{1,3},{2,0},{3,1},{4,6},{5,7},{6,4},{7,5},{8,10},{9,11},{10,... | collective-permute-start | bytes 196616 | tf_op jit(solution)/shard_map/ppermute | solution.py:19
  28.8 8.3 %copy-start.3 = (bf16[1,256,8,256]{1,3,2,0:T(8,128)(2,1)}, bf16[1,256,8,256]{1,3,2,0:T(8,128)(2,1)S(1)}, u32[]{:S(2)}) copy-start(bf16[1,256,8,256]{1,3,2,0:T(8,128)(2,1)S(1)} %copy.141) | copy-start | bytes 3145732
  34.4 0.6 copy-start.15
  35.0 127.6 %reduce-scatter.8.cloned.1.call-start = ((), (), s32[]{:S(2)}) async-start(), calls=%async_computation.7 | async-start | bytes 5242880 | tf_op jit(solution)/shard_map/reduce_scatter | solution.py:35
  39.4 19.2 %collective-permute-start.2 = (bf16[256,8,256]{0,2,1:T(8,128)(2,1)}, bf16[256,8,256]{0,2,1:T(8,128)(2,1)}, u32[]{:S(2)}, u32[]{:S(2)}) collective-permute-start(bf16[256,8,256]{0,2,1:T(8,128)(2,1)} %get-tuple-element.17), channel_id=1, source_target_pairs={{0,1},{1,0},{2,3},{3,2},{4,5},{5,4},{6,7},{7,6},{8,9},{9,8},{10,11... | collective-permute-start | bytes 3145736 | tf_op jit(solution)/shard_map/ppermute | solution.py:19
  42.2 37.7 %collective-permute-start.5 = (bf16[256,8,256]{2,0,1:T(8,128)(2,1)}, bf16[256,8,256]{2,0,1:T(8,128)(2,1)}, u32[]{:S(2)}, u32[]{:S(2)}) collective-permute-start(bf16[256,8,256]{2,0,1:T(8,128)(2,1)} %copy.93), channel_id=1, source_target_pairs={{0,2},{1,3},{2,0},{3,1},{4,6},{5,7},{6,4},{7,5},{8,10},{9,11},{10,... | collective-permute-start | bytes 3145736 | tf_op jit(solution)/shard_map/ppermute | solution.py:19
  53.7 3.1 copy-start.14
  56.8 1.8 copy-start.6
  87.1 1.1 copy-start.13
  102.6 111.0 %reduce-scatter.10.cloned.1.call-start = ((), (), s32[]{:S(2)}) async-start(), calls=%async_computation.8 | async-start | bytes 5242880 | tf_op jit(solution)/shard_map/reduce_scatter | solution.py:35
  102.6 28.1 %collective-permute-start.3 = (bf16[256,8,256]{0,2,1:T(8,128)(2,1)}, bf16[256,8,256]{0,2,1:T(8,128)(2,1)S(1)}, u32[]{:S(2)}, u32[]{:S(2)}) collective-permute-start(bf16[256,8,256]{0,2,1:T(8,128)(2,1)} %get-tuple-element.19), channel_id=1, source_target_pairs={{0,2},{1,3},{2,0},{3,1},{4,6},{5,7},{6,4},{7,5},{8,10},{9,11},{10,... | collective-permute-start | bytes 3145736 | tf_op jit(solution)/shard_map/ppermute | solution.py:19
  130.7 2.4 copy-start.11
  137.5 127.5 %reduce-scatter.6.cloned.1.call-start = ((), (), s32[]{:S(2)}) async-start(), calls=%async_computation.6 | async-start | bytes 5242880 | tf_op jit(solution)/shard_map/reduce_scatter | solution.py:35
  140.9 4.5 %collective-permute-start.6 = (f32[256,8,256]{0,2,1:T(8,128)}, f32[256,8,256]{0,2,1:T(8,128)}, u32[]{:S(2)}, u32[]{:S(2)}) collective-permute-start(f32[256,8,256]{0,2,1:T(8,128)} %convolution_bitcast_fusion), channel_id=1, source_target_pairs={{0,1},{1,0},{2,3},{3,2},{4,5},{5,4},{6,7},{7,6},{8,9},{9,8},{10,11... | collective-permute-start | bytes 6291464 | tf_op jit(solution)/shard_map/ppermute | solution.py:19
  145.4 4.2 %copy-start.5 = (bf16[256,1,2,4,256]{4,0,3,2,1:T(8,128)(2,1)S(1)}, bf16[256,1,2,4,256]{4,0,3,2,1:T(8,128)(2,1)}, u32[]{:S(2)}) copy-start(bf16[256,1,2,4,256]{4,0,3,2,1:T(8,128)(2,1)} %rev.8) | copy-start | bytes 3145732
  145.4 4.2 %copy-start.10 = (bf16[256,8,256]{2,0,1:T(8,128)(2,1)S(1)}, bf16[256,8,256]{2,0,1:T(8,128)(2,1)}, u32[]{:S(2)}) copy-start(bf16[256,8,256]{2,0,1:T(8,128)(2,1)} %copy.105) | copy-start | bytes 3145732
  149.6 119.3 %copy-start.7 = (bf16[256,8,256]{0,2,1:T(8,128)(2,1)}, bf16[256,8,256]{0,2,1:T(8,128)(2,1)S(1)}, u32[]{:S(2)}) copy-start(bf16[256,8,256]{0,2,1:T(8,128)(2,1)S(1)} %fusion.21) | copy-start | bytes 3145732
  162.6 148.3 %reduce-scatter.12.cloned.1.call-start = ((), (), s32[]{:S(2)}) async-start(), calls=%async_computation.9 | async-start | bytes 3932160 | tf_op jit(solution)/shard_map/reduce_scatter | solution.py:45
  268.9 73.5 %reduce-scatter.14.cloned.1.call-start = ((), (), s32[]{:S(2)}) async-start(), calls=%async_computation.10 | async-start | bytes 983040 | tf_op jit(solution)/shard_map/reduce_scatter | solution.py:45
  275.0 3.2 copy-start.4
  280.6 1.4 copy-start
  282.0 29.0 %copy-start.2 = (bf16[256,8,256]{0,2,1:T(8,128)(2,1)S(1)}, bf16[256,8,256]{0,2,1:T(8,128)(2,1)}, u32[]{:S(2)}) copy-start(bf16[256,8,256]{0,2,1:T(8,128)(2,1)} %get-tuple-element.19) | copy-start | bytes 3145732
  282.3 30.4 %collective-permute-start.7 = (f32[256]{0:T(256)S(1)}, f32[256]{0:T(256)S(1)}, u32[]{:S(2)}, u32[]{:S(2)}) collective-permute-start(f32[256]{0:T(256)S(1)} %fusion.3), channel_id=1, source_target_pairs={{0,1},{1,0},{2,3},{3,2},{4,5},{5,4},{6,7},{7,6},{8,9},{9,8},{10,11... | collective-permute-start | bytes 3080 | tf_op jit(solution)/shard_map/ppermute | solution.py:19
  310.9 7.7 %copy-start.9 = (bf16[1,256,8,256]{1,3,2,0:T(8,128)(2,1)S(1)}, bf16[1,256,8,256]{1,3,2,0:T(8,128)(2,1)}, u32[]{:S(2)}) copy-start(bf16[1,256,8,256]{1,3,2,0:T(8,128)(2,1)} %copy-done.8) | copy-start | bytes 3145732
  310.9 7.7 %copy-start.12 = (bf16[256,8,256]{0,2,1:T(8,128)(2,1)S(1)}, bf16[256,8,256]{0,2,1:T(8,128)(2,1)}, u32[]{:S(2)}) copy-start(bf16[256,8,256]{0,2,1:T(8,128)(2,1)} %copy-done.11) | copy-start | bytes 3145732
  312.8 7.6 %copy-start.1 = (f32[256,8,256]{0,2,1:T(8,128)S(1)}, f32[256,8,256]{0,2,1:T(8,128)}, u32[]{:S(2)}) copy-start(f32[256,8,256]{0,2,1:T(8,128)} %copy-done) | copy-start | bytes 6291460
  312.8 7.6 %collective-permute-start.8 = (f32[256]{0:T(256)S(1)}, f32[256]{0:T(256)S(1)}, u32[]{:S(2)}, u32[]{:S(2)}) collective-permute-start(f32[256]{0:T(256)S(1)} %add.105), channel_id=1, source_target_pairs={{0,2},{1,3},{2,0},{3,1},{4,6},{5,7},{6,4},{7,5},{8,10},{9,11},{10,... | collective-permute-start | bytes 3080 | tf_op jit(solution)/shard_map/ppermute | solution.py:19
Sparse Core Ops, SparseCore 0:
  35.1 47.9 all-gather.1
  102.7 58.9 reduce-scatter.7
  164.4 49.1 reduce-scatter.9
  215.9 49.0 reduce-scatter.5
  269.0 41.8 reduce-scatter.11
  314.0 28.3 reduce-scatter.13

commit v3 on v2

--- a/solution.py
+++ b/solution.py
@@ -87,6 +87,10 @@
     device_bits = blocks_dev.bit_length() - 1
     data_size = lax.axis_size(("dy", "dz", "dx"))
     grad_scale = 1.0 / math.sqrt(tok_rows * data_size)
+    top = FACTORS - 1
+    assert block_bits - 1 - device_bits == 1
+    cot_blocks = cotangent.reshape(tok_rows, blocks_dev, BLK)
+    partner_cot = swapped(cot_blocks, "tensor", 1)
     tokens_f32 = tokens.astype(jnp.float32)
     square_sum = tensor_sum(jnp.sum(tokens_f32 * tokens_f32, axis=1))
     inv_rms = lax.rsqrt(square_sum / D + epsilon)[:, None]
@@ -94,8 +98,7 @@
     hidden = normed.astype(jnp.bfloat16).reshape(tok_rows, blocks_dev, BLK)
     stored_inputs = []
     stored_preact = []
-    preact = None
-    for factor in range(FACTORS):
+    for factor in range(top):
         bit_index = block_bits - FACTORS + factor
         stride = 1 << bit_index
         if stride < blocks_dev:
@@ -105,52 +108,58 @@
         preact = apply_factor(hidden, partner, weights[factor])
         stored_inputs.append((hidden, partner))
         stored_preact.append(preact)
-        if factor < FACTORS - 1:
-            hidden = gelu_value(preact).astype(jnp.bfloat16)
-    mixed = (tokens_f32 + preact.reshape(tok_rows, local_width)).astype(jnp.bfloat16)
-    grad_pre = cotangent.reshape(tok_rows, blocks_dev, BLK)
-    grad_terms = []
-    grad_hidden = None
-    for factor in reversed(range(FACTORS)):
+        hidden = gelu_value(preact).astype(jnp.bfloat16)
+    hidden, partner_cot = lax.optimization_barrier((hidden, partner_cot))
+    partner_top = swapped(hidden, "tensor", 1)
+    top_weights = weights[top]
+    grad_hidden = jnp.einsum(
+        "tbd,cbd->tbc", cot_blocks, top_weights[:BLK], preferred_element_type=jnp.float32
+    ) + jnp.einsum(
+        "tbd,cbd->tbc",
+        partner_cot,
+        partner_rows(top_weights[BLK:]),
+        preferred_element_type=jnp.float32,
+    )
+    grad_pre = (grad_hidden * gelu_slope(stored_preact[top - 1])).astype(jnp.bfloat16)
+    grad_terms = [None] * FACTORS
+    for factor in reversed(range(top)):
         bit_index = block_bits - FACTORS + factor
         stride = 1 << bit_index
         kept_hidden, kept_partner = stored_inputs[factor]
         joined = jnp.concatenate([kept_hidden, kept_partner], axis=2)
-        grad_terms.append(
-            scatter_first(
-                jnp.einsum("tbc,tbd->cbd", joined, grad_pre, preferred_element_type=jnp.float32)
-                * grad_scale
-            )
+        grad_terms[factor] = scatter_first(
+            jnp.einsum("tbc,tbd->cbd", joined, grad_pre, preferred_element_type=jnp.float32)
+            * grad_scale
         )
         layer_weights = weights[factor]
         near_term = jnp.einsum(
             "tbd,cbd->tbc", grad_pre, layer_weights[:BLK], preferred_element_type=jnp.float32
         )
-        if stride < blocks_dev or factor < FACTORS - 1 or bit_index - device_bits != 1:
-            far_term = jnp.einsum(
-                "tbd,cbd->tbc", grad_pre, layer_weights[BLK:], preferred_element_type=jnp.float32
-            )
+        far_term = jnp.einsum(
+            "tbd,cbd->tbc", grad_pre, layer_weights[BLK:], preferred_element_type=jnp.float32
+        )
         if stride < blocks_dev:
             arrived = local_partner(far_term, stride)
-        elif factor < FACTORS - 1 or bit_index - device_bits != 1:
+        else:
             arrived = swapped(far_term, "tensor", bit_index - device_bits)
-        else:
-            arrived = jnp.einsum(
-                "tbd,cbd->tbc",
-                swapped(grad_pre, "tensor", 1),
-                partner_rows(layer_weights[BLK:]),
-                preferred_element_type=jnp.float32,
-            )
         grad_hidden = near_term + arrived
         if factor > 0:
             previous = stored_preact[factor - 1]
             grad_pre = (grad_hidden * gelu_slope(previous)).astype(jnp.bfloat16)
+    partner_top, _ = lax.optimization_barrier((partner_top, grad_hidden))
+    preact = apply_factor(hidden, partner_top, top_weights)
+    mixed = (tokens_f32 + preact.reshape(tok_rows, local_width)).astype(jnp.bfloat16)
+    joined = jnp.concatenate([hidden, partner_top], axis=2)
+    grad_terms[top] = scatter_first(
+        jnp.einsum("tbc,tbd->cbd", joined, cot_blocks, preferred_element_type=jnp.float32)
+        * grad_scale
+    )
     flat = grad_hidden.reshape(tok_rows, local_width)
     inner_sum = tensor_sum(jnp.sum(flat * normed, axis=1))
     token_grads = (
         cotangent.astype(jnp.float32) + inv_rms * (flat - normed * (inner_sum / D)[:, None])
     ).astype(jnp.bfloat16)
-    weight_grads = scatter_rest(grad_terms[::-1])
+    weight_grads = scatter_rest(grad_terms)
     return (mixed, token_grads, weight_grads)
 
 

time: 350 us -> 348 us (level)
  waiting for transfers between devices: 197 us -> 206 us
  local copies, waits for them, and re-layouts: 66.4 us -> 60.3 us
  matrix products: 41.2 us -> 36.7 us
    reduce_scatter x3, waiting for transfers between devices: 102 us -> 83 us  [scatter_first(): g = lax.psum_scatter(g, 'dx', scatter_dimension=0, tiled=True)]
    ppermute x9, waiting for transfers between devices: 46.3 us -> 61.9 us  [swapped(): lax.ppermute(x, axis, [(i, i ^ 1 << stride) for i in range(lax.axis_size(...]
    reduce_scatter x2, waiting for transfers between devices: 45.3 us -> 55.3 us  [scatter_rest(): g = lax.psum_scatter(g, axis, scatter_dimension=0, tiled=True)]
    dot_general x3 -> x2, matrix products: 9.69 us -> 4.17 us  [shards(): jnp.einsum('tbd,cbd->tbc', grad_pre, layer_weights[:BLK], preferred_eleme...]
    unnamed x42 -> x46, local copies, waits for them, and re-layouts: 21.9 us -> 17.1 us
    dot_general x1 -> x3, matrix products: 3.96 us -> 8.11 us  [the longest x1 3.96 us: shards(): jnp.einsum('tbd,cbd->tbc', partner_cot, partner_rows(top_weights[BLK:]),...]
    dot_general x2, matrix products: 6.45 us -> 2.31 us  [shards(): jnp.einsum('tbd,cbd->tbc', grad_pre, layer_weights[BLK:], preferred_eleme...]
    dot_general x3 -> x2, matrix products: 9.28 us -> 8.8 us  [shards(): jnp.einsum('tbc,tbd->cbd', joined, grad_pre, preferred_element_type=jnp.f...]
  transfers between devices with their start and end apart: 15 -> 15, of which waited for: 10 -> 8; matrix products, arithmetic and copies ran while one was open for 25% -> 22% of each run, Pallas kernels for 0% -> 0%
where the time goes in v3:
time: 348 us; the launch traced here: 347 us
  waiting for transfers between devices  206 us (59%)
  local copies, waits for them, and re-layouts  60.3 us (17%)
  matrix products  36.7 us (11%)
  starting transfers between devices  23.8 us (7%)
  between operations  14.5 us (4%)
  other arithmetic  6.63 us (2%)
    reduce_scatter x3, waiting for transfers between devices, scatter_first(): g = lax.psum_scatter(g, 'dx', scatter_dimension=0, tiled=True)  83 us
    ppermute x9, waiting for transfers between devices, swapped(): lax.ppermute(x, axis, [(i, i ^ 1 << stride) for i in range(lax.axis_size(...  61.9 us
    reduce_scatter x2, waiting for transfers between devices, scatter_rest(): g = lax.psum_scatter(g, axis, scatter_dimension=0, tiled=True)  55.3 us
    ppermute x9, starting transfers between devices, swapped(): lax.ppermute(x, axis, [(i, i ^ 1 << stride) for i in range(lax.axis_size(...  23.4 us
    unnamed x46, local copies, waits for them, and re-layouts  17.1 us
    mul x2, local copies, waits for them, and re-layouts, shards(): jnp.einsum('tbc,tbd->cbd', joined, grad_pre, preferred_element_type=jnp.f...  11 us
    transpose x2, local copies, waits for them, and re-layouts, scatter_first(): g = jnp.moveaxis(g, 2, 0).reshape(nx, -1, rest[-1])  9.44 us
    dot_general x2, matrix products, shards(): jnp.einsum('tbc,tbd->cbd', joined, grad_pre, preferred_element_type=jnp.f...  8.8 us
  transfers between devices with their start and end apart: 15, of which 8 were waited for; matrix products, arithmetic and copies ran while one was open for 22% of the time, Pallas kernels for 0%

profile of v3, /device:TPU:2, one launch (start us, length us, event | category | flops | bytes accessed | tf_op | source)
XLA Modules:
  0.0 347.5 jit_solution(5529882192654073510)
XLA Ops:
  7.2 1.5 copy.76
  8.7 0.3 fusion.8
  9.0 0.1 collective-permute-start
  9.1 5.2 %fusion.54 = (bf16[1,256,8,256]{3,2,1,0:T(8,128)(2,1)}, bf16[1,256,8,256]{3,2,1,0:T(8,128)(2,1)}, bf16[1,256,8,256]{3,2,1,0:T(8,128)(2,1)}, bf16[1,256,8,256]{3,...) fusion(bf16[3,512,8,256]{3,2,1,0:T(8,128)(2,1)} %param.4), kind=kLoop, calls=%fused_computation.79 | loop fusion | bytes 12582912 | tf_op jit(solution)/shard_map/slice | solution.py:79
  14.3 1.6 copy.140
  16.0 7.3 %collective-permute-start.1 = (f32[256]{0:T(256)S(1)}, f32[256]{0:T(256)S(1)}, u32[]{:S(2)}, u32[]{:S(2)}) collective-permute-start(f32[256]{0:T(256)S(1)} %add.84), channel_id=1, source_target_pairs={{0,2},{1,3},{2,0},{3,1},{4,6},{5,7},{6,4},{7,5},{8,10},{9,11},{10,... | collective-permute-start | bytes 3080 | tf_op jit(solution)/shard_map/ppermute | solution.py:19
  23.3 1.0 constant_dynamic-slice_fusion
  24.3 1.2 copy.93
  25.5 0.1 collective-permute-start.5
  25.6 2.4 copy.137
  28.0 1.6 copy.136
  29.6 0.2 fusion.2
  29.8 1.3 copy.79
  31.1 1.3 rev.8
  32.4 1.9 collective-permute-done.5
  34.4 0.6 copy-done.18
  35.1 1.8 fusion.46
  36.9 2.3 fusion.38
  39.2 1.0 copy.153
  40.3 4.0 %collective-permute-start.3 = (bf16[256,8,256]{2,0,1:T(8,128)(2,1)}, bf16[256,8,256]{2,0,1:T(8,128)(2,1)}, u32[]{:S(2)}, u32[]{:S(2)}) collective-permute-start(bf16[256,8,256]{2,0,1:T(8,128)(2,1)} %bitcast.137), channel_id=1, source_target_pairs={{0,2},{1,3},{2,0},{3,1},{4,6},{5,7},{6,4},{7,5},{8,10},{9,11},{10,... | collective-permute-start | bytes 3145736 | tf_op jit(solution)/shard_map/ppermute | solution.py:19
  44.3 1.6 copy.135
  46.0 1.8 fusion.41
  47.8 0.2 copy-done.13
  48.0 1.8 fusion.50
  49.8 3.7 %fusion.34 = (bf16[256,8,256]{0,2,1:T(8,128)(2,1)}, f32[8,256,256]{1,2,0:T(8,128)}) fusion(f32[8,256,256]{1,2,0:T(8,128)S(1)} %fusion.50, bf16[256,8,256]{0,2,1:T(8,128)(2,1)} %collective-permute-done.2, bf16[1,256,8,256]{3,2,1,0:T(8,128)(2,1)S(1)} %copy-done.3), kind=kOutput, calls=%fused_computation.47 | convolution fusion | flops 271581184 | bytes 7340032 | tf_op jit(solution)/shard_map/tbc,cbd->tbd/dot_general | solution.py:78
  53.5 24.3 %collective-permute-done.3 = bf16[256,8,256]{2,0,1:T(8,128)(2,1)} collective-permute-done((bf16[256,8,256]{2,0,1:T(8,128)(2,1)}, bf16[256,8,256]{2,0,1:T(8,128)(2,1)}, u32[]{:S(2)}, u32[]{:S(2)}) %collective-permute-start.3) | collective-permute-done | bytes 1048608 | tf_op jit(solution)/shard_map/ppermute | solution.py:19
  77.8 5.2 %all-gather.2.cloned.1.call-done = bf16[256,8,256]{2,0,1:T(8,128)(2,1)} async-done(((bf16[16,8,256]{2,0,1:T(8,128)(2,1)}), bf16[256,8,256]{2,0,1:T(8,128)(2,1)}) %all-gather.2.cloned.1.call-update) | async-done | bytes 1048592 | tf_op jit(solution)/shard_map/all_gather | solution.py:55
  83.0 4.0 %fusion.15 = bf16[256,8,256]{0,2,1:T(8,128)(2,1)S(1)} fusion(f32[8,256,256]{1,2,0:T(8,128)} %get-tuple-element.26, f32[8,256,256]{2,1,0:T(8,128)} %fusion.41, bf16[256,8,256]{2,0,1:T(8,128)(2,1)} %all-gather.2.cloned.1.call-done, bf16[256,8,256]{2,0,1:T(8,128)(2,1)} %collective-permute-done.3), kind=kOutput, calls=%fused_computation.24 | convolution fusion | flops 274202624 | bytes 7340032 | tf_op jit(solution)/shard_map/tbd,cbd->tbc/dot_general | solution.py:117
  87.0 1.0 copy-done.15
  88.0 4.2 %multiply_bitcast_fusion = f32[512,8,256]{0,2,1:T(8,128)} fusion(bf16[256,8,256]{0,2,1:T(8,128)(2,1)S(1)} %fusion.15, bf16[256,8,256]{0,2,1:T(8,128)(2,1)} %collective-permute-done.2, bf16[256,8,256]{0,2,1:T(8,128)(2,1)} %get-tuple-element.23), kind=kOutput, calls=%fused_computation | convolution fusion | flops 542113792 | bytes 7340032 | tf_op jit(solution)/shard_map/tbc,tbd->cbd/dot_general | solution.py:131
  92.2 5.5 %copy.109 = f32[512,8,256]{2,1,0:T(8,128)} copy(f32[512,8,256]{0,2,1:T(8,128)} %multiply_bitcast_fusion) | data formatting | bytes 8388608 | tf_op jit(solution)/shard_map/mul | solution.py:131
  97.8 4.6 %copy.110 = f32[4,4,4,8,8,256]{5,4,3,2,1,0:T(8,128)} copy(f32[4,4,4,8,8,256]{5,4,3,0,2,1:T(8,128)} %bitcast.145) | data formatting | bytes 8388608 | tf_op jit(solution)/shard_map/transpose | solution.py:34
  102.5 0.2 reduce-scatter.10.cloned.1.call-start
  102.7 1.8 convolution_bitcast_fusion
  104.5 0.1 collective-permute-start.6
  104.6 5.8 %collective-permute-start.4 = (bf16[256,8,256]{0,2,1:T(8,128)(2,1)}, bf16[256,8,256]{0,2,1:T(8,128)(2,1)}, u32[]{:S(2)}, u32[]{:S(2)}) collective-permute-start(bf16[256,8,256]{0,2,1:T(8,128)(2,1)} %get-tuple-element.6), channel_id=1, source_target_pairs={{0,2},{1,3},{2,0},{3,1},{4,6},{5,7},{6,4},{7,5},{8,10},{9,11},{10,... | collective-permute-start | bytes 3145736 | tf_op jit(solution)/shard_map/ppermute | solution.py:19
  110.5 1.4 fusion.21
  111.9 0.5 fusion.44
  112.4 0.5 copy-done.6
  112.8 1.9 copy.102
  114.8 3.1 rev.9
  117.8 2.8 bitcast_add_fusion
  120.7 35.6 %collective-permute-done.4 = bf16[256,8,256]{0,2,1:T(8,128)(2,1)} collective-permute-done((bf16[256,8,256]{0,2,1:T(8,128)(2,1)}, bf16[256,8,256]{0,2,1:T(8,128)(2,1)}, u32[]{:S(2)}, u32[]{:S(2)}) %collective-permute-start.4) | collective-permute-done | bytes 1048608 | tf_op jit(solution)/shard_map/ppermute | solution.py:19
  156.3 2.3 convolution_multiply_fusion
  158.6 4.5 %copy.112 = f32[4,4,4,8,8,256]{5,4,3,1,0,2:T(8,128)} copy(f32[4,4,4,8,8,256]{5,3,2,1,0,4:T(8,128)S(1)} %bitcast.138) | data formatting | bytes 8388608 | tf_op jit(solution)/shard_map/reshape | solution.py:33
  163.1 2.3 copy.105
  165.4 4.6 %multiply_bitcast_fusion.1 = f32[512,8,256]{0,2,1:T(8,128)} fusion(bf16[256,8,256]{0,2,1:T(8,128)(2,1)} %copy-done.6, bf16[256,8,256]{2,0,1:T(8,128)(2,1)} %bitcast.152, bf16[256,8,256]{2,0,1:T(8,128)(2,1)} %copy.105), kind=kOutput, calls=%fused_computation.1 | convolution fusion | flops 542113792 | bytes 7340032 | tf_op jit(solution)/shard_map/tbc,tbd->cbd/dot_general | solution.py:131
  169.9 5.4 %copy.106 = f32[512,8,256]{2,1,0:T(8,128)} copy(f32[512,8,256]{0,2,1:T(8,128)} %multiply_bitcast_fusion.1) | data formatting | bytes 8388608 | tf_op jit(solution)/shard_map/mul | solution.py:131
  175.4 4.8 %copy.107 = f32[4,4,4,8,8,256]{5,4,3,2,1,0:T(8,128)} copy(f32[4,4,4,8,8,256]{5,4,3,0,2,1:T(8,128)} %bitcast.146) | data formatting | bytes 8388608 | tf_op jit(solution)/shard_map/transpose | solution.py:34
  180.2 0.0 reduce-scatter.12.cloned.1.call-start
  180.3 31.5 %reduce-scatter.10.cloned.1.call-done = f32[1,1024,256]{2,1,0:T(8,128)} async-done(((f32[4,1024,256]{2,1,0:T(8,128)}), f32[1,1024,256]{2,1,0:T(8,128)}) %reduce-scatter.10.cloned.1.call-update) | async-done | bytes 1048592 | tf_op jit(solution)/shard_map/reduce_scatter | solution.py:35
  211.7 51.5 %reduce-scatter.6.cloned.1.call-done = f32[1,1024,256]{2,1,0:T(8,128)} async-done(((f32[4,1024,256]{2,1,0:T(8,128)}), f32[1,1024,256]{2,1,0:T(8,128)}) %reduce-scatter.6.cloned.1.call-update) | async-done | bytes 1048592 | tf_op jit(solution)/shard_map/reduce_scatter | solution.py:35
  263.3 3.8 %pad_maximum_fusion = f32[4,4,3,8,8,256]{5,4,3,2,1,0:T(8,128)} fusion(f32[4,4,1,8,8,256]{5,4,3,2,1,0:T(8,128)} %bitcast.155, f32[4,4,1,8,8,256]{5,4,3,2,1,0:T(8,128)} %bitcast.154, f32[4,4,1,8,8,256]{5,4,3,2,1,0:T(8,128)} %bitcast.156), kind=kLoop, calls=%fused_computation.2 | loop fusion | flops 1572864 | bytes 6291456 | tf_op jit(solution)/shard_map/stack | solution.py:42
  267.2 2.3 copy.104
  269.5 0.3 fusion.3
  269.8 0.1 collective-permute-start.7
  269.9 39.2 %reduce-scatter.12.cloned.1.call-done = f32[1,768,256]{2,1,0:T(8,128)} async-done(((f32[4,768,256]{2,1,0:T(8,128)}), f32[1,768,256]{2,1,0:T(8,128)}) %reduce-scatter.12.cloned.1.call-update) | async-done | bytes 786448 | tf_op jit(solution)/shard_map/reduce_scatter | solution.py:45
  309.1 2.1 fusion.39
  311.2 5.8 %collective-permute-start.8 = (f32[256]{0:T(256)S(1)}, f32[256]{0:T(256)S(1)}, u32[]{:S(2)}, u32[]{:S(2)}) collective-permute-start(f32[256]{0:T(256)S(1)} %add.105), channel_id=1, source_target_pairs={{0,2},{1,3},{2,0},{3,1},{4,6},{5,7},{6,4},{7,5},{8,10},{9,11},{10,... | collective-permute-start | bytes 3080 | tf_op jit(solution)/shard_map/ppermute | solution.py:19
  317.1 1.7 convolution_add_fusion
  318.8 1.9 fusion.7
  320.7 2.4 copy.116
  323.1 1.4 copy.117
  324.5 16.1 %reduce-scatter.14.cloned.1.call-done = f32[1,192,256]{2,1,0:T(8,128)} async-done(((f32[4,192,256]{2,1,0:T(8,128)}), f32[1,192,256]{2,1,0:T(8,128)}) %reduce-scatter.14.cloned.1.call-update) | async-done | bytes 196624 | tf_op jit(solution)/shard_map/reduce_scatter | solution.py:45
  (56 shorter events, 0.4 us)
Async XLA Ops:
  7.2 75.9 %all-gather.2.cloned.1.call-start = ((), (), s32[]{:S(2)}) async-start(), calls=%async_computation.5 | async-start | bytes 1114112 | tf_op jit(solution)/shard_map/all_gather | solution.py:55
  9.0 7.0 %collective-permute-start = (f32[256]{0:T(256)S(1)}, f32[256]{0:T(256)S(1)}, u32[]{:S(2)}, u32[]{:S(2)}) collective-permute-start(f32[256]{0:T(256)S(1)} %fusion.8), channel_id=1, source_target_pairs={{0,1},{1,0},{2,3},{3,2},{4,5},{5,4},{6,7},{7,6},{8,9},{9,8},{10,11... | collective-permute-start | bytes 3080 | tf_op jit(solution)/shard_map/ppermute | solution.py:19
  16.0 13.6 %copy-start.10 = (bf16[1,256,8,256]{1,3,2,0:T(8,128)(2,1)}, bf16[1,256,8,256]{1,3,2,0:T(8,128)(2,1)S(1)}, u32[]{:S(2)}) copy-start(bf16[1,256,8,256]{1,3,2,0:T(8,128)(2,1)S(1)} %copy.140) | copy-start | bytes 3145732
  16.0 13.6 %collective-permute-start.1 = (f32[256]{0:T(256)S(1)}, f32[256]{0:T(256)S(1)}, u32[]{:S(2)}, u32[]{:S(2)}) collective-permute-start(f32[256]{0:T(256)S(1)} %add.84), channel_id=1, source_target_pairs={{0,2},{1,3},{2,0},{3,1},{4,6},{5,7},{6,4},{7,5},{8,10},{9,11},{10,... | collective-permute-start | bytes 3080 | tf_op jit(solution)/shard_map/ppermute | solution.py:19
  25.5 8.9 %collective-permute-start.5 = (bf16[16,8,256]{2,0,1:T(8,128)(2,1)S(1)}, bf16[16,8,256]{2,0,1:T(8,128)(2,1)S(1)}, u32[]{:S(2)}, u32[]{:S(2)}) collective-permute-start(bf16[16,8,256]{2,0,1:T(8,128)(2,1)S(1)} %bitcast.158), channel_id=1, source_target_pairs={{0,2},{1,3},{2,0},{3,1},{4,6},{5,7},{6,4},{7,5},{8,10},{9,11},{10,... | collective-permute-start | bytes 196616 | tf_op jit(solution)/shard_map/ppermute | solution.py:19
  29.8 7.1 %copy-start = (bf16[256,2048]{0,1:T(8,128)(2,1)}, bf16[256,2048]{0,1:T(8,128)(2,1)S(1)}, u32[]{:S(2)}) copy-start(bf16[256,2048]{0,1:T(8,128)(2,1)S(1)} %fusion.2) | copy-start | bytes 3145732
  32.4 4.4 %copy-start.4 = (bf16[256,1,2,4,256]{4,0,3,2,1:T(8,128)(2,1)}, bf16[256,1,2,4,256]{4,0,3,2,1:T(8,128)(2,1)S(1)}, u32[]{:S(2)}) copy-start(bf16[256,1,2,4,256]{4,0,3,2,1:T(8,128)(2,1)S(1)} %rev.8) | copy-start | bytes 3145732
  34.4 0.6 copy-start.18
  35.0 145.3 %reduce-scatter.8.cloned.1.call-start = ((), (), s32[]{:S(2)}) async-start(), calls=%async_computation.7 | async-start | bytes 5242880 | tf_op jit(solution)/shard_map/reduce_scatter | solution.py:35
  35.1 1.8 copy-start.5
  36.9 2.3 copy-start.1
  39.2 10.6 %collective-permute-start.2 = (bf16[256,8,256]{0,2,1:T(8,128)(2,1)}, bf16[256,8,256]{0,2,1:T(8,128)(2,1)}, u32[]{:S(2)}, u32[]{:S(2)}) collective-permute-start(bf16[256,8,256]{0,2,1:T(8,128)(2,1)} %get-tuple-element.23), channel_id=1, source_target_pairs={{0,1},{1,0},{2,3},{3,2},{4,5},{5,4},{6,7},{7,6},{8,9},{9,8},{10,11... | collective-permute-start | bytes 3145736 | tf_op jit(solution)/shard_map/ppermute | solution.py:19
  40.3 37.6 %collective-permute-start.3 = (bf16[256,8,256]{2,0,1:T(8,128)(2,1)}, bf16[256,8,256]{2,0,1:T(8,128)(2,1)}, u32[]{:S(2)}, u32[]{:S(2)}) collective-permute-start(bf16[256,8,256]{2,0,1:T(8,128)(2,1)} %bitcast.137), channel_id=1, source_target_pairs={{0,2},{1,3},{2,0},{3,1},{4,6},{5,7},{6,4},{7,5},{8,10},{9,11},{10,... | collective-permute-start | bytes 3145736 | tf_op jit(solution)/shard_map/ppermute | solution.py:19
  45.9 1.9 copy-start.7
  45.9 2.0 copy-start.13
  48.0 1.8 copy-start.3
  87.0 1.0 copy-start.15
  102.4 8.0 %copy-start.14 = (bf16[1,256,8,256]{3,2,1,0:T(8,128)(2,1)S(1)}, bf16[1,256,8,256]{3,2,1,0:T(8,128)(2,1)}, u32[]{:S(2)}) copy-start(bf16[1,256,8,256]{3,2,1,0:T(8,128)(2,1)} %get-tuple-element.16) | copy-start | bytes 3145732
  102.5 109.3 %reduce-scatter.10.cloned.1.call-start = ((), (), s32[]{:S(2)}) async-start(), calls=%async_computation.8 | async-start | bytes 5242880 | tf_op jit(solution)/shard_map/reduce_scatter | solution.py:35
  102.7 7.8 %copy-start.16 = (bf16[256,8,256]{0,2,1:T(8,128)(2,1)S(1)}, bf16[256,8,256]{0,2,1:T(8,128)(2,1)}, u32[]{:S(2)}) copy-start(bf16[256,8,256]{0,2,1:T(8,128)(2,1)} %copy-done.15) | copy-start | bytes 3145732
  102.7 7.8 %copy-start.17 = (f32[8,256,256]{1,2,0:T(8,128)S(1)}, f32[8,256,256]{1,2,0:T(8,128)}, u32[]{:S(2)}) copy-start(f32[8,256,256]{1,2,0:T(8,128)} %get-tuple-element.24) | copy-start | bytes 6291460
  104.5 5.9 %collective-permute-start.6 = (f32[256,8,256]{0,2,1:T(8,128)S(1)}, f32[256,8,256]{0,2,1:T(8,128)S(1)}, u32[]{:S(2)}, u32[]{:S(2)}) collective-permute-start(f32[256,8,256]{0,2,1:T(8,128)S(1)} %convolution_bitcast_fusion), channel_id=1, source_target_pairs={{0,1},{1,0},{2,3},{3,2},{4,5},{5,4},{6,7},{7,6},{8,9},{9,8},{10,11... | collective-permute-start | bytes 6291464 | tf_op jit(solution)/shard_map/ppermute | solution.py:19
  104.6 51.7 %collective-permute-start.4 = (bf16[256,8,256]{0,2,1:T(8,128)(2,1)}, bf16[256,8,256]{0,2,1:T(8,128)(2,1)}, u32[]{:S(2)}, u32[]{:S(2)}) collective-permute-start(bf16[256,8,256]{0,2,1:T(8,128)(2,1)} %get-tuple-element.6), channel_id=1, source_target_pairs={{0,2},{1,3},{2,0},{3,1},{4,6},{5,7},{6,4},{7,5},{8,10},{9,11},{10,... | collective-permute-start | bytes 3145736 | tf_op jit(solution)/shard_map/ppermute | solution.py:19
  110.5 1.4 copy-start.9
  111.9 1.0 copy-start.6
  117.8 38.4 %copy-start.2 = (bf16[256,2048]{1,0:T(8,128)(2,1)S(1)}, bf16[256,2048]{1,0:T(8,128)(2,1)}, u32[]{:S(2)}) copy-start(bf16[256,2048]{1,0:T(8,128)(2,1)} %param.5) | copy-start | bytes 3145732
  163.1 100.2 %reduce-scatter.6.cloned.1.call-start = ((), (), s32[]{:S(2)}) async-start(), calls=%async_computation.6 | async-start | bytes 5242880 | tf_op jit(solution)/shard_map/reduce_scatter | solution.py:35
  180.2 128.9 %reduce-scatter.12.cloned.1.call-start = ((), (), s32[]{:S(2)}) async-start(), calls=%async_computation.9 | async-start | bytes 3932160 | tf_op jit(solution)/shard_map/reduce_scatter | solution.py:45
  267.1 73.5 %reduce-scatter.14.cloned.1.call-start = ((), (), s32[]{:S(2)}) async-start(), calls=%async_computation.10 | async-start | bytes 983040 | tf_op jit(solution)/shard_map/reduce_scatter | solution.py:45
  269.8 41.4 %collective-permute-start.7 = (f32[256]{0:T(256)S(1)}, f32[256]{0:T(256)S(1)}, u32[]{:S(2)}, u32[]{:S(2)}) collective-permute-start(f32[256]{0:T(256)S(1)} %fusion.3), channel_id=1, source_target_pairs={{0,1},{1,0},{2,3},{3,2},{4,5},{5,4},{6,7},{7,6},{8,9},{9,8},{10,11... | collective-permute-start | bytes 3080 | tf_op jit(solution)/shard_map/ppermute | solution.py:19
  309.1 8.0 %copy-start.8 = (bf16[1,256,8,256]{1,3,2,0:T(8,128)(2,1)S(1)}, bf16[1,256,8,256]{1,3,2,0:T(8,128)(2,1)}, u32[]{:S(2)}) copy-start(bf16[1,256,8,256]{1,3,2,0:T(8,128)(2,1)} %copy-done.7) | copy-start | bytes 3145732
  311.2 7.6 %copy-start.11 = (bf16[256,2048]{0,1:T(8,128)(2,1)S(1)}, bf16[256,2048]{0,1:T(8,128)(2,1)}, u32[]{:S(2)}) copy-start(bf16[256,2048]{0,1:T(8,128)(2,1)} %copy.104) | copy-start | bytes 3145732
  311.2 7.6 %collective-permute-start.8 = (f32[256]{0:T(256)S(1)}, f32[256]{0:T(256)S(1)}, u32[]{:S(2)}, u32[]{:S(2)}) collective-permute-start(f32[256]{0:T(256)S(1)} %add.105), channel_id=1, source_target_pairs={{0,2},{1,3},{2,0},{3,1},{4,6},{5,7},{6,4},{7,5},{8,10},{9,11},{10,... | collective-permute-start | bytes 3080 | tf_op jit(solution)/shard_map/ppermute | solution.py:19
  320.7 2.4 copy-start.12
Sparse Core Ops, SparseCore 0:
  35.1 47.8 all-gather.1
  102.6 56.9 reduce-scatter.7
  163.2 48.4 reduce-scatter.9
  214.1 49.0 reduce-scatter.5
  267.3 41.7 reduce-scatter.11
  312.3 28.3 reduce-scatter.13

commit v4 on v3

--- a/solution.py
+++ b/solution.py
@@ -36,14 +36,26 @@
     return g.reshape((ny, nz, share) + rest)
 
 
-def scatter_rest(parts):
-    ny, nz, share = parts[0].shape[:3]
-    rest = parts[0].shape[3:]
-    g = jnp.stack(parts, axis=2)
-    for axis, size in (("dy", ny), ("dz", nz)):
-        g = g.reshape(size, -1, rest[-1])
-        g = lax.psum_scatter(g, axis, scatter_dimension=0, tiled=True)
-    return g.reshape((len(parts), share) + rest)
+def exchange_sum(g, axis):
+    return jnp.sum(lax.all_to_all(g, axis, 0, 0), axis=0)
+
+
+def scatter_by_exchange(grads):
+    rows = grads.shape[0]
+    rest = grads.shape[1:]
+    ny, nz, nx = (lax.axis_size(a) for a in ("dy", "dz", "dx"))
+    g = grads.reshape((ny, nz, nx, rows // (ny * nz * nx)) + rest)
+    g = exchange_sum(g, "dy")
+    return exchange_sum(jnp.moveaxis(g, 1, 0), "dx")
+
+
+def scatter_rest(sc_parts, tc_parts):
+    ny, nz = sc_parts[0].shape[:2]
+    g = jnp.stack(sc_parts, axis=1)
+    shape = g.shape[1:]
+    g = lax.psum_scatter(g.reshape(ny, -1, g.shape[-1]), "dy", scatter_dimension=0, tiled=True)
+    g = jnp.concatenate([g.reshape(shape), jnp.stack(tc_parts, axis=0)], axis=0)
+    return exchange_sum(jnp.moveaxis(g, 1, 0), "dz")
 
 
 def partner_rows(rows):
@@ -150,7 +162,7 @@
     preact = apply_factor(hidden, partner_top, top_weights)
     mixed = (tokens_f32 + preact.reshape(tok_rows, local_width)).astype(jnp.bfloat16)
     joined = jnp.concatenate([hidden, partner_top], axis=2)
-    grad_terms[top] = scatter_first(
+    top_term = scatter_by_exchange(
         jnp.einsum("tbc,tbd->cbd", joined, cot_blocks, preferred_element_type=jnp.float32)
         * grad_scale
     )
@@ -159,7 +171,7 @@
     token_grads = (
         cotangent.astype(jnp.float32) + inv_rms * (flat - normed * (inner_sum / D)[:, None])
     ).astype(jnp.bfloat16)
-    weight_grads = scatter_rest(grad_terms)
+    weight_grads = scatter_rest(grad_terms[:top], [top_term])
     return (mixed, token_grads, weight_grads)
 
 

time: 348 us -> 350 us (level)
  waiting for transfers between devices: 206 us -> 114 us
  blocking collectives: 0 us -> 69.9 us
  starting transfers between devices: 23.8 us -> 34.2 us
  other arithmetic: 6.63 us -> 14.8 us
  matrix products: 36.7 us -> 43.8 us
    all_to_all x0 -> x1, blocking collectives: none -> 69.9 us  [exchange_sum(): return jnp.sum(lax.all_to_all(g, axis, 0, 0), axis=0)]
    reduce_scatter x2 -> x1, waiting for transfers between devices: 55.3 us -> 0.02 us  [scatter_rest(): lax.psum_scatter(g.reshape(ny, -1, g.shape[-1]), 'dy', scatter_dimension=...]
    reduce_scatter x3 -> x2, waiting for transfers between devices: 83 us -> 53.8 us  [scatter_first(): g = lax.psum_scatter(g, 'dx', scatter_dimension=0, tiled=True)]
    ppermute x9, waiting for transfers between devices: 61.9 us -> 44.6 us  [swapped(): lax.ppermute(x, axis, [(i, i ^ 1 << stride) for i in range(lax.axis_size(...]
    all_to_all x0 -> x2, waiting for transfers between devices: none -> 11 us  [exchange_sum(): return jnp.sum(lax.all_to_all(g, axis, 0, 0), axis=0)]
    all_to_all x0 -> x2, starting transfers between devices: none -> 10.8 us  [exchange_sum(): return jnp.sum(lax.all_to_all(g, axis, 0, 0), axis=0)]
    reduce_sum x0 -> x3, other arithmetic: none -> 6.9 us  [exchange_sum(): return jnp.sum(lax.all_to_all(g, axis, 0, 0), axis=0)]
    reshape x1, local copies, waits for them, and re-layouts: 4.46 us -> 0.58 us  [scatter_by_exchange(): g = grads.reshape((ny, nz, nx, rows // (ny * nz * nx)) + rest)]
  transfers between devices with their start and end apart: 15 -> 15, of which waited for: 8 -> 9; matrix products, arithmetic and copies ran while one was open for 22% -> 25% of each run, Pallas kernels for 0% -> 0%
where the time goes in v4:
time: 350 us; the launch traced here: 348 us
  waiting for transfers between devices  114 us (33%)
  blocking collectives  69.9 us (20%)
  local copies, waits for them, and re-layouts  57.2 us (16%)
  matrix products  43.8 us (13%)
  starting transfers between devices  34.2 us (10%)
  other arithmetic  14.8 us (4%)
  between operations  14 us (4%)
    all_to_all x1, blocking collectives, exchange_sum(): return jnp.sum(lax.all_to_all(g, axis, 0, 0), axis=0)  69.9 us
    reduce_scatter x2, waiting for transfers between devices, scatter_first(): g = lax.psum_scatter(g, 'dx', scatter_dimension=0, tiled=True)  53.8 us
    ppermute x9, waiting for transfers between devices, swapped(): lax.ppermute(x, axis, [(i, i ^ 1 << stride) for i in range(lax.axis_size(...  44.6 us
    ppermute x9, starting transfers between devices, swapped(): lax.ppermute(x, axis, [(i, i ^ 1 << stride) for i in range(lax.axis_size(...  23.1 us
    unnamed x36, local copies, waits for them, and re-layouts  17.9 us
    mul x2, local copies, waits for them, and re-layouts, shards(): jnp.einsum('tbc,tbd->cbd', joined, grad_pre, preferred_element_type=jnp.f...  11 us
    all_to_all x2, waiting for transfers between devices, exchange_sum(): return jnp.sum(lax.all_to_all(g, axis, 0, 0), axis=0)  11 us
    all_to_all x2, starting transfers between devices, exchange_sum(): return jnp.sum(lax.all_to_all(g, axis, 0, 0), axis=0)  10.8 us
  transfers between devices with their start and end apart: 15, of which 9 were waited for; matrix products, arithmetic and copies ran while one was open for 25% of the time, Pallas kernels for 0%

profile of v4, /device:TPU:2, one launch (start us, length us, event | category | flops | bytes accessed | tf_op | source)
XLA Modules:
  0.0 348.3 jit_solution(12716663050523471345)
XLA Ops:
  7.2 1.5 copy.77
  9.1 5.3 %fusion.54 = (bf16[1,256,8,256]{3,2,1,0:T(8,128)(2,1)}, bf16[1,256,8,256]{3,2,1,0:T(8,128)(2,1)}, bf16[1,256,8,256]{3,2,1,0:T(8,128)(2,1)}, bf16[1,256,8,256]{3,...) fusion(bf16[3,512,8,256]{3,2,1,0:T(8,128)(2,1)} %param.4), kind=kLoop, calls=%fused_computation.80 | loop fusion | bytes 12582912 | tf_op jit(solution)/shard_map/slice | solution.py:91
  14.4 1.6 copy.144
  16.0 7.3 %collective-permute-start.1 = (f32[256]{0:T(256)S(1)}, f32[256]{0:T(256)S(1)}, u32[]{:S(2)}, u32[]{:S(2)}) collective-permute-start(f32[256]{0:T(256)S(1)} %add.80), channel_id=1, source_target_pairs={{0,2},{1,3},{2,0},{3,1},{4,6},{5,7},{6,4},{7,5},{8,10},{9,11},{10,... | collective-permute-start | bytes 3080 | tf_op jit(solution)/shard_map/ppermute | solution.py:19
  23.3 1.0 constant_dynamic-slice_fusion
  24.3 1.2 copy.94
  25.6 2.4 copy.140
  28.0 1.6 copy.139
  29.8 1.3 copy.80
  31.1 1.3 rev.8
  32.4 2.0 collective-permute-done.5
  34.4 0.6 copy-done.13
  35.1 1.8 fusion.46
  36.9 2.3 fusion.38
  39.3 1.0 copy.159
  40.3 4.0 %collective-permute-start.3 = (bf16[256,8,256]{2,0,1:T(8,128)(2,1)}, bf16[256,8,256]{2,0,1:T(8,128)(2,1)}, u32[]{:S(2)}, u32[]{:S(2)}) collective-permute-start(bf16[256,8,256]{2,0,1:T(8,128)(2,1)} %bitcast.134), channel_id=1, source_target_pairs={{0,2},{1,3},{2,0},{3,1},{4,6},{5,7},{6,4},{7,5},{8,10},{9,11},{10,... | collective-permute-start | bytes 3145736 | tf_op jit(solution)/shard_map/ppermute | solution.py:19
  44.3 2.4 copy.143
  46.7 3.1 fusion.41
  49.8 1.8 fusion.50
  51.7 3.7 %fusion.34 = (bf16[256,8,256]{0,2,1:T(8,128)(2,1)}, f32[8,256,256]{1,2,0:T(8,128)}) fusion(f32[8,256,256]{1,2,0:T(8,128)S(1)} %fusion.50, bf16[256,8,256]{0,2,1:T(8,128)(2,1)} %collective-permute-done.2, bf16[1,256,8,256]{3,2,1,0:T(8,128)(2,1)S(1)} %copy-done.1), kind=kOutput, calls=%fused_computation.47 | convolution fusion | flops 271581184 | bytes 7340032 | tf_op jit(solution)/shard_map/tbc,cbd->tbd/dot_general | solution.py:90
  55.4 22.8 %collective-permute-done.3 = bf16[256,8,256]{2,0,1:T(8,128)(2,1)} collective-permute-done((bf16[256,8,256]{2,0,1:T(8,128)(2,1)}, bf16[256,8,256]{2,0,1:T(8,128)(2,1)}, u32[]{:S(2)}, u32[]{:S(2)}) %collective-permute-start.3) | collective-permute-done | bytes 1048608 | tf_op jit(solution)/shard_map/ppermute | solution.py:19
  78.1 4.9 %all-gather.2.cloned.1.call-done = bf16[256,8,256]{2,0,1:T(8,128)(2,1)} async-done(((bf16[16,8,256]{2,0,1:T(8,128)(2,1)}), bf16[256,8,256]{2,0,1:T(8,128)(2,1)}) %all-gather.2.cloned.1.call-update) | async-done | bytes 1048592 | tf_op jit(solution)/shard_map/all_gather | solution.py:67
  83.0 4.0 %fusion.15 = bf16[256,8,256]{0,2,1:T(8,128)(2,1)S(1)} fusion(f32[8,256,256]{1,2,0:T(8,128)} %get-tuple-element.26, f32[8,256,256]{2,1,0:T(8,128)} %fusion.41, bf16[256,8,256]{2,0,1:T(8,128)(2,1)} %all-gather.2.cloned.1.call-done, bf16[256,8,256]{2,0,1:T(8,128)(2,1)} %collective-permute-done.3), kind=kOutput, calls=%fused_computation.23 | convolution fusion | flops 274202624 | bytes 7340032 | tf_op jit(solution)/shard_map/tbd,cbd->tbc/dot_general | solution.py:129
  87.0 1.0 copy-done.12
  88.0 4.2 %multiply_bitcast_fusion = f32[512,8,256]{0,2,1:T(8,128)} fusion(bf16[256,8,256]{0,2,1:T(8,128)(2,1)S(1)} %fusion.15, bf16[256,8,256]{0,2,1:T(8,128)(2,1)} %collective-permute-done.2, bf16[256,8,256]{0,2,1:T(8,128)(2,1)} %get-tuple-element.23), kind=kOutput, calls=%fused_computation | convolution fusion | flops 542113792 | bytes 7340032 | tf_op jit(solution)/shard_map/tbc,tbd->cbd/dot_general | solution.py:143
  92.2 5.5 %copy.110 = f32[512,8,256]{2,1,0:T(8,128)} copy(f32[512,8,256]{0,2,1:T(8,128)} %multiply_bitcast_fusion) | data formatting | bytes 8388608 | tf_op jit(solution)/shard_map/mul | solution.py:143
  97.7 4.6 %copy.111 = f32[4,4,4,8,8,256]{5,4,3,2,1,0:T(8,128)} copy(f32[4,4,4,8,8,256]{5,4,3,0,2,1:T(8,128)} %bitcast.141) | data formatting | bytes 8388608 | tf_op jit(solution)/shard_map/transpose | solution.py:34
  102.6 3.0 convolution_bitcast_fusion
  105.6 0.5 copy.106
  106.2 4.0 %collective-permute-done.6 = f32[256,8,256]{0,2,1:T(8,128)} collective-permute-done((f32[256,8,256]{0,2,1:T(8,128)}, f32[256,8,256]{0,2,1:T(8,128)}, u32[]{:S(2)}, u32[]{:S(2)}) %collective-permute-start.6) | collective-permute-done | bytes 2097184 | tf_op jit(solution)/shard_map/ppermute | solution.py:19
  110.1 4.1 %fusion.21 = bf16[256,8,256]{0,2,1:T(8,128)(2,1)S(1)} fusion(f32[256,8,256]{0,2,1:T(8,128)} %collective-permute-done.6, f32[8,256,256]{1,2,0:T(8,128)} %get-tuple-element.24, bf16[256,8,256]{0,2,1:T(8,128)(2,1)} %copy-done.12, bf16[1,256,8,256]{3,2,1,0:T(8,128)(2,1)} %get-tuple-element.17), kind=kOutput, calls=%fused_computation.29 | convolution fusion | flops 274202624 | bytes 7340032 | tf_op jit(solution)/shard_map/tbd,cbd->tbc/dot_general | solution.py:147
  114.3 2.7 multiply_bitcast_fusion.1
  117.0 5.5 %copy.107 = f32[512,8,256]{2,1,0:T(8,128)} copy(f32[512,8,256]{0,2,1:T(8,128)} %multiply_bitcast_fusion.1) | data formatting | bytes 8388608 | tf_op jit(solution)/shard_map/mul | solution.py:143
  122.5 5.1 %copy.108 = f32[4,4,4,8,8,256]{5,4,3,2,1,0:T(8,128)} copy(f32[4,4,4,8,8,256]{5,4,3,0,2,1:T(8,128)} %bitcast.142) | data formatting | bytes 8388608 | tf_op jit(solution)/shard_map/transpose | solution.py:34
  127.7 5.8 %collective-permute-start.4 = (bf16[256,8,256]{0,2,1:T(8,128)(2,1)}, bf16[256,8,256]{0,2,1:T(8,128)(2,1)}, u32[]{:S(2)}, u32[]{:S(2)}) collective-permute-start(bf16[256,8,256]{0,2,1:T(8,128)(2,1)} %get-tuple-element.6), channel_id=1, source_target_pairs={{0,2},{1,3},{2,0},{3,1},{4,6},{5,7},{6,4},{7,5},{8,10},{9,11},{10,... | collective-permute-start | bytes 3145736 | tf_op jit(solution)/shard_map/ppermute | solution.py:19
  133.5 1.9 fusion.44
  135.4 1.9 copy.103
  137.3 1.6 rev.9
  138.9 2.8 bitcast_add_fusion
  141.7 15.9 %collective-permute-done.4 = bf16[256,8,256]{0,2,1:T(8,128)(2,1)} collective-permute-done((bf16[256,8,256]{0,2,1:T(8,128)(2,1)}, bf16[256,8,256]{0,2,1:T(8,128)(2,1)}, u32[]{:S(2)}, u32[]{:S(2)}) %collective-permute-start.4) | collective-permute-done | bytes 1048608 | tf_op jit(solution)/shard_map/ppermute | solution.py:19
  157.6 1.9 reduce-scatter.6.cloned.1.call-done
  159.5 51.9 %reduce-scatter.4.cloned.1.call-done = f32[1,1024,256]{2,1,0:T(8,128)} async-done(((f32[4,1024,256]{2,1,0:T(8,128)}), f32[1,1024,256]{2,1,0:T(8,128)}) %reduce-scatter.4.cloned.1.call-update) | async-done | bytes 1048592 | tf_op jit(solution)/shard_map/reduce_scatter | solution.py:35
  211.4 3.1 pad_maximum_fusion
  214.5 2.6 convolution_multiply_fusion
  217.1 0.6 copy.115
  217.7 69.9 %all_to_all.15 = f32[4,4,4,8,8,256]{5,3,2,1,4,0:T(8,128)} all-to-all(f32[4,4,4,8,8,256]{5,3,2,1,4,0:T(8,128)S(1)} %copy.115), channel_id=1, replica_groups=mesh['dy'=4,'dz'=4,'dx'=4,'tensor'=4] {'dy'}, dimensions={0} | all-to-all | bytes 8388608 | tf_op jit(solution)/shard_map/all_to_all | solution.py:40
  287.6 3.7 %reduce_sum.47 = f32[4,4,8,8,256]{4,2,1,0,3:T(8,128)} reduce(f32[4,4,4,8,8,256]{5,3,2,1,4,0:T(8,128)} %all_to_all.15, f32[]{:T(128)} %constant.7.clone.1), dimensions={0}, to_apply=%region_5.6 | reduce | flops 786432 | bytes 5242884 | tf_op jit(solution)/shard_map/reduce_sum | solution.py:40
  291.3 2.8 copy.117
  294.1 6.0 %all-to-all-start.1 = ((f32[4,4,8,8,256]{4,3,2,1,0:T(8,128)}), f32[4,4,8,8,256]{4,3,2,1,0:T(8,128)}, u32[]{:S(2)}, u32[]{:S(2)}) async-start(f32[4,4,8,8,256]{4,3,2,1,0:T(8,128)} %copy.117), calls=%async_computation.4 | async-start | bytes 2097152 | tf_op jit(solution)/shard_map/all_to_all | solution.py:40
  300.1 2.3 copy.105
  302.3 0.3 fusion.3
  302.8 0.8 copy-done.8
  303.6 3.0 fusion.39
  306.6 5.7 %collective-permute-start.8 = (f32[256]{0:T(256)S(1)}, f32[256]{0:T(256)S(1)}, u32[]{:S(2)}, u32[]{:S(2)}) collective-permute-start(f32[256]{0:T(256)S(1)} %add.101), channel_id=1, source_target_pairs={{0,2},{1,3},{2,0},{3,1},{4,6},{5,7},{6,4},{7,5},{8,10},{9,11},{10,... | collective-permute-start | bytes 3080 | tf_op jit(solution)/shard_map/ppermute | solution.py:19
  312.3 0.7 all-to-all-done.1
  313.0 1.3 reduce_sum.48
  314.3 2.0 maximum_bitcast_fusion
  316.3 4.8 %all-to-all-start.2 = ((f32[4,3,8,8,256]{4,3,2,1,0:T(8,128)}), f32[4,3,8,8,256]{4,3,2,1,0:T(8,128)}, u32[]{:S(2)}, u32[]{:S(2)}) async-start(f32[4,3,8,8,256]{4,3,2,1,0:T(8,128)} %maximum_bitcast_fusion), calls=%async_computation.5 | async-start | bytes 1572864 | tf_op jit(solution)/shard_map/all_to_all | solution.py:40
  321.1 2.8 convolution_add_fusion
  323.9 1.9 fusion.7
  325.8 2.4 copy.119
  328.2 1.4 copy.120
  329.6 10.3 %all-to-all-done.2 = f32[4,3,8,8,256]{4,3,2,1,0:T(8,128)} async-done(((f32[4,3,8,8,256]{4,3,2,1,0:T(8,128)}), f32[4,3,8,8,256]{4,3,2,1,0:T(8,128)}, u32[]{:S(2)}, u32[]{:S(2)}) %all-to-all-start.2) | async-done | bytes 786464 | tf_op jit(solution)/shard_map/all_to_all | solution.py:40
  339.9 1.9 reduce_sum.49
  (50 shorter events, 1.3 us)
Async XLA Ops:
  7.2 75.9 %all-gather.2.cloned.1.call-start = ((), (), s32[]{:S(2)}) async-start(), calls=%async_computation.6 | async-start | bytes 1114112 | tf_op jit(solution)/shard_map/all_gather | solution.py:67
  9.0 7.0 %collective-permute-start = (f32[256]{0:T(256)S(1)}, f32[256]{0:T(256)S(1)}, u32[]{:S(2)}, u32[]{:S(2)}) collective-permute-start(f32[256]{0:T(256)S(1)} %fusion.8), channel_id=1, source_target_pairs={{0,1},{1,0},{2,3},{3,2},{4,5},{5,4},{6,7},{7,6},{8,9},{9,8},{10,11... | collective-permute-start | bytes 3080 | tf_op jit(solution)/shard_map/ppermute | solution.py:19
  16.0 13.6 %copy-start.7 = (bf16[1,256,8,256]{1,3,2,0:T(8,128)(2,1)}, bf16[1,256,8,256]{1,3,2,0:T(8,128)(2,1)S(1)}, u32[]{:S(2)}) copy-start(bf16[1,256,8,256]{1,3,2,0:T(8,128)(2,1)S(1)} %copy.144) | copy-start | bytes 3145732
  16.0 13.6 %collective-permute-start.1 = (f32[256]{0:T(256)S(1)}, f32[256]{0:T(256)S(1)}, u32[]{:S(2)}, u32[]{:S(2)}) collective-permute-start(f32[256]{0:T(256)S(1)} %add.80), channel_id=1, source_target_pairs={{0,2},{1,3},{2,0},{3,1},{4,6},{5,7},{6,4},{7,5},{8,10},{9,11},{10,... | collective-permute-start | bytes 3080 | tf_op jit(solution)/shard_map/ppermute | solution.py:19
  25.5 8.9 %collective-permute-start.5 = (bf16[16,8,256]{2,0,1:T(8,128)(2,1)S(1)}, bf16[16,8,256]{2,0,1:T(8,128)(2,1)S(1)}, u32[]{:S(2)}, u32[]{:S(2)}) collective-permute-start(bf16[16,8,256]{2,0,1:T(8,128)(2,1)S(1)} %bitcast.155), channel_id=1, source_target_pairs={{0,2},{1,3},{2,0},{3,1},{4,6},{5,7},{6,4},{7,5},{8,10},{9,11},{10,... | collective-permute-start | bytes 196616 | tf_op jit(solution)/shard_map/ppermute | solution.py:19
  32.4 4.5 %copy-start.3 = (bf16[256,1,2,4,256]{4,0,3,2,1:T(8,128)(2,1)}, bf16[256,1,2,4,256]{4,0,3,2,1:T(8,128)(2,1)S(1)}, u32[]{:S(2)}) copy-start(bf16[256,1,2,4,256]{4,0,3,2,1:T(8,128)(2,1)S(1)} %rev.8) | copy-start | bytes 3145732
  34.4 0.6 copy-start.13
  35.1 124.4 %reduce-scatter.6.cloned.1.call-start = ((), (), s32[]{:S(2)}) async-start(), calls=%async_computation.8 | async-start | bytes 5242880 | tf_op jit(solution)/shard_map/reduce_scatter | solution.py:35
  35.1 1.8 copy-start.2
  36.9 2.3 copy-start
  39.3 12.4 %collective-permute-start.2 = (bf16[256,8,256]{0,2,1:T(8,128)(2,1)}, bf16[256,8,256]{0,2,1:T(8,128)(2,1)}, u32[]{:S(2)}, u32[]{:S(2)}) collective-permute-start(bf16[256,8,256]{0,2,1:T(8,128)(2,1)} %get-tuple-element.23), channel_id=1, source_target_pairs={{0,1},{1,0},{2,3},{3,2},{4,5},{5,4},{6,7},{7,6},{8,9},{9,8},{10,11... | collective-permute-start | bytes 3145736 | tf_op jit(solution)/shard_map/ppermute | solution.py:19
  40.3 37.8 %collective-permute-start.3 = (bf16[256,8,256]{2,0,1:T(8,128)(2,1)}, bf16[256,8,256]{2,0,1:T(8,128)(2,1)}, u32[]{:S(2)}, u32[]{:S(2)}) collective-permute-start(bf16[256,8,256]{2,0,1:T(8,128)(2,1)} %bitcast.134), channel_id=1, source_target_pairs={{0,2},{1,3},{2,0},{3,1},{4,6},{5,7},{6,4},{7,5},{8,10},{9,11},{10,... | collective-permute-start | bytes 3145736 | tf_op jit(solution)/shard_map/ppermute | solution.py:19
  46.7 3.1 copy-start.11
  49.8 1.8 copy-start.1
  87.0 1.0 copy-start.12
  102.4 109.0 %reduce-scatter.4.cloned.1.call-start = ((), (), s32[]{:S(2)}) async-start(), calls=%async_computation.7 | async-start | bytes 5242880 | tf_op jit(solution)/shard_map/reduce_scatter | solution.py:35
  105.6 4.5 %collective-permute-start.6 = (f32[256,8,256]{0,2,1:T(8,128)}, f32[256,8,256]{0,2,1:T(8,128)}, u32[]{:S(2)}, u32[]{:S(2)}) collective-permute-start(f32[256,8,256]{0,2,1:T(8,128)} %convolution_bitcast_fusion), channel_id=1, source_target_pairs={{0,1},{1,0},{2,3},{3,2},{4,5},{5,4},{6,7},{7,6},{8,9},{9,8},{10,11... | collective-permute-start | bytes 6291464 | tf_op jit(solution)/shard_map/ppermute | solution.py:19
  110.1 4.1 %copy-start.4 = (bf16[256,1,2,4,256]{4,0,3,2,1:T(8,128)(2,1)S(1)}, bf16[256,1,2,4,256]{4,0,3,2,1:T(8,128)(2,1)}, u32[]{:S(2)}) copy-start(bf16[256,1,2,4,256]{4,0,3,2,1:T(8,128)(2,1)} %copy-done.3) | copy-start | bytes 3145732
  114.3 19.2 %copy-start.5 = (bf16[256,8,256]{0,2,1:T(8,128)(2,1)}, bf16[256,8,256]{0,2,1:T(8,128)(2,1)S(1)}, u32[]{:S(2)}) copy-start(bf16[256,8,256]{0,2,1:T(8,128)(2,1)S(1)} %fusion.21) | copy-start | bytes 3145732
  127.6 5.9 %copy-start.6 = (bf16[1,256,8,256]{1,3,2,0:T(8,128)(2,1)S(1)}, bf16[1,256,8,256]{1,3,2,0:T(8,128)(2,1)}, u32[]{:S(2)}) copy-start(bf16[1,256,8,256]{1,3,2,0:T(8,128)(2,1)} %copy.140) | copy-start | bytes 3145732
  127.6 186.7 %reduce-scatter.8.cloned.1.call-start = ((), (), s32[]{:S(2)}) async-start(), calls=%async_computation.9 | async-start | bytes 2621440 | tf_op jit(solution)/shard_map/reduce_scatter | solution.py:56
  127.7 30.0 %collective-permute-start.4 = (bf16[256,8,256]{0,2,1:T(8,128)(2,1)}, bf16[256,8,256]{0,2,1:T(8,128)(2,1)}, u32[]{:S(2)}, u32[]{:S(2)}) collective-permute-start(bf16[256,8,256]{0,2,1:T(8,128)(2,1)} %get-tuple-element.6), channel_id=1, source_target_pairs={{0,2},{1,3},{2,0},{3,1},{4,6},{5,7},{6,4},{7,5},{8,10},{9,11},{10,... | collective-permute-start | bytes 3145736 | tf_op jit(solution)/shard_map/ppermute | solution.py:19
  294.1 18.9 %all-to-all-start.1 = ((f32[4,4,8,8,256]{4,3,2,1,0:T(8,128)}), f32[4,4,8,8,256]{4,3,2,1,0:T(8,128)}, u32[]{:S(2)}, u32[]{:S(2)}) async-start(f32[4,4,8,8,256]{4,3,2,1,0:T(8,128)} %copy.117), calls=%async_computation.4 | async-start | bytes 2097152 | tf_op jit(solution)/shard_map/all_to_all | solution.py:40
  302.3 1.2 copy-start.8
  302.7 3.9 %collective-permute-start.7 = (f32[256]{0:T(256)S(1)}, f32[256]{0:T(256)S(1)}, u32[]{:S(2)}, u32[]{:S(2)}) collective-permute-start(f32[256]{0:T(256)S(1)} %fusion.3), channel_id=1, source_target_pairs={{0,1},{1,0},{2,3},{3,2},{4,5},{5,4},{6,7},{7,6},{8,9},{9,8},{10,11... | collective-permute-start | bytes 3080 | tf_op jit(solution)/shard_map/ppermute | solution.py:19
  306.6 17.3 %collective-permute-start.8 = (f32[256]{0:T(256)S(1)}, f32[256]{0:T(256)S(1)}, u32[]{:S(2)}, u32[]{:S(2)}) collective-permute-start(f32[256]{0:T(256)S(1)} %add.101), channel_id=1, source_target_pairs={{0,2},{1,3},{2,0},{3,1},{4,6},{5,7},{6,4},{7,5},{8,10},{9,11},{10,... | collective-permute-start | bytes 3080 | tf_op jit(solution)/shard_map/ppermute | solution.py:19
  316.3 23.6 %all-to-all-start.2 = ((f32[4,3,8,8,256]{4,3,2,1,0:T(8,128)}), f32[4,3,8,8,256]{4,3,2,1,0:T(8,128)}, u32[]{:S(2)}, u32[]{:S(2)}) async-start(f32[4,3,8,8,256]{4,3,2,1,0:T(8,128)} %maximum_bitcast_fusion), calls=%async_computation.5 | async-start | bytes 1572864 | tf_op jit(solution)/shard_map/all_to_all | solution.py:40
  321.1 2.8 copy-start.9
  325.8 2.4 copy-start.10
Sparse Core Ops, SparseCore 0:
  35.2 47.7 all-gather.1
  102.5 56.9 reduce-scatter.5
  162.2 49.1 reduce-scatter.3
  214.6 67.0 reduce-scatter.7

commit v5 on v3

--- a/solution.py
+++ b/solution.py
@@ -30,19 +30,17 @@
     ny, nz, nx = (lax.axis_size(a) for a in ("dy", "dz", "dx"))
     rest = grads.shape[1:]
     share = rows // (ny * nz * nx)
-    g = grads.reshape((ny, nz, nx, share) + rest)
-    g = jnp.moveaxis(g, 2, 0).reshape(nx, -1, rest[-1])
-    g = lax.psum_scatter(g, "dx", scatter_dimension=0, tiled=True)
-    return g.reshape((ny, nz, share) + rest)
+    g = lax.psum_scatter(grads.reshape(ny, -1, rest[-1]), "dy", scatter_dimension=0, tiled=True)
+    return g.reshape((nz, nx, share) + rest)
 
 
 def scatter_rest(parts):
-    ny, nz, share = parts[0].shape[:3]
+    nz, nx, share = parts[0].shape[:3]
     rest = parts[0].shape[3:]
-    g = jnp.stack(parts, axis=2)
-    for axis, size in (("dy", ny), ("dz", nz)):
-        g = g.reshape(size, -1, rest[-1])
-        g = lax.psum_scatter(g, axis, scatter_dimension=0, tiled=True)
+    g = jnp.moveaxis(jnp.stack(parts, axis=0), 2, 0)
+    g = lax.psum_scatter(g.reshape(nx, -1, rest[-1]), "dx", scatter_dimension=0, tiled=True)
+    g = jnp.moveaxis(g.reshape((len(parts), nz, share) + rest), 1, 0)
+    g = lax.psum_scatter(g.reshape(nz, -1, rest[-1]), "dz", scatter_dimension=0, tiled=True)
     return g.reshape((len(parts), share) + rest)
 
 

time: 348 us -> 344 us (0.989)
  local copies, waits for them, and re-layouts: 60.3 us -> 54.8 us
    transpose x2 -> x1, local copies, waits for them, and re-layouts: 9.44 us -> 2.07 us  [scatter_rest(): g = jnp.moveaxis(g.reshape((len(parts), nz, share) + rest), 1, 0)]
    mul x0 -> x1, local copies, waits for them, and re-layouts: none -> 4.46 us  [shards(): jnp.einsum('tbc,tbd->cbd', joined, cot_blocks, preferred_element_type=jnp...]
    reshape x1 -> x0, local copies, waits for them, and re-layouts: 4.46 us -> none  [scatter_first(): g = grads.reshape((ny, nz, nx, share) + rest)]
  transfers between devices with their start and end apart: 15 -> 15, of which waited for: 8 -> 9; matrix products, arithmetic and copies ran while one was open for 22% -> 22% of each run, Pallas kernels for 0% -> 0%
where the time goes in v5:
time: 344 us; the launch traced here: 343 us
  waiting for transfers between devices  208 us (60%)
  local copies, waits for them, and re-layouts  54.8 us (16%)
  matrix products  36.7 us (11%)
  starting transfers between devices  23.7 us (7%)
  between operations  14.5 us (4%)
  other arithmetic  5 us (1%)
    reduce_scatter x3, waiting for transfers between devices, scatter_first(): lax.psum_scatter(grads.reshape(ny, -1, rest[-1]), 'dy', scatter_dimension...  89.2 us
    ppermute x9, waiting for transfers between devices, swapped(): lax.ppermute(x, axis, [(i, i ^ 1 << stride) for i in range(lax.axis_size(...  62 us
    reduce_scatter x1, waiting for transfers between devices, scatter_rest(): lax.psum_scatter(g.reshape(nx, -1, rest[-1]), 'dx', scatter_dimension=0,...  36.7 us
    ppermute x9, starting transfers between devices, swapped(): lax.ppermute(x, axis, [(i, i ^ 1 << stride) for i in range(lax.axis_size(...  23.5 us
    unnamed x46, local copies, waits for them, and re-layouts  17.1 us
    reduce_scatter x1, waiting for transfers between devices, scatter_rest(): lax.psum_scatter(g.reshape(nz, -1, rest[-1]), 'dz', scatter_dimension=0,...  15.3 us
    mul x2, local copies, waits for them, and re-layouts, shards(): jnp.einsum('tbc,tbd->cbd', joined, grad_pre, preferred_element_type=jnp.f...  10.9 us
    dot_general x2, matrix products, shards(): jnp.einsum('tbc,tbd->cbd', joined, grad_pre, preferred_element_type=jnp.f...  8.82 us
  transfers between devices with their start and end apart: 15, of which 9 were waited for; matrix products, arithmetic and copies ran while one was open for 22% of the time, Pallas kernels for 0%

profile of v5, /device:TPU:2, one launch (start us, length us, event | category | flops | bytes accessed | tf_op | source)
XLA Modules:
  0.0 343.2 jit_solution(15135319612141088759)
XLA Ops:
  7.2 1.5 copy.77
  8.7 0.3 fusion.8
  9.0 0.1 collective-permute-start
  9.1 5.2 %fusion.54 = (bf16[1,256,8,256]{3,2,1,0:T(8,128)(2,1)}, bf16[1,256,8,256]{3,2,1,0:T(8,128)(2,1)}, bf16[1,256,8,256]{3,2,1,0:T(8,128)(2,1)}, bf16[1,256,8,256]{3,...) fusion(bf16[3,512,8,256]{3,2,1,0:T(8,128)(2,1)} %param.4), kind=kLoop, calls=%fused_computation.79 | loop fusion | bytes 12582912 | tf_op jit(solution)/shard_map/slice | solution.py:77
  14.3 1.6 copy.141
  16.0 7.3 %collective-permute-start.1 = (f32[256]{0:T(256)S(1)}, f32[256]{0:T(256)S(1)}, u32[]{:S(2)}, u32[]{:S(2)}) collective-permute-start(f32[256]{0:T(256)S(1)} %add.84), channel_id=1, source_target_pairs={{0,2},{1,3},{2,0},{3,1},{4,6},{5,7},{6,4},{7,5},{8,10},{9,11},{10,... | collective-permute-start | bytes 3080 | tf_op jit(solution)/shard_map/ppermute | solution.py:19
  23.3 1.0 constant_dynamic-slice_fusion
  24.3 1.2 copy.94
  25.5 0.1 collective-permute-start.5
  25.6 2.4 copy.138
  28.0 1.6 copy.137
  29.6 0.2 fusion.2
  29.8 1.3 copy.80
  31.1 1.3 rev.8
  32.4 1.9 collective-permute-done.5
  34.4 0.6 copy-done.18
  35.1 1.8 fusion.46
  36.9 2.3 fusion.38
  39.2 1.0 copy.154
  40.3 4.0 %collective-permute-start.3 = (bf16[256,8,256]{2,0,1:T(8,128)(2,1)}, bf16[256,8,256]{2,0,1:T(8,128)(2,1)}, u32[]{:S(2)}, u32[]{:S(2)}) collective-permute-start(bf16[256,8,256]{2,0,1:T(8,128)(2,1)} %bitcast.127), channel_id=1, source_target_pairs={{0,2},{1,3},{2,0},{3,1},{4,6},{5,7},{6,4},{7,5},{8,10},{9,11},{10,... | collective-permute-start | bytes 3145736 | tf_op jit(solution)/shard_map/ppermute | solution.py:19
  44.3 1.6 copy.136
  46.0 1.8 fusion.41
  47.8 0.2 copy-done.13
  48.0 1.8 fusion.50
  49.8 3.7 %fusion.34 = (bf16[256,8,256]{0,2,1:T(8,128)(2,1)}, f32[8,256,256]{1,2,0:T(8,128)}) fusion(f32[8,256,256]{1,2,0:T(8,128)S(1)} %fusion.50, bf16[256,8,256]{0,2,1:T(8,128)(2,1)} %collective-permute-done.2, bf16[1,256,8,256]{3,2,1,0:T(8,128)(2,1)S(1)} %copy-done.3), kind=kOutput, calls=%fused_computation.47 | convolution fusion | flops 271581184 | bytes 7340032 | tf_op jit(solution)/shard_map/tbc,cbd->tbd/dot_general | solution.py:76
  53.5 24.4 %collective-permute-done.3 = bf16[256,8,256]{2,0,1:T(8,128)(2,1)} collective-permute-done((bf16[256,8,256]{2,0,1:T(8,128)(2,1)}, bf16[256,8,256]{2,0,1:T(8,128)(2,1)}, u32[]{:S(2)}, u32[]{:S(2)}) %collective-permute-start.3) | collective-permute-done | bytes 1048608 | tf_op jit(solution)/shard_map/ppermute | solution.py:19
  77.9 5.2 %all-gather.2.cloned.1.call-done = bf16[256,8,256]{2,0,1:T(8,128)(2,1)} async-done(((bf16[16,8,256]{2,0,1:T(8,128)(2,1)}), bf16[256,8,256]{2,0,1:T(8,128)(2,1)}) %all-gather.2.cloned.1.call-update) | async-done | bytes 1048592 | tf_op jit(solution)/shard_map/all_gather | solution.py:53
  83.0 4.0 %fusion.15 = bf16[256,8,256]{0,2,1:T(8,128)(2,1)S(1)} fusion(f32[8,256,256]{1,2,0:T(8,128)} %get-tuple-element.26, f32[8,256,256]{2,1,0:T(8,128)} %fusion.41, bf16[256,8,256]{2,0,1:T(8,128)(2,1)} %all-gather.2.cloned.1.call-done, bf16[256,8,256]{2,0,1:T(8,128)(2,1)} %collective-permute-done.3), kind=kOutput, calls=%fused_computation.24 | convolution fusion | flops 274202624 | bytes 7340032 | tf_op jit(solution)/shard_map/tbd,cbd->tbc/dot_general | solution.py:115
  87.0 1.0 copy-done.15
  88.0 4.3 %multiply_bitcast_fusion.1 = f32[512,8,256]{0,2,1:T(8,128)} fusion(bf16[256,8,256]{0,2,1:T(8,128)(2,1)S(1)} %fusion.15, bf16[256,8,256]{0,2,1:T(8,128)(2,1)} %collective-permute-done.2, bf16[256,8,256]{0,2,1:T(8,128)(2,1)} %get-tuple-element.23), kind=kOutput, calls=%fused_computation.1 | convolution fusion | flops 542113792 | bytes 7340032 | tf_op jit(solution)/shard_map/tbc,tbd->cbd/dot_general | solution.py:129
  92.3 5.4 %copy.109 = f32[512,8,256]{2,1,0:T(8,128)} copy(f32[512,8,256]{0,2,1:T(8,128)} %multiply_bitcast_fusion.1) | data formatting | bytes 8388608 | tf_op jit(solution)/shard_map/mul | solution.py:129
  97.8 1.8 convolution_bitcast_fusion
  99.6 0.3 collective-permute-start.6
  99.9 5.8 %collective-permute-start.4 = (bf16[256,8,256]{0,2,1:T(8,128)(2,1)}, bf16[256,8,256]{0,2,1:T(8,128)(2,1)}, u32[]{:S(2)}, u32[]{:S(2)}) collective-permute-start(bf16[256,8,256]{0,2,1:T(8,128)(2,1)} %get-tuple-element.6), channel_id=1, source_target_pairs={{0,2},{1,3},{2,0},{3,1},{4,6},{5,7},{6,4},{7,5},{8,10},{9,11},{10,... | collective-permute-start | bytes 3145736 | tf_op jit(solution)/shard_map/ppermute | solution.py:19
  105.8 1.4 fusion.21
  107.2 0.5 fusion.44
  107.7 0.5 copy-done.6
  108.1 1.9 copy.103
  110.0 3.1 rev.9
  113.1 2.8 bitcast_add_fusion
  115.9 35.6 %collective-permute-done.4 = bf16[256,8,256]{0,2,1:T(8,128)(2,1)} collective-permute-done((bf16[256,8,256]{0,2,1:T(8,128)(2,1)}, bf16[256,8,256]{0,2,1:T(8,128)(2,1)}, u32[]{:S(2)}, u32[]{:S(2)}) %collective-permute-start.4) | collective-permute-done | bytes 1048608 | tf_op jit(solution)/shard_map/ppermute | solution.py:19
  151.6 2.3 multiply_bitcast_fusion
  153.8 4.5 %copy.111 = f32[512,8,256]{2,1,0:T(8,128)} copy(f32[512,8,256]{2,0,1:T(8,128)S(1)} %multiply_bitcast_fusion) | data formatting | bytes 8388608 | tf_op jit(solution)/shard_map/mul | solution.py:152
  158.3 0.0 reduce-scatter.6.cloned.1.call-start
  158.4 2.3 copy.106
  160.6 4.5 %multiply_bitcast_fusion.2 = f32[512,8,256]{0,2,1:T(8,128)} fusion(bf16[256,8,256]{0,2,1:T(8,128)(2,1)} %copy-done.6, bf16[256,8,256]{2,0,1:T(8,128)(2,1)} %bitcast.139, bf16[256,8,256]{2,0,1:T(8,128)(2,1)} %copy.106), kind=kOutput, calls=%fused_computation.2 | convolution fusion | flops 542113792 | bytes 7340032 | tf_op jit(solution)/shard_map/tbc,tbd->cbd/dot_general | solution.py:129
  165.1 5.5 %copy.107 = f32[512,8,256]{2,1,0:T(8,128)} copy(f32[512,8,256]{0,2,1:T(8,128)} %multiply_bitcast_fusion.2) | data formatting | bytes 8388608 | tf_op jit(solution)/shard_map/mul | solution.py:129
  170.7 37.6 %reduce-scatter.10.cloned.1.call-done = f32[1,1024,256]{2,1,0:T(8,128)} async-done(((f32[4,1024,256]{2,1,0:T(8,128)}), f32[1,1024,256]{2,1,0:T(8,128)}) %reduce-scatter.10.cloned.1.call-update) | async-done | bytes 1048592 | tf_op jit(solution)/shard_map/reduce_scatter | solution.py:33
  208.3 51.6 %reduce-scatter.6.cloned.1.call-done = f32[1,1024,256]{2,1,0:T(8,128)} async-done(((f32[4,1024,256]{2,1,0:T(8,128)}), f32[1,1024,256]{2,1,0:T(8,128)}) %reduce-scatter.6.cloned.1.call-update) | async-done | bytes 1048592 | tf_op jit(solution)/shard_map/reduce_scatter | solution.py:33
  259.9 2.2 pad_maximum_fusion
  262.1 2.0 copy.135
  264.2 2.3 copy.105
  266.4 0.3 fusion.3
  266.8 0.1 collective-permute-start.7
  266.9 36.7 %reduce-scatter.12.cloned.1.call-done = f32[1,768,256]{2,1,0:T(8,128)} async-done(((f32[4,768,256]{2,1,0:T(8,128)}), f32[1,768,256]{2,1,0:T(8,128)}) %reduce-scatter.12.cloned.1.call-update) | async-done | bytes 786448 | tf_op jit(solution)/shard_map/reduce_scatter | solution.py:41
  303.6 2.1 copy.115
  305.7 2.1 fusion.39
  307.8 5.8 %collective-permute-start.8 = (f32[256]{0:T(256)S(1)}, f32[256]{0:T(256)S(1)}, u32[]{:S(2)}, u32[]{:S(2)}) collective-permute-start(f32[256]{0:T(256)S(1)} %add.105), channel_id=1, source_target_pairs={{0,2},{1,3},{2,0},{3,1},{4,6},{5,7},{6,4},{7,5},{8,10},{9,11},{10,... | collective-permute-start | bytes 3080 | tf_op jit(solution)/shard_map/ppermute | solution.py:19
  313.6 1.7 convolution_add_fusion
  315.3 0.1 collective-permute-done.8
  315.4 1.9 fusion.7
  317.3 2.4 copy.116
  319.6 1.4 copy.117
  321.0 15.3 %reduce-scatter.14.cloned.1.call-done = f32[1,192,256]{2,1,0:T(8,128)} async-done(((f32[4,192,256]{2,1,0:T(8,128)}), f32[1,192,256]{2,1,0:T(8,128)}) %reduce-scatter.14.cloned.1.call-update) | async-done | bytes 196624 | tf_op jit(solution)/shard_map/reduce_scatter | solution.py:43
  (56 shorter events, 0.4 us)
Async XLA Ops:
  7.2 75.9 %all-gather.2.cloned.1.call-start = ((), (), s32[]{:S(2)}) async-start(), calls=%async_computation.5 | async-start | bytes 1114112 | tf_op jit(solution)/shard_map/all_gather | solution.py:53
  9.0 7.0 %collective-permute-start = (f32[256]{0:T(256)S(1)}, f32[256]{0:T(256)S(1)}, u32[]{:S(2)}, u32[]{:S(2)}) collective-permute-start(f32[256]{0:T(256)S(1)} %fusion.8), channel_id=1, source_target_pairs={{0,1},{1,0},{2,3},{3,2},{4,5},{5,4},{6,7},{7,6},{8,9},{9,8},{10,11... | collective-permute-start | bytes 3080 | tf_op jit(solution)/shard_map/ppermute | solution.py:19
  16.0 13.6 %copy-start.10 = (bf16[1,256,8,256]{1,3,2,0:T(8,128)(2,1)}, bf16[1,256,8,256]{1,3,2,0:T(8,128)(2,1)S(1)}, u32[]{:S(2)}) copy-start(bf16[1,256,8,256]{1,3,2,0:T(8,128)(2,1)S(1)} %copy.141) | copy-start | bytes 3145732
  16.0 13.6 %collective-permute-start.1 = (f32[256]{0:T(256)S(1)}, f32[256]{0:T(256)S(1)}, u32[]{:S(2)}, u32[]{:S(2)}) collective-permute-start(f32[256]{0:T(256)S(1)} %add.84), channel_id=1, source_target_pairs={{0,2},{1,3},{2,0},{3,1},{4,6},{5,7},{6,4},{7,5},{8,10},{9,11},{10,... | collective-permute-start | bytes 3080 | tf_op jit(solution)/shard_map/ppermute | solution.py:19
  25.5 8.9 %collective-permute-start.5 = (bf16[16,8,256]{2,0,1:T(8,128)(2,1)S(1)}, bf16[16,8,256]{2,0,1:T(8,128)(2,1)S(1)}, u32[]{:S(2)}, u32[]{:S(2)}) collective-permute-start(bf16[16,8,256]{2,0,1:T(8,128)(2,1)S(1)} %bitcast.146), channel_id=1, source_target_pairs={{0,2},{1,3},{2,0},{3,1},{4,6},{5,7},{6,4},{7,5},{8,10},{9,11},{10,... | collective-permute-start | bytes 196616 | tf_op jit(solution)/shard_map/ppermute | solution.py:19
  29.8 7.1 %copy-start = (bf16[256,2048]{0,1:T(8,128)(2,1)}, bf16[256,2048]{0,1:T(8,128)(2,1)S(1)}, u32[]{:S(2)}) copy-start(bf16[256,2048]{0,1:T(8,128)(2,1)S(1)} %fusion.2) | copy-start | bytes 3145732
  32.4 4.4 %copy-start.4 = (bf16[256,1,2,4,256]{4,0,3,2,1:T(8,128)(2,1)}, bf16[256,1,2,4,256]{4,0,3,2,1:T(8,128)(2,1)S(1)}, u32[]{:S(2)}) copy-start(bf16[256,1,2,4,256]{4,0,3,2,1:T(8,128)(2,1)S(1)} %rev.8) | copy-start | bytes 3145732
  34.4 0.6 copy-start.18
  35.0 135.7 %reduce-scatter.8.cloned.1.call-start = ((), (), s32[]{:S(2)}) async-start(), calls=%async_computation.7 | async-start | bytes 5242880 | tf_op jit(solution)/shard_map/reduce_scatter | solution.py:33
  35.1 1.8 copy-start.5
  36.9 2.3 copy-start.1
  39.2 10.6 %collective-permute-start.2 = (bf16[256,8,256]{0,2,1:T(8,128)(2,1)}, bf16[256,8,256]{0,2,1:T(8,128)(2,1)}, u32[]{:S(2)}, u32[]{:S(2)}) collective-permute-start(bf16[256,8,256]{0,2,1:T(8,128)(2,1)} %get-tuple-element.23), channel_id=1, source_target_pairs={{0,1},{1,0},{2,3},{3,2},{4,5},{5,4},{6,7},{7,6},{8,9},{9,8},{10,11... | collective-permute-start | bytes 3145736 | tf_op jit(solution)/shard_map/ppermute | solution.py:19
  40.3 37.6 %collective-permute-start.3 = (bf16[256,8,256]{2,0,1:T(8,128)(2,1)}, bf16[256,8,256]{2,0,1:T(8,128)(2,1)}, u32[]{:S(2)}, u32[]{:S(2)}) collective-permute-start(bf16[256,8,256]{2,0,1:T(8,128)(2,1)} %bitcast.127), channel_id=1, source_target_pairs={{0,2},{1,3},{2,0},{3,1},{4,6},{5,7},{6,4},{7,5},{8,10},{9,11},{10,... | collective-permute-start | bytes 3145736 | tf_op jit(solution)/shard_map/ppermute | solution.py:19
  45.9 1.9 copy-start.7
  45.9 2.0 copy-start.13
  48.0 1.8 copy-start.3
  87.0 1.0 copy-start.15
  97.7 8.0 %copy-start.14 = (bf16[1,256,8,256]{3,2,1,0:T(8,128)(2,1)S(1)}, bf16[1,256,8,256]{3,2,1,0:T(8,128)(2,1)}, u32[]{:S(2)}) copy-start(bf16[1,256,8,256]{3,2,1,0:T(8,128)(2,1)} %get-tuple-element.16) | copy-start | bytes 3145732
  97.8 110.6 %reduce-scatter.10.cloned.1.call-start = ((), (), s32[]{:S(2)}) async-start(), calls=%async_computation.8 | async-start | bytes 5242880 | tf_op jit(solution)/shard_map/reduce_scatter | solution.py:33
  97.8 7.9 %copy-start.16 = (bf16[256,8,256]{0,2,1:T(8,128)(2,1)S(1)}, bf16[256,8,256]{0,2,1:T(8,128)(2,1)}, u32[]{:S(2)}) copy-start(bf16[256,8,256]{0,2,1:T(8,128)(2,1)} %copy-done.15) | copy-start | bytes 3145732
  97.8 7.9 %copy-start.17 = (f32[8,256,256]{1,2,0:T(8,128)S(1)}, f32[8,256,256]{1,2,0:T(8,128)}, u32[]{:S(2)}) copy-start(f32[8,256,256]{1,2,0:T(8,128)} %get-tuple-element.24) | copy-start | bytes 6291460
  99.6 6.1 %collective-permute-start.6 = (f32[256,8,256]{0,2,1:T(8,128)S(1)}, f32[256,8,256]{0,2,1:T(8,128)S(1)}, u32[]{:S(2)}, u32[]{:S(2)}) collective-permute-start(f32[256,8,256]{0,2,1:T(8,128)S(1)} %convolution_bitcast_fusion), channel_id=1, source_target_pairs={{0,1},{1,0},{2,3},{3,2},{4,5},{5,4},{6,7},{7,6},{8,9},{9,8},{10,11... | collective-permute-start | bytes 6291464 | tf_op jit(solution)/shard_map/ppermute | solution.py:19
  99.9 51.6 %collective-permute-start.4 = (bf16[256,8,256]{0,2,1:T(8,128)(2,1)}, bf16[256,8,256]{0,2,1:T(8,128)(2,1)}, u32[]{:S(2)}, u32[]{:S(2)}) collective-permute-start(bf16[256,8,256]{0,2,1:T(8,128)(2,1)} %get-tuple-element.6), channel_id=1, source_target_pairs={{0,2},{1,3},{2,0},{3,1},{4,6},{5,7},{6,4},{7,5},{8,10},{9,11},{10,... | collective-permute-start | bytes 3145736 | tf_op jit(solution)/shard_map/ppermute | solution.py:19
  105.8 1.4 copy-start.9
  107.2 1.0 copy-start.6
  113.1 38.4 %copy-start.2 = (bf16[256,2048]{1,0:T(8,128)(2,1)S(1)}, bf16[256,2048]{1,0:T(8,128)(2,1)}, u32[]{:S(2)}) copy-start(bf16[256,2048]{1,0:T(8,128)(2,1)} %param.5) | copy-start | bytes 3145732
  158.3 101.6 %reduce-scatter.6.cloned.1.call-start = ((), (), s32[]{:S(2)}) async-start(), calls=%async_computation.6 | async-start | bytes 5242880 | tf_op jit(solution)/shard_map/reduce_scatter | solution.py:33
  170.6 133.0 %reduce-scatter.12.cloned.1.call-start = ((), (), s32[]{:S(2)}) async-start(), calls=%async_computation.9 | async-start | bytes 3932160 | tf_op jit(solution)/shard_map/reduce_scatter | solution.py:41
  264.1 72.2 %reduce-scatter.14.cloned.1.call-start = ((), (), s32[]{:S(2)}) async-start(), calls=%async_computation.10 | async-start | bytes 983040 | tf_op jit(solution)/shard_map/reduce_scatter | solution.py:43
  266.8 41.0 %collective-permute-start.7 = (f32[256]{0:T(256)S(1)}, f32[256]{0:T(256)S(1)}, u32[]{:S(2)}, u32[]{:S(2)}) collective-permute-start(f32[256]{0:T(256)S(1)} %fusion.3), channel_id=1, source_target_pairs={{0,1},{1,0},{2,3},{3,2},{4,5},{5,4},{6,7},{7,6},{8,9},{9,8},{10,11... | collective-permute-start | bytes 3080 | tf_op jit(solution)/shard_map/ppermute | solution.py:19
  305.7 7.9 %copy-start.8 = (bf16[1,256,8,256]{1,3,2,0:T(8,128)(2,1)S(1)}, bf16[1,256,8,256]{1,3,2,0:T(8,128)(2,1)}, u32[]{:S(2)}) copy-start(bf16[1,256,8,256]{1,3,2,0:T(8,128)(2,1)} %copy-done.7) | copy-start | bytes 3145732
  307.8 7.6 %copy-start.11 = (bf16[256,2048]{0,1:T(8,128)(2,1)S(1)}, bf16[256,2048]{0,1:T(8,128)(2,1)}, u32[]{:S(2)}) copy-start(bf16[256,2048]{0,1:T(8,128)(2,1)} %copy.105) | copy-start | bytes 3145732
  307.8 7.6 %collective-permute-start.8 = (f32[256]{0:T(256)S(1)}, f32[256]{0:T(256)S(1)}, u32[]{:S(2)}, u32[]{:S(2)}) collective-permute-start(f32[256]{0:T(256)S(1)} %add.105), channel_id=1, source_target_pairs={{0,2},{1,3},{2,0},{3,1},{4,6},{5,7},{6,4},{7,5},{8,10},{9,11},{10,... | collective-permute-start | bytes 3080 | tf_op jit(solution)/shard_map/ppermute | solution.py:19
  317.3 2.4 copy-start.12
Sparse Core Ops, SparseCore 0:
  35.1 47.8 all-gather.1
  97.9 58.2 reduce-scatter.7
  158.8 49.4 reduce-scatter.9
  210.7 49.1 reduce-scatter.5
  264.2 39.2 reduce-scatter.11
  306.7 29.5 reduce-scatter.13

commit v6 on v5

--- a/solution.py
+++ b/solution.py
@@ -34,14 +34,25 @@
     return g.reshape((nz, nx, share) + rest)
 
 
-def scatter_rest(parts):
-    nz, nx, share = parts[0].shape[:3]
-    rest = parts[0].shape[3:]
-    g = jnp.moveaxis(jnp.stack(parts, axis=0), 2, 0)
-    g = lax.psum_scatter(g.reshape(nx, -1, rest[-1]), "dx", scatter_dimension=0, tiled=True)
-    g = jnp.moveaxis(g.reshape((len(parts), nz, share) + rest), 1, 0)
+def exchange_first(grads):
+    rows = grads.shape[0]
+    ny, nz, nx = (lax.axis_size(a) for a in ("dy", "dz", "dx"))
+    rest = grads.shape[1:]
+    g = grads.reshape((ny, nz, nx, rows // (ny * nz * nx)) + rest)
+    return jnp.sum(lax.all_to_all(g, "dx", 2, 2), axis=2)
+
+
+def scatter_rest(on_sc, on_tc):
+    nz, nx, share = on_sc[0].shape[:3]
+    rest = on_sc[0].shape[3:]
+    a, on_tc = lax.optimization_barrier((jnp.stack(on_sc, axis=0), on_tc))
+    a = jnp.moveaxis(a, 2, 0)
+    a = lax.psum_scatter(a.reshape(nx, -1, rest[-1]), "dx", scatter_dimension=0, tiled=True)
+    a = a.reshape((len(on_sc), nz, share) + rest)
+    b = jnp.sum(lax.all_to_all(on_tc, "dy", 0, 0), axis=0)
+    g = jnp.moveaxis(jnp.concatenate([b[None], a], axis=0), 1, 0)
     g = lax.psum_scatter(g.reshape(nz, -1, rest[-1]), "dz", scatter_dimension=0, tiled=True)
-    return g.reshape((len(parts), share) + rest)
+    return g.reshape((len(on_sc) + 1, share) + rest)
 
 
 def partner_rows(rows):
@@ -125,7 +136,7 @@
         stride = 1 << bit_index
         kept_hidden, kept_partner = stored_inputs[factor]
         joined = jnp.concatenate([kept_hidden, kept_partner], axis=2)
-        grad_terms[factor] = scatter_first(
+        grad_terms[factor] = (exchange_first if factor == 0 else scatter_first)(
             jnp.einsum("tbc,tbd->cbd", joined, grad_pre, preferred_element_type=jnp.float32)
             * grad_scale
         )
@@ -157,7 +168,7 @@
     token_grads = (
         cotangent.astype(jnp.float32) + inv_rms * (flat - normed * (inner_sum / D)[:, None])
     ).astype(jnp.bfloat16)
-    weight_grads = scatter_rest(grad_terms)
+    weight_grads = scatter_rest(grad_terms[1:], grad_terms[0])
     return (mixed, token_grads, weight_grads)
 
 

time: 344 us -> 304 us (0.88)
  waiting for transfers between devices: 208 us -> 127 us
  blocking collectives: 0 us -> 30.7 us
  other arithmetic: 5 us -> 10.5 us
  starting transfers between devices: 23.7 us -> 27.9 us
    reduce_scatter x3 -> x2, waiting for transfers between devices: 89.2 us -> 0.69 us  [scatter_first(): lax.psum_scatter(grads.reshape(ny, -1, rest[-1]), 'dy', scatter_dimension...]
    all_to_all x0 -> x1, blocking collectives: none -> 30.7 us  [exchange_first(): return jnp.sum(lax.all_to_all(g, 'dx', 2, 2), axis=2)]
    all_to_all x0 -> x1, waiting for transfers between devices: none -> 12.7 us  [scatter_rest(): b = jnp.sum(lax.all_to_all(on_tc, 'dy', 0, 0), axis=0)]
    reduce_scatter x1, waiting for transfers between devices: 36.7 us -> 31.2 us  [scatter_rest(): lax.psum_scatter(a.reshape(nx, -1, rest[-1]), 'dx', scatter_dimension=0,...]
    reduce_sum x0 -> x2, other arithmetic: none -> 4.98 us  [the longest x1 3.66 us: exchange_first(): return jnp.sum(lax.all_to_all(g, 'dx', 2, 2), axis=2)]
    all_to_all x0 -> x1, starting transfers between devices: none -> 4.25 us  [scatter_rest(): b = jnp.sum(lax.all_to_all(on_tc, 'dy', 0, 0), axis=0)]
  transfers between devices with their start and end apart: 15 -> 15, of which waited for: 9 -> 9; matrix products, arithmetic and copies ran while one was open for 22% -> 27% of each run, Pallas kernels for 0% -> 0%
where the time goes in v6:
time: 304 us; the launch traced here: 303 us
  waiting for transfers between devices  127 us (42%)
  local copies, waits for them, and re-layouts  55.7 us (18%)
  matrix products  36.7 us (12%)
  blocking collectives  30.7 us (10%)
  starting transfers between devices  27.9 us (9%)
  between operations  14.2 us (5%)
  other arithmetic  10.5 us (3%)
    ppermute x9, waiting for transfers between devices, swapped(): lax.ppermute(x, axis, [(i, i ^ 1 << stride) for i in range(lax.axis_size(...  62.3 us
    reduce_scatter x1, waiting for transfers between devices, scatter_rest(): lax.psum_scatter(a.reshape(nx, -1, rest[-1]), 'dx', scatter_dimension=0,...  31.2 us
    all_to_all x1, blocking collectives, exchange_first(): return jnp.sum(lax.all_to_all(g, 'dx', 2, 2), axis=2)  30.7 us
    ppermute x9, starting transfers between devices, swapped(): lax.ppermute(x, axis, [(i, i ^ 1 << stride) for i in range(lax.axis_size(...  23.5 us
    unnamed x46, local copies, waits for them, and re-layouts  17.1 us
    reduce_scatter x1, waiting for transfers between devices, scatter_rest(): lax.psum_scatter(g.reshape(nz, -1, rest[-1]), 'dz', scatter_dimension=0,...  15.3 us
    all_to_all x1, waiting for transfers between devices, scatter_rest(): b = jnp.sum(lax.all_to_all(on_tc, 'dy', 0, 0), axis=0)  12.7 us
    mul x2, local copies, waits for them, and re-layouts, shards(): jnp.einsum('tbc,tbd->cbd', joined, grad_pre, preferred_element_type=jnp.f...  10.9 us
  transfers between devices with their start and end apart: 15, of which 9 were waited for; matrix products, arithmetic and copies ran while one was open for 27% of the time, Pallas kernels for 0%

profile of v6, /device:TPU:2, one launch (start us, length us, event | category | flops | bytes accessed | tf_op | source)
XLA Modules:
  0.0 303.0 jit_solution(8945936479069369302)
XLA Ops:
  7.2 1.5 copy.157
  8.7 0.3 fusion.8
  9.1 5.2 %fusion.54 = (bf16[1,256,8,256]{3,2,1,0:T(8,128)(2,1)}, bf16[1,256,8,256]{3,2,1,0:T(8,128)(2,1)}, bf16[1,256,8,256]{3,2,1,0:T(8,128)(2,1)}, bf16[1,256,8,256]{3,...) fusion(bf16[3,512,8,256]{3,2,1,0:T(8,128)(2,1)} %param.4), kind=kLoop, calls=%fused_computation.80 | loop fusion | bytes 12582912 | tf_op jit(solution)/shard_map/slice | solution.py:88
  14.3 1.6 copy.221
  16.0 7.3 %collective-permute-start.1 = (f32[256]{0:T(256)S(1)}, f32[256]{0:T(256)S(1)}, u32[]{:S(2)}, u32[]{:S(2)}) collective-permute-start(f32[256]{0:T(256)S(1)} %add.82), channel_id=1, source_target_pairs={{0,2},{1,3},{2,0},{3,1},{4,6},{5,7},{6,4},{7,5},{8,10},{9,11},{10,... | collective-permute-start | bytes 3080 | tf_op jit(solution)/shard_map/ppermute | solution.py:19
  23.3 1.0 constant_dynamic-slice_fusion
  24.3 1.2 copy.174
  25.6 2.4 copy.218
  28.0 1.6 copy.217
  29.6 0.2 fusion.2
  29.8 1.3 copy.160
  31.1 1.3 rev.8
  32.4 2.0 collective-permute-done.5
  34.4 0.6 copy-done.18
  35.1 1.8 fusion.46
  36.9 2.3 fusion.38
  39.2 1.0 copy.234
  40.3 4.0 %collective-permute-start.3 = (bf16[256,8,256]{2,0,1:T(8,128)(2,1)}, bf16[256,8,256]{2,0,1:T(8,128)(2,1)}, u32[]{:S(2)}, u32[]{:S(2)}) collective-permute-start(bf16[256,8,256]{2,0,1:T(8,128)(2,1)} %bitcast.127), channel_id=1, source_target_pairs={{0,2},{1,3},{2,0},{3,1},{4,6},{5,7},{6,4},{7,5},{8,10},{9,11},{10,... | collective-permute-start | bytes 3145736 | tf_op jit(solution)/shard_map/ppermute | solution.py:19
  44.3 1.6 copy.216
  46.0 1.8 fusion.41
  48.0 1.8 fusion.50
  49.8 3.7 %fusion.34 = (bf16[256,8,256]{0,2,1:T(8,128)(2,1)}, f32[8,256,256]{1,2,0:T(8,128)}) fusion(f32[8,256,256]{1,2,0:T(8,128)S(1)} %fusion.50, bf16[256,8,256]{0,2,1:T(8,128)(2,1)} %collective-permute-done.2, bf16[1,256,8,256]{3,2,1,0:T(8,128)(2,1)S(1)} %copy-done.3), kind=kOutput, calls=%fused_computation.47 | convolution fusion | flops 271581184 | bytes 7340032 | tf_op jit(solution)/shard_map/tbc,cbd->tbd/dot_general | solution.py:87
  53.5 24.6 %collective-permute-done.3 = bf16[256,8,256]{2,0,1:T(8,128)(2,1)} collective-permute-done((bf16[256,8,256]{2,0,1:T(8,128)(2,1)}, bf16[256,8,256]{2,0,1:T(8,128)(2,1)}, u32[]{:S(2)}, u32[]{:S(2)}) %collective-permute-start.3) | collective-permute-done | bytes 1048608 | tf_op jit(solution)/shard_map/ppermute | solution.py:19
  78.1 4.9 %all-gather.2.cloned.1.call-done = bf16[256,8,256]{2,0,1:T(8,128)(2,1)} async-done(((bf16[16,8,256]{2,0,1:T(8,128)(2,1)}), bf16[256,8,256]{2,0,1:T(8,128)(2,1)}) %all-gather.2.cloned.1.call-update) | async-done | bytes 1048592 | tf_op jit(solution)/shard_map/all_gather | solution.py:64
  83.0 4.0 %fusion.15 = bf16[256,8,256]{0,2,1:T(8,128)(2,1)S(1)} fusion(f32[8,256,256]{1,2,0:T(8,128)} %get-tuple-element.36, f32[8,256,256]{2,1,0:T(8,128)} %fusion.41, bf16[256,8,256]{2,0,1:T(8,128)(2,1)} %all-gather.2.cloned.1.call-done, bf16[256,8,256]{2,0,1:T(8,128)(2,1)} %collective-permute-done.3), kind=kOutput, calls=%fused_computation.23 | convolution fusion | flops 274202624 | bytes 7340032 | tf_op jit(solution)/shard_map/tbd,cbd->tbc/dot_general | solution.py:126
  87.0 1.0 copy-done.15
  87.9 4.3 %multiply_bitcast_fusion.2 = f32[512,8,256]{0,2,1:T(8,128)} fusion(bf16[256,8,256]{0,2,1:T(8,128)(2,1)S(1)} %fusion.15, bf16[256,8,256]{0,2,1:T(8,128)(2,1)} %collective-permute-done.2, bf16[256,8,256]{0,2,1:T(8,128)(2,1)} %get-tuple-element.33), kind=kOutput, calls=%fused_computation.2 | convolution fusion | flops 542113792 | bytes 7340032 | tf_op jit(solution)/shard_map/tbc,tbd->cbd/dot_general | solution.py:140
  92.2 5.4 %copy.187 = f32[512,8,256]{2,1,0:T(8,128)} copy(f32[512,8,256]{0,2,1:T(8,128)} %multiply_bitcast_fusion.2) | data formatting | bytes 8388608 | tf_op jit(solution)/shard_map/mul | solution.py:140
  97.8 1.8 convolution_bitcast_fusion
  99.6 0.3 collective-permute-start.6
  99.9 5.8 %collective-permute-start.4 = (bf16[256,8,256]{0,2,1:T(8,128)(2,1)}, bf16[256,8,256]{0,2,1:T(8,128)(2,1)}, u32[]{:S(2)}, u32[]{:S(2)}) collective-permute-start(bf16[256,8,256]{0,2,1:T(8,128)(2,1)} %get-tuple-element.8), channel_id=1, source_target_pairs={{0,2},{1,3},{2,0},{3,1},{4,6},{5,7},{6,4},{7,5},{8,10},{9,11},{10,... | collective-permute-start | bytes 3145736 | tf_op jit(solution)/shard_map/ppermute | solution.py:19
  105.7 1.4 fusion.21
  107.1 0.5 fusion.44
  107.6 0.5 copy-done.6
  108.1 1.9 copy.183
  110.0 3.1 %rev.9 = f32[256,1,2,4,256]{0,4,3,2,1:T(8,128)} reverse(f32[256,1,2,4,256]{0,4,3,2,1:T(8,128)} %copy.183), dimensions={2} | reverse | bytes 4194304 | tf_op jit(solution)/shard_map/jit(_flip)/rev | solution.py:80
  113.1 2.8 bitcast_add_fusion
  115.9 35.7 %collective-permute-done.4 = bf16[256,8,256]{0,2,1:T(8,128)(2,1)} collective-permute-done((bf16[256,8,256]{0,2,1:T(8,128)(2,1)}, bf16[256,8,256]{0,2,1:T(8,128)(2,1)}, u32[]{:S(2)}, u32[]{:S(2)}) %collective-permute-start.4) | collective-permute-done | bytes 1048608 | tf_op jit(solution)/shard_map/ppermute | solution.py:19
  151.5 2.3 multiply_bitcast_fusion.1
  153.8 4.4 %copy.189 = f32[512,8,256]{2,1,0:T(8,128)} copy(f32[512,8,256]{2,0,1:T(8,128)S(1)} %multiply_bitcast_fusion.1) | data formatting | bytes 8388608 | tf_op jit(solution)/shard_map/mul | solution.py:163
  158.3 2.3 copy.192
  160.6 4.6 %multiply_bitcast_fusion = f32[512,8,256]{0,2,1:T(8,128)} fusion(bf16[256,8,256]{0,2,1:T(8,128)(2,1)} %copy-done.6, bf16[256,8,256]{2,0,1:T(8,128)(2,1)} %bitcast.138, bf16[256,8,256]{2,0,1:T(8,128)(2,1)} %copy.192), kind=kOutput, calls=%fused_computation | convolution fusion | flops 542113792 | bytes 7340032 | tf_op jit(solution)/shard_map/tbc,tbd->cbd/dot_general | solution.py:140
  165.1 5.4 %copy.193 = f32[512,8,256]{2,1,0:T(8,128)} copy(f32[512,8,256]{0,2,1:T(8,128)} %multiply_bitcast_fusion) | data formatting | bytes 8388608 | tf_op jit(solution)/shard_map/mul | solution.py:140
  170.6 2.6 copy.194
  173.2 30.7 %all_to_all.10 = f32[4,4,4,8,8,256]{5,4,3,1,0,2:T(8,128)} all-to-all(f32[4,4,4,8,8,256]{5,4,3,1,0,2:T(8,128)S(1)} %copy.194), channel_id=1, replica_groups=mesh['dy'=4,'dz'=4,'dx'=4,'tensor'=4] {'dx'}, dimensions={2} | all-to-all | bytes 8388608 | tf_op jit(solution)/shard_map/all_to_all | solution.py:42
  203.9 3.7 %reduce_sum.38 = f32[4,4,8,8,256]{4,3,2,1,0:T(8,128)} reduce(f32[4,4,4,8,8,256]{5,4,3,1,0,2:T(8,128)} %all_to_all.10, f32[]{:T(128)} %constant.7.clone.1), dimensions={2}, to_apply=%region_4.5 | reduce | flops 786432 | bytes 5242884 | tf_op jit(solution)/shard_map/reduce_sum | solution.py:42
  207.6 0.7 reduce-scatter.7.cloned.1.call-done
  208.3 1.7 pad_maximum_fusion
  209.9 1.5 copy.215
  211.4 4.3 %all-to-all-start.1 = ((f32[4,4,8,8,256]{4,3,2,1,0:T(8,128)}), f32[4,4,8,8,256]{4,3,2,1,0:T(8,128)}, u32[]{:S(2)}, u32[]{:S(2)}) async-start(f32[4,4,8,8,256]{4,3,2,1,0:T(8,128)} %reduce_sum.38), calls=%async_computation.3 | async-start | bytes 2097152 | tf_op jit(solution)/shard_map/all_to_all | solution.py:52
  215.8 2.3 copy.185
  218.0 0.3 fusion.3
  218.5 12.7 %all-to-all-done.1 = f32[4,4,8,8,256]{4,3,2,1,0:T(8,128)} async-done(((f32[4,4,8,8,256]{4,3,2,1,0:T(8,128)}), f32[4,4,8,8,256]{4,3,2,1,0:T(8,128)}, u32[]{:S(2)}, u32[]{:S(2)}) %all-to-all-start.1) | async-done | bytes 1048608 | tf_op jit(solution)/shard_map/all_to_all | solution.py:52
  231.2 1.3 reduce_sum.39
  232.5 31.2 %reduce-scatter.9.cloned.1.call-done = f32[1,512,256]{2,1,0:T(8,128)} async-done(((f32[4,512,256]{2,1,0:T(8,128)}), f32[1,512,256]{2,1,0:T(8,128)}) %reduce-scatter.9.cloned.1.call-update) | async-done | bytes 524304 | tf_op jit(solution)/shard_map/reduce_scatter | solution.py:50
  263.7 1.1 maximum_bitcast_fusion
  264.8 0.9 copy.195
  265.8 2.1 fusion.39
  267.9 5.8 %collective-permute-start.8 = (f32[256]{0:T(256)S(1)}, f32[256]{0:T(256)S(1)}, u32[]{:S(2)}, u32[]{:S(2)}) collective-permute-start(f32[256]{0:T(256)S(1)} %add.103), channel_id=1, source_target_pairs={{0,2},{1,3},{2,0},{3,1},{4,6},{5,7},{6,4},{7,5},{8,10},{9,11},{10,... | collective-permute-start | bytes 3080 | tf_op jit(solution)/shard_map/ppermute | solution.py:19
  273.7 1.7 convolution_add_fusion
  275.5 1.9 fusion.7
  277.4 2.4 copy.196
  279.8 1.4 copy.197
  281.2 15.3 %reduce-scatter.11.cloned.1.call-done = f32[1,192,256]{2,1,0:T(8,128)} async-done(((f32[4,192,256]{2,1,0:T(8,128)}), f32[1,192,256]{2,1,0:T(8,128)}) %reduce-scatter.11.cloned.1.call-update) | async-done | bytes 196624 | tf_op jit(solution)/shard_map/reduce_scatter | solution.py:54
  (60 shorter events, 0.9 us)
Async XLA Ops:
  7.2 75.9 %all-gather.2.cloned.1.call-start = ((), (), s32[]{:S(2)}) async-start(), calls=%async_computation.6 | async-start | bytes 1114112 | tf_op jit(solution)/shard_map/all_gather | solution.py:64
  9.0 7.0 %collective-permute-start = (f32[256]{0:T(256)S(1)}, f32[256]{0:T(256)S(1)}, u32[]{:S(2)}, u32[]{:S(2)}) collective-permute-start(f32[256]{0:T(256)S(1)} %fusion.8), channel_id=1, source_target_pairs={{0,1},{1,0},{2,3},{3,2},{4,5},{5,4},{6,7},{7,6},{8,9},{9,8},{10,11... | collective-permute-start | bytes 3080 | tf_op jit(solution)/shard_map/ppermute | solution.py:19
  16.0 13.6 %copy-start.10 = (bf16[1,256,8,256]{1,3,2,0:T(8,128)(2,1)}, bf16[1,256,8,256]{1,3,2,0:T(8,128)(2,1)S(1)}, u32[]{:S(2)}) copy-start(bf16[1,256,8,256]{1,3,2,0:T(8,128)(2,1)S(1)} %copy.221) | copy-start | bytes 3145732
  16.0 13.6 %collective-permute-start.1 = (f32[256]{0:T(256)S(1)}, f32[256]{0:T(256)S(1)}, u32[]{:S(2)}, u32[]{:S(2)}) collective-permute-start(f32[256]{0:T(256)S(1)} %add.82), channel_id=1, source_target_pairs={{0,2},{1,3},{2,0},{3,1},{4,6},{5,7},{6,4},{7,5},{8,10},{9,11},{10,... | collective-permute-start | bytes 3080 | tf_op jit(solution)/shard_map/ppermute | solution.py:19
  25.5 8.9 %collective-permute-start.5 = (bf16[16,8,256]{2,0,1:T(8,128)(2,1)S(1)}, bf16[16,8,256]{2,0,1:T(8,128)(2,1)S(1)}, u32[]{:S(2)}, u32[]{:S(2)}) collective-permute-start(bf16[16,8,256]{2,0,1:T(8,128)(2,1)S(1)} %bitcast.146), channel_id=1, source_target_pairs={{0,2},{1,3},{2,0},{3,1},{4,6},{5,7},{6,4},{7,5},{8,10},{9,11},{10,... | collective-permute-start | bytes 196616 | tf_op jit(solution)/shard_map/ppermute | solution.py:19
  29.8 7.1 %copy-start = (bf16[256,2048]{0,1:T(8,128)(2,1)}, bf16[256,2048]{0,1:T(8,128)(2,1)S(1)}, u32[]{:S(2)}) copy-start(bf16[256,2048]{0,1:T(8,128)(2,1)S(1)} %fusion.2) | copy-start | bytes 3145732
  32.4 4.5 %copy-start.4 = (bf16[256,1,2,4,256]{4,0,3,2,1:T(8,128)(2,1)}, bf16[256,1,2,4,256]{4,0,3,2,1:T(8,128)(2,1)S(1)}, u32[]{:S(2)}) copy-start(bf16[256,1,2,4,256]{4,0,3,2,1:T(8,128)(2,1)S(1)} %rev.8) | copy-start | bytes 3145732
  34.4 0.6 copy-start.18
  35.0 172.5 %reduce-scatter.5.cloned.1.call-start = ((), (), s32[]{:S(2)}) async-start(), calls=%async_computation.7 | async-start | bytes 5242880 | tf_op jit(solution)/shard_map/reduce_scatter | solution.py:33
  35.1 1.8 copy-start.5
  36.9 2.3 copy-start.1
  39.2 10.6 %collective-permute-start.2 = (bf16[256,8,256]{0,2,1:T(8,128)(2,1)}, bf16[256,8,256]{0,2,1:T(8,128)(2,1)}, u32[]{:S(2)}, u32[]{:S(2)}) collective-permute-start(bf16[256,8,256]{0,2,1:T(8,128)(2,1)} %get-tuple-element.33), channel_id=1, source_target_pairs={{0,1},{1,0},{2,3},{3,2},{4,5},{5,4},{6,7},{7,6},{8,9},{9,8},{10,11... | collective-permute-start | bytes 3145736 | tf_op jit(solution)/shard_map/ppermute | solution.py:19
  40.3 37.8 %collective-permute-start.3 = (bf16[256,8,256]{2,0,1:T(8,128)(2,1)}, bf16[256,8,256]{2,0,1:T(8,128)(2,1)}, u32[]{:S(2)}, u32[]{:S(2)}) collective-permute-start(bf16[256,8,256]{2,0,1:T(8,128)(2,1)} %bitcast.127), channel_id=1, source_target_pairs={{0,2},{1,3},{2,0},{3,1},{4,6},{5,7},{6,4},{7,5},{8,10},{9,11},{10,... | collective-permute-start | bytes 3145736 | tf_op jit(solution)/shard_map/ppermute | solution.py:19
  45.9 1.9 copy-start.7
  45.9 2.0 copy-start.13
  48.0 1.8 copy-start.3
  87.0 1.0 copy-start.15
  97.7 8.0 %copy-start.14 = (bf16[1,256,8,256]{3,2,1,0:T(8,128)(2,1)S(1)}, bf16[1,256,8,256]{3,2,1,0:T(8,128)(2,1)}, u32[]{:S(2)}) copy-start(bf16[1,256,8,256]{3,2,1,0:T(8,128)(2,1)} %get-tuple-element.26) | copy-start | bytes 3145732
  97.7 110.6 %reduce-scatter.7.cloned.1.call-start = ((), (), s32[]{:S(2)}) async-start(), calls=%async_computation.8 | async-start | bytes 5242880 | tf_op jit(solution)/shard_map/reduce_scatter | solution.py:33
  97.8 8.0 %copy-start.16 = (bf16[256,8,256]{0,2,1:T(8,128)(2,1)S(1)}, bf16[256,8,256]{0,2,1:T(8,128)(2,1)}, u32[]{:S(2)}) copy-start(bf16[256,8,256]{0,2,1:T(8,128)(2,1)} %copy-done.15) | copy-start | bytes 3145732
  97.8 8.0 %copy-start.17 = (f32[8,256,256]{1,2,0:T(8,128)S(1)}, f32[8,256,256]{1,2,0:T(8,128)}, u32[]{:S(2)}) copy-start(f32[8,256,256]{1,2,0:T(8,128)} %get-tuple-element.34) | copy-start | bytes 6291460
  99.6 6.1 %collective-permute-start.6 = (f32[256,8,256]{0,2,1:T(8,128)S(1)}, f32[256,8,256]{0,2,1:T(8,128)S(1)}, u32[]{:S(2)}, u32[]{:S(2)}) collective-permute-start(f32[256,8,256]{0,2,1:T(8,128)S(1)} %convolution_bitcast_fusion), channel_id=1, source_target_pairs={{0,1},{1,0},{2,3},{3,2},{4,5},{5,4},{6,7},{7,6},{8,9},{9,8},{10,11... | collective-permute-start | bytes 6291464 | tf_op jit(solution)/shard_map/ppermute | solution.py:19
  99.9 51.7 %collective-permute-start.4 = (bf16[256,8,256]{0,2,1:T(8,128)(2,1)}, bf16[256,8,256]{0,2,1:T(8,128)(2,1)}, u32[]{:S(2)}, u32[]{:S(2)}) collective-permute-start(bf16[256,8,256]{0,2,1:T(8,128)(2,1)} %get-tuple-element.8), channel_id=1, source_target_pairs={{0,2},{1,3},{2,0},{3,1},{4,6},{5,7},{6,4},{7,5},{8,10},{9,11},{10,... | collective-permute-start | bytes 3145736 | tf_op jit(solution)/shard_map/ppermute | solution.py:19
  105.7 1.4 copy-start.9
  107.1 1.0 copy-start.6
  113.1 38.5 %copy-start.2 = (bf16[256,2048]{1,0:T(8,128)(2,1)S(1)}, bf16[256,2048]{1,0:T(8,128)(2,1)}, u32[]{:S(2)}) copy-start(bf16[256,2048]{1,0:T(8,128)(2,1)} %param.5) | copy-start | bytes 3145732
  158.3 105.5 %reduce-scatter.9.cloned.1.call-start = ((), (), s32[]{:S(2)}) async-start(), calls=%async_computation.9 | async-start | bytes 2621440 | tf_op jit(solution)/shard_map/reduce_scatter | solution.py:50
  211.4 19.7 %all-to-all-start.1 = ((f32[4,4,8,8,256]{4,3,2,1,0:T(8,128)}), f32[4,4,8,8,256]{4,3,2,1,0:T(8,128)}, u32[]{:S(2)}, u32[]{:S(2)}) async-start(f32[4,4,8,8,256]{4,3,2,1,0:T(8,128)} %reduce_sum.38), calls=%async_computation.3 | async-start | bytes 2097152 | tf_op jit(solution)/shard_map/all_to_all | solution.py:52
  215.7 80.8 %reduce-scatter.11.cloned.1.call-start = ((), (), s32[]{:S(2)}) async-start(), calls=%async_computation.10 | async-start | bytes 983040 | tf_op jit(solution)/shard_map/reduce_scatter | solution.py:54
  218.4 49.5 %collective-permute-start.7 = (f32[256]{0:T(256)S(1)}, f32[256]{0:T(256)S(1)}, u32[]{:S(2)}, u32[]{:S(2)}) collective-permute-start(f32[256]{0:T(256)S(1)} %fusion.3), channel_id=1, source_target_pairs={{0,1},{1,0},{2,3},{3,2},{4,5},{5,4},{6,7},{7,6},{8,9},{9,8},{10,11... | collective-permute-start | bytes 3080 | tf_op jit(solution)/shard_map/ppermute | solution.py:19
  265.8 7.9 %copy-start.8 = (bf16[1,256,8,256]{1,3,2,0:T(8,128)(2,1)S(1)}, bf16[1,256,8,256]{1,3,2,0:T(8,128)(2,1)}, u32[]{:S(2)}) copy-start(bf16[1,256,8,256]{1,3,2,0:T(8,128)(2,1)} %copy-done.7) | copy-start | bytes 3145732
  267.9 7.6 %copy-start.11 = (bf16[256,2048]{0,1:T(8,128)(2,1)S(1)}, bf16[256,2048]{0,1:T(8,128)(2,1)}, u32[]{:S(2)}) copy-start(bf16[256,2048]{0,1:T(8,128)(2,1)} %copy.185) | copy-start | bytes 3145732
  267.9 7.6 %collective-permute-start.8 = (f32[256]{0:T(256)S(1)}, f32[256]{0:T(256)S(1)}, u32[]{:S(2)}, u32[]{:S(2)}) collective-permute-start(f32[256]{0:T(256)S(1)} %add.103), channel_id=1, source_target_pairs={{0,2},{1,3},{2,0},{3,1},{4,6},{5,7},{6,4},{7,5},{8,10},{9,11},{10,... | collective-permute-start | bytes 3080 | tf_op jit(solution)/shard_map/ppermute | solution.py:19
  277.4 2.4 copy-start.12
Sparse Core Ops, SparseCore 0:
  35.1 47.8 all-gather.1
  97.8 58.2 reduce-scatter.4
  158.8 49.3 reduce-scatter.6
  211.6 52.1 reduce-scatter.8
  266.9 29.5 reduce-scatter.10

commit v7 on v6

--- a/solution.py
+++ b/solution.py
@@ -45,14 +45,15 @@
 def scatter_rest(on_sc, on_tc):
     nz, nx, share = on_sc[0].shape[:3]
     rest = on_sc[0].shape[3:]
-    a, on_tc = lax.optimization_barrier((jnp.stack(on_sc, axis=0), on_tc))
+    b = jnp.stack(on_tc, axis=0)
+    a, b = lax.optimization_barrier((jnp.stack(on_sc, axis=0), b))
     a = jnp.moveaxis(a, 2, 0)
     a = lax.psum_scatter(a.reshape(nx, -1, rest[-1]), "dx", scatter_dimension=0, tiled=True)
     a = a.reshape((len(on_sc), nz, share) + rest)
-    b = jnp.sum(lax.all_to_all(on_tc, "dy", 0, 0), axis=0)
-    g = jnp.moveaxis(jnp.concatenate([b[None], a], axis=0), 1, 0)
+    b = jnp.sum(lax.all_to_all(jnp.moveaxis(b, 1, 0), "dy", 0, 0), axis=0)
+    g = jnp.moveaxis(jnp.concatenate([b, a], axis=0), 1, 0)
     g = lax.psum_scatter(g.reshape(nz, -1, rest[-1]), "dz", scatter_dimension=0, tiled=True)
-    return g.reshape((len(on_sc) + 1, share) + rest)
+    return g.reshape((len(on_tc) + len(on_sc), share) + rest)
 
 
 def partner_rows(rows):
@@ -136,7 +137,7 @@
         stride = 1 << bit_index
         kept_hidden, kept_partner = stored_inputs[factor]
         joined = jnp.concatenate([kept_hidden, kept_partner], axis=2)
-        grad_terms[factor] = (exchange_first if factor == 0 else scatter_first)(
+        grad_terms[factor] = exchange_first(
             jnp.einsum("tbc,tbd->cbd", joined, grad_pre, preferred_element_type=jnp.float32)
             * grad_scale
         )
@@ -155,7 +156,9 @@
         if factor > 0:
             previous = stored_preact[factor - 1]
             grad_pre = (grad_hidden * gelu_slope(previous)).astype(jnp.bfloat16)
-    partner_top, _ = lax.optimization_barrier((partner_top, grad_hidden))
+    partner_top, _, grad_terms[top - 1] = lax.optimization_barrier(
+        (partner_top, grad_hidden, grad_terms[top - 1])
+    )
     preact = apply_factor(hidden, partner_top, top_weights)
     mixed = (tokens_f32 + preact.reshape(tok_rows, local_width)).astype(jnp.bfloat16)
     joined = jnp.concatenate([hidden, partner_top], axis=2)
@@ -168,7 +171,7 @@
     token_grads = (
         cotangent.astype(jnp.float32) + inv_rms * (flat - normed * (inner_sum / D)[:, None])
     ).astype(jnp.bfloat16)
-    weight_grads = scatter_rest(grad_terms[1:], grad_terms[0])
+    weight_grads = scatter_rest(grad_terms[top:], grad_terms[:top])
     return (mixed, token_grads, weight_grads)
 
 

time: 304 us -> 321 us (1.056)
  waiting for transfers between devices: 127 us -> 104 us
  blocking collectives: 30.7 us -> 52.4 us
  other arithmetic: 10.5 us -> 16.9 us
  starting transfers between devices: 27.9 us -> 33.8 us
  local copies, waits for them, and re-layouts: 55.7 us -> 60.2 us
    ppermute x9, waiting for transfers between devices: 62.3 us -> 26.2 us  [swapped(): lax.ppermute(x, axis, [(i, i ^ 1 << stride) for i in range(lax.axis_size(...]
    all_to_all x1 -> x2, waiting for transfers between devices: 12.7 us -> 47.6 us  [the longest x1 31 us: exchange_first(): return jnp.sum(lax.all_to_all(g, 'dx', 2, 2), axis=2)]
    reduce_scatter x1, waiting for transfers between devices: 31.2 us -> 0.01 us  [scatter_rest(): lax.psum_scatter(a.reshape(nx, -1, rest[-1]), 'dx', scatter_dimension=0,...]
    all_to_all x1, blocking collectives: 30.7 us -> 52.4 us  [exchange_first(): return jnp.sum(lax.all_to_all(g, 'dx', 2, 2), axis=2)]
    reduce_scatter x1, waiting for transfers between devices: 15.3 us -> 24.8 us  [scatter_rest(): lax.psum_scatter(g.reshape(nz, -1, rest[-1]), 'dz', scatter_dimension=0,...]
    all_to_all x1 -> x2, starting transfers between devices: 4.25 us -> 10.3 us  [the longest x1 5.8 us: exchange_first(): return jnp.sum(lax.all_to_all(g, 'dx', 2, 2), axis=2)]
    reshape x1 -> x2, local copies, waits for them, and re-layouts: 2.64 us -> 7.12 us  [exchange_first(): g = grads.reshape((ny, nz, nx, rows // (ny * nz * nx)) + rest)]
    reduce_sum x1 -> x2, other arithmetic: 3.66 us -> 7.17 us  [exchange_first(): return jnp.sum(lax.all_to_all(g, 'dx', 2, 2), axis=2)]
  transfers between devices with their start and end apart: 15 -> 15, of which waited for: 9 -> 6; matrix products, arithmetic and copies ran while one was open for 27% -> 30% of each run, Pallas kernels for 0% -> 0%
where the time goes in v7:
time: 321 us; the launch traced here: 320 us
  waiting for transfers between devices  104 us (32%)
  local copies, waits for them, and re-layouts  60.2 us (19%)
  blocking collectives  52.4 us (16%)
  matrix products  38.5 us (12%)
  starting transfers between devices  33.8 us (11%)
  other arithmetic  16.9 us (5%)
  between operations  14.1 us (4%)
    all_to_all x1, blocking collectives, exchange_first(): return jnp.sum(lax.all_to_all(g, 'dx', 2, 2), axis=2)  52.4 us
    all_to_all x1, waiting for transfers between devices, exchange_first(): return jnp.sum(lax.all_to_all(g, 'dx', 2, 2), axis=2)  31 us
    ppermute x9, waiting for transfers between devices, swapped(): lax.ppermute(x, axis, [(i, i ^ 1 << stride) for i in range(lax.axis_size(...  26.2 us
    reduce_scatter x1, waiting for transfers between devices, scatter_rest(): lax.psum_scatter(g.reshape(nz, -1, rest[-1]), 'dz', scatter_dimension=0,...  24.8 us
    ppermute x9, starting transfers between devices, swapped(): lax.ppermute(x, axis, [(i, i ^ 1 << stride) for i in range(lax.axis_size(...  23.4 us
    all_to_all x1, waiting for transfers between devices, scatter_rest(): b = jnp.sum(lax.all_to_all(jnp.moveaxis(b, 1, 0), 'dy', 0, 0), axis=0)  16.6 us
    unnamed x38, local copies, waits for them, and re-layouts  16.1 us
    mul x2, local copies, waits for them, and re-layouts, shards(): jnp.einsum('tbc,tbd->cbd', joined, grad_pre, preferred_element_type=jnp.f...  11 us
  transfers between devices with their start and end apart: 15, of which 6 were waited for; matrix products, arithmetic and copies ran while one was open for 30% of the time, Pallas kernels for 0%

profile of v7, /device:TPU:2, one launch (start us, length us, event | category | flops | bytes accessed | tf_op | source)
XLA Modules:
  0.0 319.9 jit_solution(13578430023348678976)
XLA Ops:
  7.2 1.5 copy.194
  8.7 0.3 fusion.8
  9.1 5.2 %fusion.54 = (bf16[1,256,8,256]{3,2,1,0:T(8,128)(2,1)}, bf16[1,256,8,256]{3,2,1,0:T(8,128)(2,1)}, bf16[1,256,8,256]{3,2,1,0:T(8,128)(2,1)}, bf16[1,256,8,256]{3,...) fusion(bf16[3,512,8,256]{3,2,1,0:T(8,128)(2,1)} %param.4), kind=kLoop, calls=%fused_computation.80 | loop fusion | bytes 12582912 | tf_op jit(solution)/shard_map/slice | solution.py:89
  14.3 1.6 copy.257
  16.0 7.3 %collective-permute-start.1 = (f32[256]{0:T(256)S(1)}, f32[256]{0:T(256)S(1)}, u32[]{:S(2)}, u32[]{:S(2)}) collective-permute-start(f32[256]{0:T(256)S(1)} %add.80), channel_id=1, source_target_pairs={{0,2},{1,3},{2,0},{3,1},{4,6},{5,7},{6,4},{7,5},{8,10},{9,11},{10,... | collective-permute-start | bytes 3080 | tf_op jit(solution)/shard_map/ppermute | solution.py:19
  23.3 1.0 constant_dynamic-slice_fusion
  24.3 1.2 copy.211
  25.6 2.4 copy.254
  28.1 1.6 copy.253
  29.6 0.2 fusion.2
  29.9 1.3 copy.197
  31.2 1.3 rev.8
  32.5 1.9 collective-permute-done.5
  34.4 0.6 copy-done.14
  35.0 1.8 fusion.46
  36.9 2.3 fusion.38
  39.2 1.0 copy.270
  40.2 4.1 %collective-permute-start.3 = (bf16[256,8,256]{2,0,1:T(8,128)(2,1)}, bf16[256,8,256]{2,0,1:T(8,128)(2,1)}, u32[]{:S(2)}, u32[]{:S(2)}) collective-permute-start(bf16[256,8,256]{2,0,1:T(8,128)(2,1)} %bitcast.127), channel_id=1, source_target_pairs={{0,2},{1,3},{2,0},{3,1},{4,6},{5,7},{6,4},{7,5},{8,10},{9,11},{10,... | collective-permute-start | bytes 3145736 | tf_op jit(solution)/shard_map/ppermute | solution.py:19
  44.3 1.6 copy.252
  46.0 1.8 fusion.41
  47.8 0.2 copy-done.12
  48.0 1.8 fusion.50
  49.8 3.6 %fusion.34 = (bf16[256,8,256]{0,2,1:T(8,128)(2,1)}, f32[8,256,256]{1,2,0:T(8,128)}) fusion(f32[8,256,256]{1,2,0:T(8,128)S(1)} %fusion.50, bf16[256,8,256]{0,2,1:T(8,128)(2,1)} %collective-permute-done.2, bf16[1,256,8,256]{3,2,1,0:T(8,128)(2,1)S(1)} %copy-done.2), kind=kOutput, calls=%fused_computation.47 | convolution fusion | flops 271581184 | bytes 7340032 | tf_op jit(solution)/shard_map/tbc,cbd->tbd/dot_general | solution.py:88
  53.5 24.3 %collective-permute-done.3 = bf16[256,8,256]{2,0,1:T(8,128)(2,1)} collective-permute-done((bf16[256,8,256]{2,0,1:T(8,128)(2,1)}, bf16[256,8,256]{2,0,1:T(8,128)(2,1)}, u32[]{:S(2)}, u32[]{:S(2)}) %collective-permute-start.3) | collective-permute-done | bytes 1048608 | tf_op jit(solution)/shard_map/ppermute | solution.py:19
  77.8 5.3 %all-gather.2.cloned.1.call-done = bf16[256,8,256]{2,0,1:T(8,128)(2,1)} async-done(((bf16[16,8,256]{2,0,1:T(8,128)(2,1)}), bf16[256,8,256]{2,0,1:T(8,128)(2,1)}) %all-gather.2.cloned.1.call-update) | async-done | bytes 1048592 | tf_op jit(solution)/shard_map/all_gather | solution.py:65
  83.1 4.0 %fusion.15 = bf16[256,8,256]{0,2,1:T(8,128)(2,1)S(1)} fusion(f32[8,256,256]{1,2,0:T(8,128)} %get-tuple-element.41, f32[8,256,256]{2,1,0:T(8,128)} %fusion.41, bf16[256,8,256]{2,0,1:T(8,128)(2,1)} %all-gather.2.cloned.1.call-done, bf16[256,8,256]{2,0,1:T(8,128)(2,1)} %collective-permute-done.3), kind=kOutput, calls=%fused_computation.23 | convolution fusion | flops 274202624 | bytes 7340032 | tf_op jit(solution)/shard_map/tbd,cbd->tbc/dot_general | solution.py:127
  87.0 1.8 convolution_bitcast_fusion
  88.9 4.2 %multiply_bitcast_fusion.2 = f32[512,8,256]{0,2,1:T(8,128)} fusion(bf16[256,8,256]{0,2,1:T(8,128)(2,1)S(1)} %fusion.15, bf16[256,8,256]{0,2,1:T(8,128)(2,1)} %collective-permute-done.2, bf16[256,8,256]{0,2,1:T(8,128)(2,1)} %get-tuple-element.38), kind=kOutput, calls=%fused_computation.2 | convolution fusion | flops 542113792 | bytes 7340032 | tf_op jit(solution)/shard_map/tbc,tbd->cbd/dot_general | solution.py:141
  93.1 5.5 %copy.222 = f32[512,8,256]{2,1,0:T(8,128)} copy(f32[512,8,256]{0,2,1:T(8,128)} %multiply_bitcast_fusion.2) | data formatting | bytes 8388608 | tf_op jit(solution)/shard_map/mul | solution.py:141
  98.6 4.6 %copy.223 = f32[4,4,4,8,8,256]{5,4,3,1,0,2:T(8,128)} copy(f32[4,4,4,8,8,256]{5,4,3,2,1,0:T(8,128)} %bitcast.132) | data formatting | bytes 8388608 | tf_op jit(solution)/shard_map/reshape | solution.py:41
  103.2 5.8 %all-to-all-start = ((f32[4,4,4,8,8,256]{5,4,3,1,0,2:T(8,128)}), f32[4,4,4,8,8,256]{5,4,3,1,0,2:T(8,128)}, u32[]{:S(2)}, u32[]{:S(2)}) async-start(f32[4,4,4,8,8,256]{5,4,3,1,0,2:T(8,128)} %copy.223), calls=%async_computation | async-start | bytes 8388608 | tf_op jit(solution)/shard_map/all_to_all | solution.py:42
  109.0 5.7 %collective-permute-start.4 = (bf16[256,8,256]{0,2,1:T(8,128)(2,1)}, bf16[256,8,256]{0,2,1:T(8,128)(2,1)}, u32[]{:S(2)}, u32[]{:S(2)}) collective-permute-start(bf16[256,8,256]{0,2,1:T(8,128)(2,1)} %get-tuple-element.9), channel_id=1, source_target_pairs={{0,2},{1,3},{2,0},{3,1},{4,6},{5,7},{6,4},{7,5},{8,10},{9,11},{10,... | collective-permute-start | bytes 3145736 | tf_op jit(solution)/shard_map/ppermute | solution.py:19
  114.8 3.0 fusion.21
  117.8 0.5 fusion.44
  118.3 0.5 copy-done.5
  118.7 1.8 copy.220
  120.6 3.1 rev.9
  123.7 2.7 bitcast_add_fusion
  126.4 31.0 %all-to-all-done = f32[4,4,4,8,8,256]{5,4,3,1,0,2:T(8,128)} async-done(((f32[4,4,4,8,8,256]{5,4,3,1,0,2:T(8,128)}), f32[4,4,4,8,8,256]{5,4,3,1,0,2:T(8,128)}, u32[]{:S(2)}, u32[]{:S(2)}) %all-to-all-start) | async-done | bytes 4194336 | tf_op jit(solution)/shard_map/all_to_all | solution.py:42
  157.4 3.6 %reduce_sum.46 = f32[4,4,8,8,256]{4,3,2,1,0:T(8,128)} reduce(f32[4,4,4,8,8,256]{5,4,3,1,0,2:T(8,128)} %all-to-all-done, f32[]{:T(128)} %constant.7.clone.1), dimensions={2}, to_apply=%region_1.2 | reduce | flops 786432 | bytes 5242884 | tf_op jit(solution)/shard_map/reduce_sum | solution.py:42
  161.0 2.6 multiply_bitcast_fusion.1
  163.6 4.4 %copy.227 = f32[512,8,256]{2,1,0:T(8,128)} copy(f32[512,8,256]{2,0,1:T(8,128)S(1)} %multiply_bitcast_fusion.1) | data formatting | bytes 8388608 | tf_op jit(solution)/shard_map/mul | solution.py:166
  168.0 2.3 copy.228
  170.4 4.5 %multiply_bitcast_fusion = f32[512,8,256]{0,2,1:T(8,128)} fusion(bf16[256,8,256]{0,2,1:T(8,128)(2,1)} %copy-done.5, bf16[256,8,256]{2,0,1:T(8,128)(2,1)} %bitcast.138, bf16[256,8,256]{2,0,1:T(8,128)(2,1)} %copy.228), kind=kOutput, calls=%fused_computation | convolution fusion | flops 542113792 | bytes 7340032 | tf_op jit(solution)/shard_map/tbc,tbd->cbd/dot_general | solution.py:141
  174.9 5.5 %copy.229 = f32[512,8,256]{2,1,0:T(8,128)} copy(f32[512,8,256]{0,2,1:T(8,128)} %multiply_bitcast_fusion) | data formatting | bytes 8388608 | tf_op jit(solution)/shard_map/mul | solution.py:141
  180.4 2.5 copy.230
  182.9 52.4 %all_to_all.15 = f32[4,4,4,8,8,256]{5,4,3,1,0,2:T(8,128)} all-to-all(f32[4,4,4,8,8,256]{5,4,3,1,0,2:T(8,128)S(1)} %copy.230), channel_id=1, replica_groups=mesh['dy'=4,'dz'=4,'dx'=4,'tensor'=4] {'dx'}, dimensions={2} | all-to-all | bytes 8388608 | tf_op jit(solution)/shard_map/all_to_all | solution.py:42
  235.3 3.6 %reduce_sum.48 = f32[4,4,8,8,256]{4,3,2,1,0:T(8,128)} reduce(f32[4,4,4,8,8,256]{5,4,3,1,0,2:T(8,128)} %all_to_all.15, f32[]{:T(128)} %constant.7.clone.1), dimensions={2}, to_apply=%region_4.5 | reduce | flops 786432 | bytes 5242884 | tf_op jit(solution)/shard_map/reduce_sum | solution.py:42
  238.9 3.1 pad_maximum_fusion
  242.0 2.3 copy.231
  244.3 4.5 %all-to-all-start.2 = ((f32[4,2,4,8,8,256]{5,4,3,2,1,0:T(8,128)}), f32[4,2,4,8,8,256]{5,4,3,2,1,0:T(8,128)}, u32[]{:S(2)}, u32[]{:S(2)}) async-start(f32[4,2,4,8,8,256]{5,4,3,2,1,0:T(8,128)} %bitcast.139), calls=%async_computation.3 | async-start | bytes 4194304 | tf_op jit(solution)/shard_map/all_to_all | solution.py:53
  248.8 0.3 fusion.3
  249.2 2.3 copy.225
  251.5 6.0 %collective-permute-start.8 = (f32[256]{0:T(256)S(1)}, f32[256]{0:T(256)S(1)}, u32[]{:S(2)}, u32[]{:S(2)}) collective-permute-start(f32[256]{0:T(256)S(1)} %add.101), channel_id=1, source_target_pairs={{0,2},{1,3},{2,0},{3,1},{4,6},{5,7},{6,4},{7,5},{8,10},{9,11},{10,... | collective-permute-start | bytes 3080 | tf_op jit(solution)/shard_map/ppermute | solution.py:19
  257.5 16.6 %all-to-all-done.2 = f32[4,2,4,8,8,256]{5,4,3,2,1,0:T(8,128)} async-done(((f32[4,2,4,8,8,256]{5,4,3,2,1,0:T(8,128)}), f32[4,2,4,8,8,256]{5,4,3,2,1,0:T(8,128)}, u32[]{:S(2)}, u32[]{:S(2)}) %all-to-all-start.2) | async-done | bytes 2097184 | tf_op jit(solution)/shard_map/all_to_all | solution.py:53
  274.2 2.6 reduce_sum.49
  276.8 1.2 maximum_bitcast_fusion
  278.0 0.9 copy.232
  279.0 2.1 fusion.39
  281.1 1.8 convolution_add_fusion
  282.9 1.9 fusion.7
  284.8 2.4 copy.233
  287.2 1.4 copy.234
  288.6 24.8 %reduce-scatter.8.cloned.1.call-done = f32[1,192,256]{2,1,0:T(8,128)} async-done(((f32[4,192,256]{2,1,0:T(8,128)}), f32[1,192,256]{2,1,0:T(8,128)}) %reduce-scatter.8.cloned.1.call-update) | async-done | bytes 196624 | tf_op jit(solution)/shard_map/reduce_scatter | solution.py:55
  (53 shorter events, 0.6 us)
Async XLA Ops:
  7.2 75.9 %all-gather.2.cloned.1.call-start = ((), (), s32[]{:S(2)}) async-start(), calls=%async_computation.6 | async-start | bytes 1114112 | tf_op jit(solution)/shard_map/all_gather | solution.py:65
  9.0 7.0 %collective-permute-start = (f32[256]{0:T(256)S(1)}, f32[256]{0:T(256)S(1)}, u32[]{:S(2)}, u32[]{:S(2)}) collective-permute-start(f32[256]{0:T(256)S(1)} %fusion.8), channel_id=1, source_target_pairs={{0,1},{1,0},{2,3},{3,2},{4,5},{5,4},{6,7},{7,6},{8,9},{9,8},{10,11... | collective-permute-start | bytes 3080 | tf_op jit(solution)/shard_map/ppermute | solution.py:19
  16.0 13.6 %copy-start.9 = (bf16[1,256,8,256]{1,3,2,0:T(8,128)(2,1)}, bf16[1,256,8,256]{1,3,2,0:T(8,128)(2,1)S(1)}, u32[]{:S(2)}) copy-start(bf16[1,256,8,256]{1,3,2,0:T(8,128)(2,1)S(1)} %copy.257) | copy-start | bytes 3145732
  16.0 13.6 %collective-permute-start.1 = (f32[256]{0:T(256)S(1)}, f32[256]{0:T(256)S(1)}, u32[]{:S(2)}, u32[]{:S(2)}) collective-permute-start(f32[256]{0:T(256)S(1)} %add.80), channel_id=1, source_target_pairs={{0,2},{1,3},{2,0},{3,1},{4,6},{5,7},{6,4},{7,5},{8,10},{9,11},{10,... | collective-permute-start | bytes 3080 | tf_op jit(solution)/shard_map/ppermute | solution.py:19
  25.5 8.9 %collective-permute-start.5 = (bf16[16,8,256]{2,0,1:T(8,128)(2,1)S(1)}, bf16[16,8,256]{2,0,1:T(8,128)(2,1)S(1)}, u32[]{:S(2)}, u32[]{:S(2)}) collective-permute-start(bf16[16,8,256]{2,0,1:T(8,128)(2,1)S(1)} %bitcast.147), channel_id=1, source_target_pairs={{0,2},{1,3},{2,0},{3,1},{4,6},{5,7},{6,4},{7,5},{8,10},{9,11},{10,... | collective-permute-start | bytes 196616 | tf_op jit(solution)/shard_map/ppermute | solution.py:19
  29.9 7.0 %copy-start = (bf16[256,2048]{0,1:T(8,128)(2,1)}, bf16[256,2048]{0,1:T(8,128)(2,1)S(1)}, u32[]{:S(2)}) copy-start(bf16[256,2048]{0,1:T(8,128)(2,1)S(1)} %fusion.2) | copy-start | bytes 3145732
  32.5 4.4 %copy-start.3 = (bf16[256,1,2,4,256]{4,0,3,2,1:T(8,128)(2,1)}, bf16[256,1,2,4,256]{4,0,3,2,1:T(8,128)(2,1)S(1)}, u32[]{:S(2)}) copy-start(bf16[256,1,2,4,256]{4,0,3,2,1:T(8,128)(2,1)S(1)} %rev.8) | copy-start | bytes 3145732
  34.4 0.6 copy-start.14
  35.0 1.8 copy-start.4
  36.9 2.3 copy-start.1
  39.2 10.6 %collective-permute-start.2 = (bf16[256,8,256]{0,2,1:T(8,128)(2,1)}, bf16[256,8,256]{0,2,1:T(8,128)(2,1)}, u32[]{:S(2)}, u32[]{:S(2)}) collective-permute-start(bf16[256,8,256]{0,2,1:T(8,128)(2,1)} %get-tuple-element.38), channel_id=1, source_target_pairs={{0,1},{1,0},{2,3},{3,2},{4,5},{5,4},{6,7},{7,6},{8,9},{9,8},{10,11... | collective-permute-start | bytes 3145736 | tf_op jit(solution)/shard_map/ppermute | solution.py:19
  40.2 37.5 %collective-permute-start.3 = (bf16[256,8,256]{2,0,1:T(8,128)(2,1)}, bf16[256,8,256]{2,0,1:T(8,128)(2,1)}, u32[]{:S(2)}, u32[]{:S(2)}) collective-permute-start(bf16[256,8,256]{2,0,1:T(8,128)(2,1)} %bitcast.127), channel_id=1, source_target_pairs={{0,2},{1,3},{2,0},{3,1},{4,6},{5,7},{6,4},{7,5},{8,10},{9,11},{10,... | collective-permute-start | bytes 3145736 | tf_op jit(solution)/shard_map/ppermute | solution.py:19
  45.9 1.9 copy-start.6
  46.0 2.0 copy-start.12
  48.0 1.8 copy-start.2
  88.9 25.9 %collective-permute-start.6 = (f32[256,8,256]{0,2,1:T(8,128)}, f32[256,8,256]{0,2,1:T(8,128)}, u32[]{:S(2)}, u32[]{:S(2)}) collective-permute-start(f32[256,8,256]{0,2,1:T(8,128)} %convolution_bitcast_fusion), channel_id=1, source_target_pairs={{0,1},{1,0},{2,3},{3,2},{4,5},{5,4},{6,7},{7,6},{8,9},{9,8},{10,11... | collective-permute-start | bytes 6291464 | tf_op jit(solution)/shard_map/ppermute | solution.py:19
  103.2 11.5 %copy-start.13 = (bf16[1,256,8,256]{3,2,1,0:T(8,128)(2,1)S(1)}, bf16[1,256,8,256]{3,2,1,0:T(8,128)(2,1)}, u32[]{:S(2)}) copy-start(bf16[1,256,8,256]{3,2,1,0:T(8,128)(2,1)} %get-tuple-element.31) | copy-start | bytes 3145732
  103.2 54.2 %all-to-all-start = ((f32[4,4,4,8,8,256]{5,4,3,1,0,2:T(8,128)}), f32[4,4,4,8,8,256]{5,4,3,1,0,2:T(8,128)}, u32[]{:S(2)}, u32[]{:S(2)}) async-start(f32[4,4,4,8,8,256]{5,4,3,1,0,2:T(8,128)} %copy.223), calls=%async_computation | async-start | bytes 8388608 | tf_op jit(solution)/shard_map/all_to_all | solution.py:42
  109.0 132.9 %reduce-scatter.4.cloned.1.call-start = ((), (), s32[]{:S(2)}) async-start(), calls=%async_computation.7 | async-start | bytes 5242880 | tf_op jit(solution)/shard_map/reduce_scatter | solution.py:33
  109.0 52.0 %collective-permute-start.4 = (bf16[256,8,256]{0,2,1:T(8,128)(2,1)}, bf16[256,8,256]{0,2,1:T(8,128)(2,1)}, u32[]{:S(2)}, u32[]{:S(2)}) collective-permute-start(bf16[256,8,256]{0,2,1:T(8,128)(2,1)} %get-tuple-element.9), channel_id=1, source_target_pairs={{0,2},{1,3},{2,0},{3,1},{4,6},{5,7},{6,4},{7,5},{8,10},{9,11},{10,... | collective-permute-start | bytes 3145736 | tf_op jit(solution)/shard_map/ppermute | solution.py:19
  114.8 3.0 copy-start.8
  117.8 1.0 copy-start.5
  168.0 108.8 %reduce-scatter.6.cloned.1.call-start = ((), (), s32[]{:S(2)}) async-start(), calls=%async_computation.8 | async-start | bytes 1310720 | tf_op jit(solution)/shard_map/reduce_scatter | solution.py:51
  244.3 29.9 %all-to-all-start.2 = ((f32[4,2,4,8,8,256]{5,4,3,2,1,0:T(8,128)}), f32[4,2,4,8,8,256]{5,4,3,2,1,0:T(8,128)}, u32[]{:S(2)}, u32[]{:S(2)}) async-start(f32[4,2,4,8,8,256]{5,4,3,2,1,0:T(8,128)} %bitcast.139), calls=%async_computation.3 | async-start | bytes 4194304 | tf_op jit(solution)/shard_map/all_to_all | solution.py:53
  248.7 64.6 %reduce-scatter.8.cloned.1.call-start = ((), (), s32[]{:S(2)}) async-start(), calls=%async_computation.9 | async-start | bytes 983040 | tf_op jit(solution)/shard_map/reduce_scatter | solution.py:55
  249.1 2.4 collective-permute-start.7
  251.5 27.5 %collective-permute-start.8 = (f32[256]{0:T(256)S(1)}, f32[256]{0:T(256)S(1)}, u32[]{:S(2)}, u32[]{:S(2)}) collective-permute-start(f32[256]{0:T(256)S(1)} %add.101), channel_id=1, source_target_pairs={{0,2},{1,3},{2,0},{3,1},{4,6},{5,7},{6,4},{7,5},{8,10},{9,11},{10,... | collective-permute-start | bytes 3080 | tf_op jit(solution)/shard_map/ppermute | solution.py:19
  279.0 2.1 copy-start.7
  281.1 1.8 copy-start.10
  284.8 2.4 copy-start.11
Sparse Core Ops, SparseCore 0:
  35.2 47.8 all-gather.1
  168.1 56.9 reduce-scatter.3
  244.4 31.5 reduce-scatter.5
  279.1 34.2 reduce-scatter.7

commit v8 on v6

--- a/solution.py
+++ b/solution.py
@@ -42,17 +42,18 @@
     return jnp.sum(lax.all_to_all(g, "dx", 2, 2), axis=2)
 
 
-def scatter_rest(on_sc, on_tc):
+def scatter_rest(on_sc, on_tc, order):
     nz, nx, share = on_sc[0].shape[:3]
     rest = on_sc[0].shape[3:]
-    a, on_tc = lax.optimization_barrier((jnp.stack(on_sc, axis=0), on_tc))
+    a, b = lax.optimization_barrier((jnp.stack(on_sc, axis=0), jnp.stack(on_tc, axis=0)))
     a = jnp.moveaxis(a, 2, 0)
     a = lax.psum_scatter(a.reshape(nx, -1, rest[-1]), "dx", scatter_dimension=0, tiled=True)
     a = a.reshape((len(on_sc), nz, share) + rest)
-    b = jnp.sum(lax.all_to_all(on_tc, "dy", 0, 0), axis=0)
-    g = jnp.moveaxis(jnp.concatenate([b[None], a], axis=0), 1, 0)
+    b = jnp.sum(lax.all_to_all(jnp.moveaxis(b, 1, 0), "dy", 0, 0), axis=0)
+    g = jnp.concatenate([b, a], axis=0)
+    g = jnp.moveaxis(jnp.stack([g[i] for i in order], axis=0), 1, 0)
     g = lax.psum_scatter(g.reshape(nz, -1, rest[-1]), "dz", scatter_dimension=0, tiled=True)
-    return g.reshape((len(on_sc) + 1, share) + rest)
+    return g.reshape((len(order), share) + rest)
 
 
 def partner_rows(rows):
@@ -159,7 +160,7 @@
     preact = apply_factor(hidden, partner_top, top_weights)
     mixed = (tokens_f32 + preact.reshape(tok_rows, local_width)).astype(jnp.bfloat16)
     joined = jnp.concatenate([hidden, partner_top], axis=2)
-    grad_terms[top] = scatter_first(
+    grad_terms[top] = exchange_first(
         jnp.einsum("tbc,tbd->cbd", joined, cot_blocks, preferred_element_type=jnp.float32)
         * grad_scale
     )
@@ -168,7 +169,9 @@
     token_grads = (
         cotangent.astype(jnp.float32) + inv_rms * (flat - normed * (inner_sum / D)[:, None])
     ).astype(jnp.bfloat16)
-    weight_grads = scatter_rest(grad_terms[1:], grad_terms[0])
+    weight_grads = scatter_rest(
+        grad_terms[1:top], [grad_terms[0], grad_terms[top]], [0] + list(range(2, top + 1)) + [1]
+    )
     return (mixed, token_grads, weight_grads)
 
 

time: 304 us -> 346 us (1.14)
  waiting for transfers between devices: 127 us -> 172 us
  blocking collectives: 30.7 us -> 0 us
  starting transfers between devices: 27.9 us -> 39.8 us
  local copies, waits for them, and re-layouts: 55.7 us -> 63.6 us
  other arithmetic: 10.5 us -> 16.9 us
    all_to_all x1 -> x3, waiting for transfers between devices: 12.7 us -> 93.1 us  [the longest x2 71 us: exchange_first(): return jnp.sum(lax.all_to_all(g, 'dx', 2, 2), axis=2)]
    all_to_all x1 -> x0, blocking collectives: 30.7 us -> none  [exchange_first(): return jnp.sum(lax.all_to_all(g, 'dx', 2, 2), axis=2)]
    ppermute x9, waiting for transfers between devices: 62.3 us -> 39 us  [swapped(): lax.ppermute(x, axis, [(i, i ^ 1 << stride) for i in range(lax.axis_size(...]
    reduce_scatter x1, waiting for transfers between devices: 31.2 us -> 9.8 us  [scatter_rest(): lax.psum_scatter(a.reshape(nx, -1, rest[-1]), 'dx', scatter_dimension=0,...]
    all_to_all x1 -> x3, starting transfers between devices: 4.25 us -> 16.4 us  [the longest x2 12 us: exchange_first(): return jnp.sum(lax.all_to_all(g, 'dx', 2, 2), axis=2)]
    reduce_scatter x1, waiting for transfers between devices: 15.3 us -> 25 us  [scatter_rest(): lax.psum_scatter(g.reshape(nz, -1, rest[-1]), 'dz', scatter_dimension=0,...]
    transpose x1 -> x3, local copies, waits for them, and re-layouts: 0.95 us -> 6.37 us  [the longest x1 3.12 us: scatter_rest(): b = jnp.sum(lax.all_to_all(jnp.moveaxis(b, 1, 0), 'dy', 0, 0), axis=0)]
    reshape x1 -> x2, local copies, waits for them, and re-layouts: 2.64 us -> 7.26 us  [exchange_first(): g = grads.reshape((ny, nz, nx, rows // (ny * nz * nx)) + rest)]
  transfers between devices with their start and end apart: 15 -> 16, of which waited for: 9 -> 10; matrix products, arithmetic and copies ran while one was open for 27% -> 31% of each run, Pallas kernels for 0% -> 0%
where the time goes in v8:
time: 346 us; the launch traced here: 345 us
  waiting for transfers between devices  172 us (50%)
  local copies, waits for them, and re-layouts  63.6 us (18%)
  starting transfers between devices  39.8 us (12%)
  matrix products  38.3 us (11%)
  other arithmetic  16.9 us (5%)
  between operations  14.1 us (4%)
    all_to_all x2, waiting for transfers between devices, exchange_first(): return jnp.sum(lax.all_to_all(g, 'dx', 2, 2), axis=2)  71 us
    ppermute x9, waiting for transfers between devices, swapped(): lax.ppermute(x, axis, [(i, i ^ 1 << stride) for i in range(lax.axis_size(...  39 us
    reduce_scatter x1, waiting for transfers between devices, scatter_rest(): lax.psum_scatter(g.reshape(nz, -1, rest[-1]), 'dz', scatter_dimension=0,...  25 us
    ppermute x9, starting transfers between devices, swapped(): lax.ppermute(x, axis, [(i, i ^ 1 << stride) for i in range(lax.axis_size(...  23.3 us
    all_to_all x1, waiting for transfers between devices, scatter_rest(): b = jnp.sum(lax.all_to_all(jnp.moveaxis(b, 1, 0), 'dy', 0, 0), axis=0)  22 us
    unnamed x40, local copies, waits for them, and re-layouts  16.1 us
    all_to_all x2, starting transfers between devices, exchange_first(): return jnp.sum(lax.all_to_all(g, 'dx', 2, 2), axis=2)  12 us
    mul x2, local copies, waits for them, and re-layouts, shards(): jnp.einsum('tbc,tbd->cbd', joined, grad_pre, preferred_element_type=jnp.f...  10.9 us
  transfers between devices with their start and end apart: 16, of which 10 were waited for; matrix products, arithmetic and copies ran while one was open for 31% of the time, Pallas kernels for 0%

profile of v8, /device:TPU:2, one launch (start us, length us, event | category | flops | bytes accessed | tf_op | source)
XLA Modules:
  0.0 344.8 jit_solution(3713301393269863243)
XLA Ops:
  7.2 1.5 copy.190
  9.1 5.2 %fusion.54 = (bf16[1,256,8,256]{3,2,1,0:T(8,128)(2,1)}, bf16[1,256,8,256]{3,2,1,0:T(8,128)(2,1)}, bf16[1,256,8,256]{3,2,1,0:T(8,128)(2,1)}, bf16[1,256,8,256]{3,...) fusion(bf16[3,512,8,256]{3,2,1,0:T(8,128)(2,1)} %param.4), kind=kLoop, calls=%fused_computation.81 | loop fusion | bytes 12582912 | tf_op jit(solution)/shard_map/slice | solution.py:89
  14.3 1.6 copy.256
  16.0 7.3 %collective-permute-start.1 = (f32[256]{0:T(256)S(1)}, f32[256]{0:T(256)S(1)}, u32[]{:S(2)}, u32[]{:S(2)}) collective-permute-start(f32[256]{0:T(256)S(1)} %add.80), channel_id=1, source_target_pairs={{0,2},{1,3},{2,0},{3,1},{4,6},{5,7},{6,4},{7,5},{8,10},{9,11},{10,... | collective-permute-start | bytes 3080 | tf_op jit(solution)/shard_map/ppermute | solution.py:19
  23.3 1.0 constant_dynamic-slice_fusion
  24.3 1.2 copy.207
  25.6 2.4 copy.252
  28.0 1.6 copy.251
  29.8 1.3 copy.193
  31.2 1.3 rev.8
  32.5 1.9 collective-permute-done.5
  34.4 0.6 copy-done.15
  35.1 1.8 fusion.46
  36.9 2.3 fusion.38
  39.2 1.1 copy.270
  40.3 4.1 %collective-permute-start.3 = (bf16[256,8,256]{2,0,1:T(8,128)(2,1)}, bf16[256,8,256]{2,0,1:T(8,128)(2,1)}, u32[]{:S(2)}, u32[]{:S(2)}) collective-permute-start(bf16[256,8,256]{2,0,1:T(8,128)(2,1)} %bitcast.128), channel_id=1, source_target_pairs={{0,2},{1,3},{2,0},{3,1},{4,6},{5,7},{6,4},{7,5},{8,10},{9,11},{10,... | collective-permute-start | bytes 3145736 | tf_op jit(solution)/shard_map/ppermute | solution.py:19
  44.4 1.6 copy.255
  46.0 1.8 fusion.41
  48.1 1.8 fusion.50
  49.9 3.7 %fusion.34 = (bf16[256,8,256]{0,2,1:T(8,128)(2,1)}, f32[8,256,256]{1,2,0:T(8,128)}) fusion(f32[8,256,256]{1,2,0:T(8,128)S(1)} %fusion.50, bf16[256,8,256]{0,2,1:T(8,128)(2,1)} %collective-permute-done.2, bf16[1,256,8,256]{3,2,1,0:T(8,128)(2,1)S(1)} %copy-done.3), kind=kOutput, calls=%fused_computation.47 | convolution fusion | flops 271581184 | bytes 7340032 | tf_op jit(solution)/shard_map/tbc,cbd->tbd/dot_general | solution.py:88
  53.6 24.3 %collective-permute-done.3 = bf16[256,8,256]{2,0,1:T(8,128)(2,1)} collective-permute-done((bf16[256,8,256]{2,0,1:T(8,128)(2,1)}, bf16[256,8,256]{2,0,1:T(8,128)(2,1)}, u32[]{:S(2)}, u32[]{:S(2)}) %collective-permute-start.3) | collective-permute-done | bytes 1048608 | tf_op jit(solution)/shard_map/ppermute | solution.py:19
  77.8 5.2 %all-gather.2.cloned.1.call-done = bf16[256,8,256]{2,0,1:T(8,128)(2,1)} async-done(((bf16[16,8,256]{2,0,1:T(8,128)(2,1)}), bf16[256,8,256]{2,0,1:T(8,128)(2,1)}) %all-gather.2.cloned.1.call-update) | async-done | bytes 1048592 | tf_op jit(solution)/shard_map/all_gather | solution.py:65
  83.1 4.0 %fusion.15 = bf16[256,8,256]{0,2,1:T(8,128)(2,1)S(1)} fusion(f32[8,256,256]{1,2,0:T(8,128)} %get-tuple-element.41, f32[8,256,256]{2,1,0:T(8,128)} %fusion.41, bf16[256,8,256]{2,0,1:T(8,128)(2,1)} %all-gather.2.cloned.1.call-done, bf16[256,8,256]{2,0,1:T(8,128)(2,1)} %collective-permute-done.3), kind=kOutput, calls=%fused_computation.23 | convolution fusion | flops 274202624 | bytes 7340032 | tf_op jit(solution)/shard_map/tbd,cbd->tbc/dot_general | solution.py:127
  87.0 1.8 convolution_bitcast_fusion
  88.8 4.3 %multiply_bitcast_fusion.1 = f32[512,8,256]{0,2,1:T(8,128)} fusion(bf16[256,8,256]{0,2,1:T(8,128)(2,1)S(1)} %fusion.15, bf16[256,8,256]{0,2,1:T(8,128)(2,1)} %collective-permute-done.2, bf16[256,8,256]{0,2,1:T(8,128)(2,1)} %get-tuple-element.38), kind=kOutput, calls=%fused_computation.1 | convolution fusion | flops 542113792 | bytes 7340032 | tf_op jit(solution)/shard_map/tbc,tbd->cbd/dot_general | solution.py:141
  93.1 5.4 %copy.220 = f32[512,8,256]{2,1,0:T(8,128)} copy(f32[512,8,256]{0,2,1:T(8,128)} %multiply_bitcast_fusion.1) | data formatting | bytes 8388608 | tf_op jit(solution)/shard_map/mul | solution.py:141
  98.6 5.8 %collective-permute-start.4 = (bf16[256,8,256]{0,2,1:T(8,128)(2,1)}, bf16[256,8,256]{0,2,1:T(8,128)(2,1)}, u32[]{:S(2)}, u32[]{:S(2)}) collective-permute-start(bf16[256,8,256]{0,2,1:T(8,128)(2,1)} %get-tuple-element.8), channel_id=1, source_target_pairs={{0,2},{1,3},{2,0},{3,1},{4,6},{5,7},{6,4},{7,5},{8,10},{9,11},{10,... | collective-permute-start | bytes 3145736 | tf_op jit(solution)/shard_map/ppermute | solution.py:19
  104.4 3.0 fusion.21
  107.4 0.5 fusion.44
  108.4 1.9 copy.216
  110.3 3.1 rev.9
  113.3 2.8 bitcast_add_fusion
  116.1 12.7 %collective-permute-done.4 = bf16[256,8,256]{0,2,1:T(8,128)(2,1)} collective-permute-done((bf16[256,8,256]{0,2,1:T(8,128)(2,1)}, bf16[256,8,256]{0,2,1:T(8,128)(2,1)}, u32[]{:S(2)}, u32[]{:S(2)}) %collective-permute-start.4) | collective-permute-done | bytes 1048608 | tf_op jit(solution)/shard_map/ppermute | solution.py:19
  128.9 2.3 convolution_multiply_fusion
  131.2 2.6 copy.225
  133.8 5.6 %all-to-all-start.1 = ((f32[4,4,4,8,8,256]{5,3,1,0,4,2:T(8,128)}), f32[4,4,4,8,8,256]{5,3,1,0,4,2:T(8,128)}, u32[]{:S(2)}, u32[]{:S(2)}) async-start(f32[4,4,4,8,8,256]{5,3,1,0,4,2:T(8,128)} %copy.225), calls=%async_computation.2 | async-start | bytes 8388608 | tf_op jit(solution)/shard_map/all_to_all | solution.py:42
  139.4 2.3 copy.221
  141.7 4.5 %multiply_bitcast_fusion = f32[512,8,256]{0,2,1:T(8,128)} fusion(bf16[256,8,256]{0,2,1:T(8,128)(2,1)} %copy-done.6, bf16[256,8,256]{2,0,1:T(8,128)(2,1)} %bitcast.140, bf16[256,8,256]{2,0,1:T(8,128)(2,1)} %copy.221), kind=kOutput, calls=%fused_computation | convolution fusion | flops 542113792 | bytes 7340032 | tf_op jit(solution)/shard_map/tbc,tbd->cbd/dot_general | solution.py:141
  146.2 5.5 %copy.222 = f32[512,8,256]{2,1,0:T(8,128)} copy(f32[512,8,256]{0,2,1:T(8,128)} %multiply_bitcast_fusion) | data formatting | bytes 8388608 | tf_op jit(solution)/shard_map/mul | solution.py:141
  151.7 4.6 %copy.223 = f32[4,4,4,8,8,256]{5,4,3,1,0,2:T(8,128)} copy(f32[4,4,4,8,8,256]{5,4,3,2,1,0:T(8,128)} %bitcast.135) | data formatting | bytes 8388608 | tf_op jit(solution)/shard_map/reshape | solution.py:41
  156.3 30.8 %all-to-all-done.1 = f32[4,4,4,8,8,256]{5,3,1,0,4,2:T(8,128)} async-done(((f32[4,4,4,8,8,256]{5,3,1,0,4,2:T(8,128)}), f32[4,4,4,8,8,256]{5,3,1,0,4,2:T(8,128)}, u32[]{:S(2)}, u32[]{:S(2)}) %all-to-all-start.1) | async-done | bytes 4194336 | tf_op jit(solution)/shard_map/all_to_all | solution.py:42
  187.1 6.3 %all-to-all-start = ((f32[4,4,4,8,8,256]{5,4,3,1,0,2:T(8,128)}), f32[4,4,4,8,8,256]{5,4,3,1,0,2:T(8,128)}, u32[]{:S(2)}, u32[]{:S(2)}) async-start(f32[4,4,4,8,8,256]{5,4,3,1,0,2:T(8,128)} %copy.223), calls=%async_computation.1 | async-start | bytes 8388608 | tf_op jit(solution)/shard_map/all_to_all | solution.py:42
  193.4 3.7 %reduce_sum.48 = f32[4,4,8,8,256]{4,2,1,0,3:T(8,128)} reduce(f32[4,4,4,8,8,256]{5,3,1,0,4,2:T(8,128)} %all-to-all-done.1, f32[]{:T(128)} %constant.7.clone.1), dimensions={2}, to_apply=%region_4.5 | reduce | flops 786432 | bytes 5242884 | tf_op jit(solution)/shard_map/reduce_sum | solution.py:42
  197.1 2.8 copy.271
  199.9 40.3 %all-to-all-done = f32[4,4,4,8,8,256]{5,4,3,1,0,2:T(8,128)} async-done(((f32[4,4,4,8,8,256]{5,4,3,1,0,2:T(8,128)}), f32[4,4,4,8,8,256]{5,4,3,1,0,2:T(8,128)}, u32[]{:S(2)}, u32[]{:S(2)}) %all-to-all-start) | async-done | bytes 4194336 | tf_op jit(solution)/shard_map/all_to_all | solution.py:42
  240.2 3.6 %reduce_sum.47 = f32[4,4,8,8,256]{4,3,2,1,0:T(8,128)} reduce(f32[4,4,4,8,8,256]{5,4,3,1,0,2:T(8,128)} %all-to-all-done, f32[]{:T(128)} %constant.7.clone.1), dimensions={2}, to_apply=%region_3.4 | reduce | flops 786432 | bytes 5242884 | tf_op jit(solution)/shard_map/reduce_sum | solution.py:42
  243.8 3.1 pad_maximum_fusion
  246.9 2.3 copy.229
  249.2 3.1 copy.228
  252.3 4.5 %all-to-all-start.2 = ((f32[4,2,4,8,8,256]{5,4,3,2,1,0:T(8,128)}), f32[4,2,4,8,8,256]{5,4,3,2,1,0:T(8,128)}, u32[]{:S(2)}, u32[]{:S(2)}) async-start(f32[4,2,4,8,8,256]{5,4,3,2,1,0:T(8,128)} %copy.228), calls=%async_computation.3 | async-start | bytes 4194304 | tf_op jit(solution)/shard_map/all_to_all | solution.py:52
  256.8 2.3 copy.218
  259.5 22.0 %all-to-all-done.2 = f32[4,2,4,8,8,256]{5,4,3,2,1,0:T(8,128)} async-done(((f32[4,2,4,8,8,256]{5,4,3,2,1,0:T(8,128)}), f32[4,2,4,8,8,256]{5,4,3,2,1,0:T(8,128)}, u32[]{:S(2)}, u32[]{:S(2)}) %all-to-all-start.2) | async-done | bytes 2097184 | tf_op jit(solution)/shard_map/all_to_all | solution.py:52
  281.6 2.6 reduce_sum.49
  284.2 1.8 fusion.55
  286.0 9.8 %reduce-scatter.6.cloned.1.call-done = f32[1,256,256]{2,1,0:T(8,128)} async-done(((f32[4,256,256]{2,1,0:T(8,128)}), f32[1,256,256]{2,1,0:T(8,128)}) %reduce-scatter.6.cloned.1.call-update) | async-done | bytes 262160 | tf_op jit(solution)/shard_map/reduce_scatter | solution.py:50
  295.8 1.1 maximum_bitcast_fusion
  296.9 1.0 copy.230
  297.9 2.1 fusion.39
  300.0 5.8 %collective-permute-start.8 = (f32[256]{0:T(256)S(1)}, f32[256]{0:T(256)S(1)}, u32[]{:S(2)}, u32[]{:S(2)}) collective-permute-start(f32[256]{0:T(256)S(1)} %add.101), channel_id=1, source_target_pairs={{0,2},{1,3},{2,0},{3,1},{4,6},{5,7},{6,4},{7,5},{8,10},{9,11},{10,... | collective-permute-start | bytes 3080 | tf_op jit(solution)/shard_map/ppermute | solution.py:19
  305.8 1.7 convolution_add_fusion
  307.6 1.9 fusion.7
  309.5 2.4 copy.231
  311.8 1.4 copy.232
  313.2 25.0 %reduce-scatter.8.cloned.1.call-done = f32[1,192,256]{2,1,0:T(8,128)} async-done(((f32[4,192,256]{2,1,0:T(8,128)}), f32[1,192,256]{2,1,0:T(8,128)}) %reduce-scatter.8.cloned.1.call-update) | async-done | bytes 196624 | tf_op jit(solution)/shard_map/reduce_scatter | solution.py:55
  (58 shorter events, 2.2 us)
Async XLA Ops:
  7.2 75.9 %all-gather.2.cloned.1.call-start = ((), (), s32[]{:S(2)}) async-start(), calls=%async_computation.6 | async-start | bytes 1114112 | tf_op jit(solution)/shard_map/all_gather | solution.py:65
  9.0 7.0 %collective-permute-start = (f32[256]{0:T(256)S(1)}, f32[256]{0:T(256)S(1)}, u32[]{:S(2)}, u32[]{:S(2)}) collective-permute-start(f32[256]{0:T(256)S(1)} %fusion.8), channel_id=1, source_target_pairs={{0,1},{1,0},{2,3},{3,2},{4,5},{5,4},{6,7},{7,6},{8,9},{9,8},{10,11... | collective-permute-start | bytes 3080 | tf_op jit(solution)/shard_map/ppermute | solution.py:19
  16.0 13.6 %copy-start.10 = (bf16[1,256,8,256]{1,3,2,0:T(8,128)(2,1)}, bf16[1,256,8,256]{1,3,2,0:T(8,128)(2,1)S(1)}, u32[]{:S(2)}) copy-start(bf16[1,256,8,256]{1,3,2,0:T(8,128)(2,1)S(1)} %copy.256) | copy-start | bytes 3145732
  16.0 13.6 %collective-permute-start.1 = (f32[256]{0:T(256)S(1)}, f32[256]{0:T(256)S(1)}, u32[]{:S(2)}, u32[]{:S(2)}) collective-permute-start(f32[256]{0:T(256)S(1)} %add.80), channel_id=1, source_target_pairs={{0,2},{1,3},{2,0},{3,1},{4,6},{5,7},{6,4},{7,5},{8,10},{9,11},{10,... | collective-permute-start | bytes 3080 | tf_op jit(solution)/shard_map/ppermute | solution.py:19
  25.5 8.9 %collective-permute-start.5 = (bf16[16,8,256]{2,0,1:T(8,128)(2,1)S(1)}, bf16[16,8,256]{2,0,1:T(8,128)(2,1)S(1)}, u32[]{:S(2)}, u32[]{:S(2)}) collective-permute-start(bf16[16,8,256]{2,0,1:T(8,128)(2,1)S(1)} %bitcast.149), channel_id=1, source_target_pairs={{0,2},{1,3},{2,0},{3,1},{4,6},{5,7},{6,4},{7,5},{8,10},{9,11},{10,... | collective-permute-start | bytes 196616 | tf_op jit(solution)/shard_map/ppermute | solution.py:19
  29.8 7.0 %copy-start = (bf16[256,2048]{0,1:T(8,128)(2,1)}, bf16[256,2048]{0,1:T(8,128)(2,1)S(1)}, u32[]{:S(2)}) copy-start(bf16[256,2048]{0,1:T(8,128)(2,1)S(1)} %fusion.2) | copy-start | bytes 3145732
  32.5 4.4 %copy-start.4 = (bf16[256,1,2,4,256]{4,0,3,2,1:T(8,128)(2,1)}, bf16[256,1,2,4,256]{4,0,3,2,1:T(8,128)(2,1)S(1)}, u32[]{:S(2)}) copy-start(bf16[256,1,2,4,256]{4,0,3,2,1:T(8,128)(2,1)S(1)} %rev.8) | copy-start | bytes 3145732
  34.4 0.6 copy-start.15
  35.0 211.8 %reduce-scatter.4.cloned.1.call-start = ((), (), s32[]{:S(2)}) async-start(), calls=%async_computation.7 | async-start | bytes 5242880 | tf_op jit(solution)/shard_map/reduce_scatter | solution.py:33
  35.1 1.8 copy-start.5
  36.9 2.3 copy-start.1
  39.2 10.7 %collective-permute-start.2 = (bf16[256,8,256]{0,2,1:T(8,128)(2,1)}, bf16[256,8,256]{0,2,1:T(8,128)(2,1)}, u32[]{:S(2)}, u32[]{:S(2)}) collective-permute-start(bf16[256,8,256]{0,2,1:T(8,128)(2,1)} %get-tuple-element.38), channel_id=1, source_target_pairs={{0,1},{1,0},{2,3},{3,2},{4,5},{5,4},{6,7},{7,6},{8,9},{9,8},{10,11... | collective-permute-start | bytes 3145736 | tf_op jit(solution)/shard_map/ppermute | solution.py:19
  40.3 37.6 %collective-permute-start.3 = (bf16[256,8,256]{2,0,1:T(8,128)(2,1)}, bf16[256,8,256]{2,0,1:T(8,128)(2,1)}, u32[]{:S(2)}, u32[]{:S(2)}) collective-permute-start(bf16[256,8,256]{2,0,1:T(8,128)(2,1)} %bitcast.128), channel_id=1, source_target_pairs={{0,2},{1,3},{2,0},{3,1},{4,6},{5,7},{6,4},{7,5},{8,10},{9,11},{10,... | collective-permute-start | bytes 3145736 | tf_op jit(solution)/shard_map/ppermute | solution.py:19
  46.0 1.8 copy-start.7
  46.0 2.0 copy-start.13
  48.1 1.8 copy-start.3
  88.8 15.6 %collective-permute-start.6 = (f32[256,8,256]{0,2,1:T(8,128)}, f32[256,8,256]{0,2,1:T(8,128)}, u32[]{:S(2)}, u32[]{:S(2)}) collective-permute-start(f32[256,8,256]{0,2,1:T(8,128)} %convolution_bitcast_fusion), channel_id=1, source_target_pairs={{0,1},{1,0},{2,3},{3,2},{4,5},{5,4},{6,7},{7,6},{8,9},{9,8},{10,11... | collective-permute-start | bytes 6291464 | tf_op jit(solution)/shard_map/ppermute | solution.py:19
  98.5 5.9 %copy-start.14 = (bf16[1,256,8,256]{3,2,1,0:T(8,128)(2,1)S(1)}, bf16[1,256,8,256]{3,2,1,0:T(8,128)(2,1)}, u32[]{:S(2)}) copy-start(bf16[1,256,8,256]{3,2,1,0:T(8,128)(2,1)} %get-tuple-element.30) | copy-start | bytes 3145732
  98.6 30.3 %collective-permute-start.4 = (bf16[256,8,256]{0,2,1:T(8,128)(2,1)}, bf16[256,8,256]{0,2,1:T(8,128)(2,1)}, u32[]{:S(2)}, u32[]{:S(2)}) collective-permute-start(bf16[256,8,256]{0,2,1:T(8,128)(2,1)} %get-tuple-element.8), channel_id=1, source_target_pairs={{0,2},{1,3},{2,0},{3,1},{4,6},{5,7},{6,4},{7,5},{8,10},{9,11},{10,... | collective-permute-start | bytes 3145736 | tf_op jit(solution)/shard_map/ppermute | solution.py:19
  104.4 3.0 copy-start.9
  107.4 1.0 copy-start.6
  113.3 15.5 %copy-start.2 = (bf16[256,2048]{1,0:T(8,128)(2,1)S(1)}, bf16[256,2048]{1,0:T(8,128)(2,1)}, u32[]{:S(2)}) copy-start(bf16[256,2048]{1,0:T(8,128)(2,1)} %param.5) | copy-start | bytes 3145732
  133.8 53.3 %all-to-all-start.1 = ((f32[4,4,4,8,8,256]{5,3,1,0,4,2:T(8,128)}), f32[4,4,4,8,8,256]{5,3,1,0,4,2:T(8,128)}, u32[]{:S(2)}, u32[]{:S(2)}) async-start(f32[4,4,4,8,8,256]{5,3,1,0,4,2:T(8,128)} %copy.225), calls=%async_computation.2 | async-start | bytes 8388608 | tf_op jit(solution)/shard_map/all_to_all | solution.py:42
  187.1 53.1 %all-to-all-start = ((f32[4,4,4,8,8,256]{5,4,3,1,0,2:T(8,128)}), f32[4,4,4,8,8,256]{5,4,3,1,0,2:T(8,128)}, u32[]{:S(2)}, u32[]{:S(2)}) async-start(f32[4,4,4,8,8,256]{5,4,3,1,0,2:T(8,128)} %copy.223), calls=%async_computation.1 | async-start | bytes 8388608 | tf_op jit(solution)/shard_map/all_to_all | solution.py:42
  193.4 102.4 %reduce-scatter.6.cloned.1.call-start = ((), (), s32[]{:S(2)}) async-start(), calls=%async_computation.8 | async-start | bytes 1310720 | tf_op jit(solution)/shard_map/reduce_scatter | solution.py:50
  252.3 29.3 %all-to-all-start.2 = ((f32[4,2,4,8,8,256]{5,4,3,2,1,0:T(8,128)}), f32[4,2,4,8,8,256]{5,4,3,2,1,0:T(8,128)}, u32[]{:S(2)}, u32[]{:S(2)}) async-start(f32[4,2,4,8,8,256]{5,4,3,2,1,0:T(8,128)} %copy.228), calls=%async_computation.3 | async-start | bytes 4194304 | tf_op jit(solution)/shard_map/all_to_all | solution.py:52
  256.8 81.5 %reduce-scatter.8.cloned.1.call-start = ((), (), s32[]{:S(2)}) async-start(), calls=%async_computation.9 | async-start | bytes 983040 | tf_op jit(solution)/shard_map/reduce_scatter | solution.py:55
  259.4 40.5 %collective-permute-start.7 = (f32[256]{0:T(256)S(1)}, f32[256]{0:T(256)S(1)}, u32[]{:S(2)}, u32[]{:S(2)}) collective-permute-start(f32[256]{0:T(256)S(1)} %fusion.3), channel_id=1, source_target_pairs={{0,1},{1,0},{2,3},{3,2},{4,5},{5,4},{6,7},{7,6},{8,9},{9,8},{10,11... | collective-permute-start | bytes 3080 | tf_op jit(solution)/shard_map/ppermute | solution.py:19
  297.9 7.9 %copy-start.8 = (bf16[1,256,8,256]{1,3,2,0:T(8,128)(2,1)S(1)}, bf16[1,256,8,256]{1,3,2,0:T(8,128)(2,1)}, u32[]{:S(2)}) copy-start(bf16[1,256,8,256]{1,3,2,0:T(8,128)(2,1)} %copy-done.7) | copy-start | bytes 3145732
  300.0 7.6 %copy-start.11 = (bf16[256,2048]{0,1:T(8,128)(2,1)S(1)}, bf16[256,2048]{0,1:T(8,128)(2,1)}, u32[]{:S(2)}) copy-start(bf16[256,2048]{0,1:T(8,128)(2,1)} %copy.218) | copy-start | bytes 3145732
  300.0 7.6 %collective-permute-start.8 = (f32[256]{0:T(256)S(1)}, f32[256]{0:T(256)S(1)}, u32[]{:S(2)}, u32[]{:S(2)}) collective-permute-start(f32[256]{0:T(256)S(1)} %add.101), channel_id=1, source_target_pairs={{0,2},{1,3},{2,0},{3,1},{4,6},{5,7},{6,4},{7,5},{8,10},{9,11},{10,... | collective-permute-start | bytes 3080 | tf_op jit(solution)/shard_map/ppermute | solution.py:19
  309.5 2.4 copy-start.12
Sparse Core Ops, SparseCore 0:
  35.1 47.8 all-gather.1
  98.7 58.4 reduce-scatter.3
  249.3 46.4 reduce-scatter.5
  298.8 39.4 reduce-scatter.7

commit v9 on v6

--- a/solution.py
+++ b/solution.py
@@ -51,8 +51,7 @@
     a = a.reshape((len(on_sc), nz, share) + rest)
     b = jnp.sum(lax.all_to_all(on_tc, "dy", 0, 0), axis=0)
     g = jnp.moveaxis(jnp.concatenate([b[None], a], axis=0), 1, 0)
-    g = lax.psum_scatter(g.reshape(nz, -1, rest[-1]), "dz", scatter_dimension=0, tiled=True)
-    return g.reshape((len(on_sc) + 1, share) + rest)
+    return jnp.sum(lax.all_to_all(g, "dz", 0, 0), axis=0)
 
 
 def partner_rows(rows):

time: 304 us -> 302 us (level)
  waiting for transfers between devices: 127 us -> 114 us
  starting transfers between devices: 27.9 us -> 32.7 us
    reduce_scatter x1 -> x0, waiting for transfers between devices: 15.3 us -> none  [scatter_rest(): lax.psum_scatter(g.reshape(nz, -1, rest[-1]), 'dz', scatter_dimension=0,...]
    all_to_all x0 -> x1, waiting for transfers between devices: none -> 11.8 us  [scatter_rest(): return jnp.sum(lax.all_to_all(g, 'dz', 0, 0), axis=0)]
    all_to_all x1, waiting for transfers between devices: 12.7 us -> 3.27 us  [scatter_rest(): b = jnp.sum(lax.all_to_all(on_tc, 'dy', 0, 0), axis=0)]
    all_to_all x0 -> x1, starting transfers between devices: none -> 4.8 us  [scatter_rest(): return jnp.sum(lax.all_to_all(g, 'dz', 0, 0), axis=0)]
  transfers between devices with their start and end apart: 15 -> 15, of which waited for: 9 -> 8; matrix products, arithmetic and copies ran while one was open for 27% -> 28% of each run, Pallas kernels for 0% -> 0%
where the time goes in v9:
time: 302 us; the launch traced here: 299 us
  waiting for transfers between devices  114 us (38%)
  local copies, waits for them, and re-layouts  55.6 us (18%)
  matrix products  38.7 us (13%)
  starting transfers between devices  32.7 us (11%)
  blocking collectives  30.7 us (10%)
  between operations  14.1 us (5%)
  other arithmetic  13.3 us (4%)
    ppermute x9, waiting for transfers between devices, swapped(): lax.ppermute(x, axis, [(i, i ^ 1 << stride) for i in range(lax.axis_size(...  61.9 us
    reduce_scatter x1, waiting for transfers between devices, scatter_rest(): lax.psum_scatter(a.reshape(nx, -1, rest[-1]), 'dx', scatter_dimension=0,...  31.2 us
    all_to_all x1, blocking collectives, exchange_first(): return jnp.sum(lax.all_to_all(g, 'dx', 2, 2), axis=2)  30.7 us
    ppermute x9, starting transfers between devices, swapped(): lax.ppermute(x, axis, [(i, i ^ 1 << stride) for i in range(lax.axis_size(...  23.5 us
    unnamed x46, local copies, waits for them, and re-layouts  17.9 us
    all_to_all x1, waiting for transfers between devices, scatter_rest(): return jnp.sum(lax.all_to_all(g, 'dz', 0, 0), axis=0)  11.8 us
    mul x2, local copies, waits for them, and re-layouts, shards(): jnp.einsum('tbc,tbd->cbd', joined, grad_pre, preferred_element_type=jnp.f...  10.9 us
    dot_general x2, matrix products, shards(): jnp.einsum('tbc,tbd->cbd', joined, grad_pre, preferred_element_type=jnp.f...  8.84 us
  transfers between devices with their start and end apart: 15, of which 8 were waited for; matrix products, arithmetic and copies ran while one was open for 28% of the time, Pallas kernels for 0%

profile of v9, /device:TPU:2, one launch (start us, length us, event | category | flops | bytes accessed | tf_op | source)
XLA Modules:
  0.0 299.2 jit_solution(10783310645281897651)
XLA Ops:
  7.2 1.5 copy.117
  8.7 0.3 fusion.8
  9.1 5.2 %fusion.54 = (bf16[1,256,8,256]{3,2,1,0:T(8,128)(2,1)}, bf16[1,256,8,256]{3,2,1,0:T(8,128)(2,1)}, bf16[1,256,8,256]{3,2,1,0:T(8,128)(2,1)}, bf16[1,256,8,256]{3,...) fusion(bf16[3,512,8,256]{3,2,1,0:T(8,128)(2,1)} %param.4), kind=kLoop, calls=%fused_computation.80 | loop fusion | bytes 12582912 | tf_op jit(solution)/shard_map/slice | solution.py:87
  14.3 1.6 copy.182
  16.0 7.3 %collective-permute-start.1 = (f32[256]{0:T(256)S(1)}, f32[256]{0:T(256)S(1)}, u32[]{:S(2)}, u32[]{:S(2)}) collective-permute-start(f32[256]{0:T(256)S(1)} %add.80), channel_id=1, source_target_pairs={{0,2},{1,3},{2,0},{3,1},{4,6},{5,7},{6,4},{7,5},{8,10},{9,11},{10,... | collective-permute-start | bytes 3080 | tf_op jit(solution)/shard_map/ppermute | solution.py:19
  23.3 1.0 constant_dynamic-slice_fusion
  24.3 1.2 copy.134
  25.6 2.4 copy.179
  28.0 1.6 copy.178
  29.9 1.3 copy.120
  31.2 1.3 rev.8
  32.5 1.9 collective-permute-done.5
  34.4 0.6 copy-done.18
  35.1 1.8 fusion.46
  36.9 2.3 fusion.38
  39.2 1.0 copy.197
  40.3 4.1 %collective-permute-start.3 = (bf16[256,8,256]{2,0,1:T(8,128)(2,1)}, bf16[256,8,256]{2,0,1:T(8,128)(2,1)}, u32[]{:S(2)}, u32[]{:S(2)}) collective-permute-start(bf16[256,8,256]{2,0,1:T(8,128)(2,1)} %bitcast.127), channel_id=1, source_target_pairs={{0,2},{1,3},{2,0},{3,1},{4,6},{5,7},{6,4},{7,5},{8,10},{9,11},{10,... | collective-permute-start | bytes 3145736 | tf_op jit(solution)/shard_map/ppermute | solution.py:19
  44.4 1.6 copy.177
  46.1 1.8 fusion.41
  48.1 1.8 fusion.50
  49.9 3.7 %fusion.34 = (bf16[256,8,256]{0,2,1:T(8,128)(2,1)}, f32[8,256,256]{1,2,0:T(8,128)}) fusion(f32[8,256,256]{1,2,0:T(8,128)S(1)} %fusion.50, bf16[256,8,256]{0,2,1:T(8,128)(2,1)} %collective-permute-done.2, bf16[1,256,8,256]{3,2,1,0:T(8,128)(2,1)S(1)} %copy-done.3), kind=kOutput, calls=%fused_computation.47 | convolution fusion | flops 271581184 | bytes 7340032 | tf_op jit(solution)/shard_map/tbc,cbd->tbd/dot_general | solution.py:86
  53.6 24.3 %collective-permute-done.3 = bf16[256,8,256]{2,0,1:T(8,128)(2,1)} collective-permute-done((bf16[256,8,256]{2,0,1:T(8,128)(2,1)}, bf16[256,8,256]{2,0,1:T(8,128)(2,1)}, u32[]{:S(2)}, u32[]{:S(2)}) %collective-permute-start.3) | collective-permute-done | bytes 1048608 | tf_op jit(solution)/shard_map/ppermute | solution.py:19
  77.9 5.2 %all-gather.2.cloned.1.call-done = bf16[256,8,256]{2,0,1:T(8,128)(2,1)} async-done(((bf16[16,8,256]{2,0,1:T(8,128)(2,1)}), bf16[256,8,256]{2,0,1:T(8,128)(2,1)}) %all-gather.2.cloned.1.call-update) | async-done | bytes 1048592 | tf_op jit(solution)/shard_map/all_gather | solution.py:63
  83.1 4.0 %fusion.15 = bf16[256,8,256]{0,2,1:T(8,128)(2,1)S(1)} fusion(f32[8,256,256]{1,2,0:T(8,128)} %get-tuple-element.33, f32[8,256,256]{2,1,0:T(8,128)} %fusion.41, bf16[256,8,256]{2,0,1:T(8,128)(2,1)} %all-gather.2.cloned.1.call-done, bf16[256,8,256]{2,0,1:T(8,128)(2,1)} %collective-permute-done.3), kind=kOutput, calls=%fused_computation.23 | convolution fusion | flops 274202624 | bytes 7340032 | tf_op jit(solution)/shard_map/tbd,cbd->tbc/dot_general | solution.py:125
  87.1 1.0 copy-done.15
  88.1 4.3 %multiply_bitcast_fusion.2 = f32[512,8,256]{0,2,1:T(8,128)} fusion(bf16[256,8,256]{0,2,1:T(8,128)(2,1)S(1)} %fusion.15, bf16[256,8,256]{0,2,1:T(8,128)(2,1)} %collective-permute-done.2, bf16[256,8,256]{0,2,1:T(8,128)(2,1)} %get-tuple-element.30), kind=kOutput, calls=%fused_computation.2 | convolution fusion | flops 542113792 | bytes 7340032 | tf_op jit(solution)/shard_map/tbc,tbd->cbd/dot_general | solution.py:139
  92.3 5.4 %copy.147 = f32[512,8,256]{2,1,0:T(8,128)} copy(f32[512,8,256]{0,2,1:T(8,128)} %multiply_bitcast_fusion.2) | data formatting | bytes 8388608 | tf_op jit(solution)/shard_map/mul | solution.py:139
  97.9 1.8 convolution_bitcast_fusion
  100.0 5.8 %collective-permute-start.4 = (bf16[256,8,256]{0,2,1:T(8,128)(2,1)}, bf16[256,8,256]{0,2,1:T(8,128)(2,1)}, u32[]{:S(2)}, u32[]{:S(2)}) collective-permute-start(bf16[256,8,256]{0,2,1:T(8,128)(2,1)} %get-tuple-element.8), channel_id=1, source_target_pairs={{0,2},{1,3},{2,0},{3,1},{4,6},{5,7},{6,4},{7,5},{8,10},{9,11},{10,... | collective-permute-start | bytes 3145736 | tf_op jit(solution)/shard_map/ppermute | solution.py:19
  105.8 1.4 fusion.21
  107.2 0.5 fusion.44
  107.7 0.5 copy-done.6
  108.2 1.9 copy.143
  110.1 3.1 %rev.9 = f32[256,1,2,4,256]{0,4,3,2,1:T(8,128)} reverse(f32[256,1,2,4,256]{0,4,3,2,1:T(8,128)} %copy.143), dimensions={2} | reverse | bytes 4194304 | tf_op jit(solution)/shard_map/jit(_flip)/rev | solution.py:79
  113.1 2.8 bitcast_add_fusion
  116.0 35.7 %collective-permute-done.4 = bf16[256,8,256]{0,2,1:T(8,128)(2,1)} collective-permute-done((bf16[256,8,256]{0,2,1:T(8,128)(2,1)}, bf16[256,8,256]{0,2,1:T(8,128)(2,1)}, u32[]{:S(2)}, u32[]{:S(2)}) %collective-permute-start.4) | collective-permute-done | bytes 1048608 | tf_op jit(solution)/shard_map/ppermute | solution.py:19
  151.6 2.3 multiply_bitcast_fusion.1
  153.9 4.4 %copy.149 = f32[512,8,256]{2,1,0:T(8,128)} copy(f32[512,8,256]{2,0,1:T(8,128)S(1)} %multiply_bitcast_fusion.1) | data formatting | bytes 8388608 | tf_op jit(solution)/shard_map/mul | solution.py:162
  158.4 2.3 copy.152
  160.7 4.6 %multiply_bitcast_fusion = f32[512,8,256]{0,2,1:T(8,128)} fusion(bf16[256,8,256]{0,2,1:T(8,128)(2,1)} %copy-done.6, bf16[256,8,256]{2,0,1:T(8,128)(2,1)} %bitcast.138, bf16[256,8,256]{2,0,1:T(8,128)(2,1)} %copy.152), kind=kOutput, calls=%fused_computation | convolution fusion | flops 542113792 | bytes 7340032 | tf_op jit(solution)/shard_map/tbc,tbd->cbd/dot_general | solution.py:139
  165.2 5.4 %copy.153 = f32[512,8,256]{2,1,0:T(8,128)} copy(f32[512,8,256]{0,2,1:T(8,128)} %multiply_bitcast_fusion) | data formatting | bytes 8388608 | tf_op jit(solution)/shard_map/mul | solution.py:139
  170.7 2.6 copy.154
  173.3 30.7 %all_to_all.15 = f32[4,4,4,8,8,256]{5,4,3,1,0,2:T(8,128)} all-to-all(f32[4,4,4,8,8,256]{5,4,3,1,0,2:T(8,128)S(1)} %copy.154), channel_id=1, replica_groups=mesh['dy'=4,'dz'=4,'dx'=4,'tensor'=4] {'dx'}, dimensions={2} | all-to-all | bytes 8388608 | tf_op jit(solution)/shard_map/all_to_all | solution.py:42
  204.0 3.7 %reduce_sum.47 = f32[4,4,8,8,256]{4,3,2,1,0:T(8,128)} reduce(f32[4,4,4,8,8,256]{5,4,3,1,0,2:T(8,128)} %all_to_all.15, f32[]{:T(128)} %constant.7.clone.1), dimensions={2}, to_apply=%region_4.5 | reduce | flops 786432 | bytes 5242884 | tf_op jit(solution)/shard_map/reduce_sum | solution.py:42
  207.7 0.7 reduce-scatter.6.cloned.1.call-done
  208.3 1.7 pad_maximum_fusion
  210.0 1.5 copy.176
  211.5 4.3 %all-to-all-start.1 = ((f32[4,4,8,8,256]{4,3,2,1,0:T(8,128)}), f32[4,4,8,8,256]{4,3,2,1,0:T(8,128)}, u32[]{:S(2)}, u32[]{:S(2)}) async-start(f32[4,4,8,8,256]{4,3,2,1,0:T(8,128)} %reduce_sum.47), calls=%async_computation.3 | async-start | bytes 2097152 | tf_op jit(solution)/shard_map/all_to_all | solution.py:52
  215.8 2.3 copy.145
  218.1 0.3 fusion.3
  218.5 0.8 copy-done.10
  219.3 3.0 %fusion.39 = f32[8,256,256]{1,2,0:T(8,128)} fusion(bf16[256,8,256]{0,2,1:T(8,128)(2,1)} %collective-permute-done.4, bf16[1,256,8,256]{1,3,2,0:T(8,128)(2,1)S(1)} %copy-done.10), kind=kOutput, calls=%fused_computation.61 | convolution fusion | flops 268435456 | bytes 4194304 | tf_op jit(solution)/shard_map/tbc,cbd->tbd/dot_general | solution.py:86
  222.3 5.7 %collective-permute-start.8 = (f32[256]{0:T(256)S(1)}, f32[256]{0:T(256)S(1)}, u32[]{:S(2)}, u32[]{:S(2)}) collective-permute-start(f32[256]{0:T(256)S(1)} %add.101), channel_id=1, source_target_pairs={{0,2},{1,3},{2,0},{3,1},{4,6},{5,7},{6,4},{7,5},{8,10},{9,11},{10,... | collective-permute-start | bytes 3080 | tf_op jit(solution)/shard_map/ppermute | solution.py:19
  228.0 3.3 %all-to-all-done.1 = f32[4,4,8,8,256]{4,3,2,1,0:T(8,128)} async-done(((f32[4,4,8,8,256]{4,3,2,1,0:T(8,128)}), f32[4,4,8,8,256]{4,3,2,1,0:T(8,128)}, u32[]{:S(2)}, u32[]{:S(2)}) %all-to-all-start.1) | async-done | bytes 1048608 | tf_op jit(solution)/shard_map/all_to_all | solution.py:52
  231.3 1.3 reduce_sum.48
  232.6 31.2 %reduce-scatter.8.cloned.1.call-done = f32[1,512,256]{2,1,0:T(8,128)} async-done(((f32[4,512,256]{2,1,0:T(8,128)}), f32[1,512,256]{2,1,0:T(8,128)}) %reduce-scatter.8.cloned.1.call-update) | async-done | bytes 524304 | tf_op jit(solution)/shard_map/reduce_scatter | solution.py:50
  263.8 2.0 maximum_bitcast_fusion
  265.8 4.8 %all-to-all-start.2 = ((f32[4,3,8,8,256]{4,3,2,1,0:T(8,128)}), f32[4,3,8,8,256]{4,3,2,1,0:T(8,128)}, u32[]{:S(2)}, u32[]{:S(2)}) async-start(f32[4,3,8,8,256]{4,3,2,1,0:T(8,128)} %maximum_bitcast_fusion), calls=%async_computation.5 | async-start | bytes 1572864 | tf_op jit(solution)/shard_map/all_to_all | solution.py:54
  270.6 2.8 convolution_add_fusion
  273.3 1.9 fusion.7
  275.3 2.4 copy.157
  277.6 1.4 copy.158
  279.0 11.8 %all-to-all-done.2 = f32[4,3,8,8,256]{4,3,2,1,0:T(8,128)} async-done(((f32[4,3,8,8,256]{4,3,2,1,0:T(8,128)}), f32[4,3,8,8,256]{4,3,2,1,0:T(8,128)}, u32[]{:S(2)}, u32[]{:S(2)}) %all-to-all-start.2) | async-done | bytes 786464 | tf_op jit(solution)/shard_map/all_to_all | solution.py:54
  290.8 1.9 reduce_sum.49
  (59 shorter events, 1.3 us)
Async XLA Ops:
  7.2 76.0 %all-gather.2.cloned.1.call-start = ((), (), s32[]{:S(2)}) async-start(), calls=%async_computation.6 | async-start | bytes 1114112 | tf_op jit(solution)/shard_map/all_gather | solution.py:63
  9.0 7.0 %collective-permute-start = (f32[256]{0:T(256)S(1)}, f32[256]{0:T(256)S(1)}, u32[]{:S(2)}, u32[]{:S(2)}) collective-permute-start(f32[256]{0:T(256)S(1)} %fusion.8), channel_id=1, source_target_pairs={{0,1},{1,0},{2,3},{3,2},{4,5},{5,4},{6,7},{7,6},{8,9},{9,8},{10,11... | collective-permute-start | bytes 3080 | tf_op jit(solution)/shard_map/ppermute | solution.py:19
  16.0 13.7 %copy-start.9 = (bf16[1,256,8,256]{1,3,2,0:T(8,128)(2,1)}, bf16[1,256,8,256]{1,3,2,0:T(8,128)(2,1)S(1)}, u32[]{:S(2)}) copy-start(bf16[1,256,8,256]{1,3,2,0:T(8,128)(2,1)S(1)} %copy.182) | copy-start | bytes 3145732
  16.0 13.7 %collective-permute-start.1 = (f32[256]{0:T(256)S(1)}, f32[256]{0:T(256)S(1)}, u32[]{:S(2)}, u32[]{:S(2)}) collective-permute-start(f32[256]{0:T(256)S(1)} %add.80), channel_id=1, source_target_pairs={{0,2},{1,3},{2,0},{3,1},{4,6},{5,7},{6,4},{7,5},{8,10},{9,11},{10,... | collective-permute-start | bytes 3080 | tf_op jit(solution)/shard_map/ppermute | solution.py:19
  25.5 8.9 %collective-permute-start.5 = (bf16[16,8,256]{2,0,1:T(8,128)(2,1)S(1)}, bf16[16,8,256]{2,0,1:T(8,128)(2,1)S(1)}, u32[]{:S(2)}, u32[]{:S(2)}) collective-permute-start(bf16[16,8,256]{2,0,1:T(8,128)(2,1)S(1)} %bitcast.145), channel_id=1, source_target_pairs={{0,2},{1,3},{2,0},{3,1},{4,6},{5,7},{6,4},{7,5},{8,10},{9,11},{10,... | collective-permute-start | bytes 196616 | tf_op jit(solution)/shard_map/ppermute | solution.py:19
  29.9 7.0 %copy-start = (bf16[256,2048]{0,1:T(8,128)(2,1)}, bf16[256,2048]{0,1:T(8,128)(2,1)S(1)}, u32[]{:S(2)}) copy-start(bf16[256,2048]{0,1:T(8,128)(2,1)S(1)} %fusion.2) | copy-start | bytes 3145732
  32.5 4.4 %copy-start.4 = (bf16[256,1,2,4,256]{4,0,3,2,1:T(8,128)(2,1)}, bf16[256,1,2,4,256]{4,0,3,2,1:T(8,128)(2,1)S(1)}, u32[]{:S(2)}) copy-start(bf16[256,1,2,4,256]{4,0,3,2,1:T(8,128)(2,1)S(1)} %rev.8) | copy-start | bytes 3145732
  34.4 0.6 copy-start.18
  35.0 172.6 %reduce-scatter.4.cloned.1.call-start = ((), (), s32[]{:S(2)}) async-start(), calls=%async_computation.7 | async-start | bytes 5242880 | tf_op jit(solution)/shard_map/reduce_scatter | solution.py:33
  35.1 1.8 copy-start.5
  36.9 2.3 copy-start.1
  39.2 10.7 %collective-permute-start.2 = (bf16[256,8,256]{0,2,1:T(8,128)(2,1)}, bf16[256,8,256]{0,2,1:T(8,128)(2,1)}, u32[]{:S(2)}, u32[]{:S(2)}) collective-permute-start(bf16[256,8,256]{0,2,1:T(8,128)(2,1)} %get-tuple-element.30), channel_id=1, source_target_pairs={{0,1},{1,0},{2,3},{3,2},{4,5},{5,4},{6,7},{7,6},{8,9},{9,8},{10,11... | collective-permute-start | bytes 3145736 | tf_op jit(solution)/shard_map/ppermute | solution.py:19
  40.3 37.7 %collective-permute-start.3 = (bf16[256,8,256]{2,0,1:T(8,128)(2,1)}, bf16[256,8,256]{2,0,1:T(8,128)(2,1)}, u32[]{:S(2)}, u32[]{:S(2)}) collective-permute-start(bf16[256,8,256]{2,0,1:T(8,128)(2,1)} %bitcast.127), channel_id=1, source_target_pairs={{0,2},{1,3},{2,0},{3,1},{4,6},{5,7},{6,4},{7,5},{8,10},{9,11},{10,... | collective-permute-start | bytes 3145736 | tf_op jit(solution)/shard_map/ppermute | solution.py:19
  46.0 1.9 copy-start.7
  46.0 2.0 copy-start.13
  48.1 1.8 copy-start.3
  87.1 1.0 copy-start.15
  97.8 8.0 %copy-start.14 = (bf16[1,256,8,256]{3,2,1,0:T(8,128)(2,1)S(1)}, bf16[1,256,8,256]{3,2,1,0:T(8,128)(2,1)}, u32[]{:S(2)}) copy-start(bf16[1,256,8,256]{3,2,1,0:T(8,128)(2,1)} %get-tuple-element.23) | copy-start | bytes 3145732
  97.8 110.5 %reduce-scatter.6.cloned.1.call-start = ((), (), s32[]{:S(2)}) async-start(), calls=%async_computation.8 | async-start | bytes 5242880 | tf_op jit(solution)/shard_map/reduce_scatter | solution.py:33
  97.9 8.0 %copy-start.16 = (bf16[256,8,256]{0,2,1:T(8,128)(2,1)S(1)}, bf16[256,8,256]{0,2,1:T(8,128)(2,1)}, u32[]{:S(2)}) copy-start(bf16[256,8,256]{0,2,1:T(8,128)(2,1)} %copy-done.15) | copy-start | bytes 3145732
  97.9 8.0 %copy-start.17 = (f32[8,256,256]{1,2,0:T(8,128)S(1)}, f32[8,256,256]{1,2,0:T(8,128)}, u32[]{:S(2)}) copy-start(f32[8,256,256]{1,2,0:T(8,128)} %get-tuple-element.31) | copy-start | bytes 6291460
  99.7 6.1 %collective-permute-start.6 = (f32[256,8,256]{0,2,1:T(8,128)S(1)}, f32[256,8,256]{0,2,1:T(8,128)S(1)}, u32[]{:S(2)}, u32[]{:S(2)}) collective-permute-start(f32[256,8,256]{0,2,1:T(8,128)S(1)} %convolution_bitcast_fusion), channel_id=1, source_target_pairs={{0,1},{1,0},{2,3},{3,2},{4,5},{5,4},{6,7},{7,6},{8,9},{9,8},{10,11... | collective-permute-start | bytes 6291464 | tf_op jit(solution)/shard_map/ppermute | solution.py:19
  100.0 51.7 %collective-permute-start.4 = (bf16[256,8,256]{0,2,1:T(8,128)(2,1)}, bf16[256,8,256]{0,2,1:T(8,128)(2,1)}, u32[]{:S(2)}, u32[]{:S(2)}) collective-permute-start(bf16[256,8,256]{0,2,1:T(8,128)(2,1)} %get-tuple-element.8), channel_id=1, source_target_pairs={{0,2},{1,3},{2,0},{3,1},{4,6},{5,7},{6,4},{7,5},{8,10},{9,11},{10,... | collective-permute-start | bytes 3145736 | tf_op jit(solution)/shard_map/ppermute | solution.py:19
  105.8 1.4 copy-start.8
  107.2 1.0 copy-start.6
  113.1 38.5 %copy-start.2 = (bf16[256,2048]{1,0:T(8,128)(2,1)S(1)}, bf16[256,2048]{1,0:T(8,128)(2,1)}, u32[]{:S(2)}) copy-start(bf16[256,2048]{1,0:T(8,128)(2,1)} %param.5) | copy-start | bytes 3145732
  158.4 105.4 %reduce-scatter.8.cloned.1.call-start = ((), (), s32[]{:S(2)}) async-start(), calls=%async_computation.9 | async-start | bytes 2621440 | tf_op jit(solution)/shard_map/reduce_scatter | solution.py:50
  211.5 19.8 %all-to-all-start.1 = ((f32[4,4,8,8,256]{4,3,2,1,0:T(8,128)}), f32[4,4,8,8,256]{4,3,2,1,0:T(8,128)}, u32[]{:S(2)}, u32[]{:S(2)}) async-start(f32[4,4,8,8,256]{4,3,2,1,0:T(8,128)} %reduce_sum.47), calls=%async_computation.3 | async-start | bytes 2097152 | tf_op jit(solution)/shard_map/all_to_all | solution.py:52
  218.1 1.2 copy-start.10
  218.4 3.9 %collective-permute-start.7 = (f32[256]{0:T(256)S(1)}, f32[256]{0:T(256)S(1)}, u32[]{:S(2)}, u32[]{:S(2)}) collective-permute-start(f32[256]{0:T(256)S(1)} %fusion.3), channel_id=1, source_target_pairs={{0,1},{1,0},{2,3},{3,2},{4,5},{5,4},{6,7},{7,6},{8,9},{9,8},{10,11... | collective-permute-start | bytes 3080 | tf_op jit(solution)/shard_map/ppermute | solution.py:19
  222.3 51.0 %collective-permute-start.8 = (f32[256]{0:T(256)S(1)}, f32[256]{0:T(256)S(1)}, u32[]{:S(2)}, u32[]{:S(2)}) collective-permute-start(f32[256]{0:T(256)S(1)} %add.101), channel_id=1, source_target_pairs={{0,2},{1,3},{2,0},{3,1},{4,6},{5,7},{6,4},{7,5},{8,10},{9,11},{10,... | collective-permute-start | bytes 3080 | tf_op jit(solution)/shard_map/ppermute | solution.py:19
  265.8 25.1 %all-to-all-start.2 = ((f32[4,3,8,8,256]{4,3,2,1,0:T(8,128)}), f32[4,3,8,8,256]{4,3,2,1,0:T(8,128)}, u32[]{:S(2)}, u32[]{:S(2)}) async-start(f32[4,3,8,8,256]{4,3,2,1,0:T(8,128)} %maximum_bitcast_fusion), calls=%async_computation.5 | async-start | bytes 1572864 | tf_op jit(solution)/shard_map/all_to_all | solution.py:54
  270.6 2.8 copy-start.11
  275.3 2.4 copy-start.12
Sparse Core Ops, SparseCore 0:
  35.1 47.9 all-gather.1
  97.9 58.2 reduce-scatter.3
  158.9 49.3 reduce-scatter.5
  211.6 52.1 reduce-scatter.7

commit v10 on v9

--- a/solution.py
+++ b/solution.py
@@ -46,9 +46,7 @@
     nz, nx, share = on_sc[0].shape[:3]
     rest = on_sc[0].shape[3:]
     a, on_tc = lax.optimization_barrier((jnp.stack(on_sc, axis=0), on_tc))
-    a = jnp.moveaxis(a, 2, 0)
-    a = lax.psum_scatter(a.reshape(nx, -1, rest[-1]), "dx", scatter_dimension=0, tiled=True)
-    a = a.reshape((len(on_sc), nz, share) + rest)
+    a = jnp.sum(lax.all_to_all(a, "dx", 2, 2), axis=2)
     b = jnp.sum(lax.all_to_all(on_tc, "dy", 0, 0), axis=0)
     g = jnp.moveaxis(jnp.concatenate([b[None], a], axis=0), 1, 0)
     return jnp.sum(lax.all_to_all(g, "dz", 0, 0), axis=0)

time: 302 us -> 317 us (1.050)
  waiting for transfers between devices: 114 us -> 87.2 us
  starting transfers between devices: 32.7 us -> 54.6 us
  blocking collectives: 30.7 us -> 49.3 us
    reduce_scatter x1 -> x0, waiting for transfers between devices: 31.2 us -> none  [scatter_rest(): lax.psum_scatter(a.reshape(nx, -1, rest[-1]), 'dx', scatter_dimension=0,...]
    all_to_all x1, starting transfers between devices: 4.8 us -> 26.1 us  [scatter_rest(): return jnp.sum(lax.all_to_all(g, 'dz', 0, 0), axis=0)]
    all_to_all x0 -> x1, blocking collectives: none -> 18.6 us  [scatter_rest(): b = jnp.sum(lax.all_to_all(on_tc, 'dy', 0, 0), axis=0)]
    all_to_all x1, waiting for transfers between devices: 3.27 us -> 10.4 us  [scatter_rest(): a = jnp.sum(lax.all_to_all(a, 'dx', 2, 2), axis=2)]
    unnamed x46 -> x48, local copies, waits for them, and re-layouts: 17.9 us -> 18 us
  transfers between devices with their start and end apart: 15 -> 14, of which waited for: 8 -> 7; matrix products, arithmetic and copies ran while one was open for 28% -> 27% of each run, Pallas kernels for 0% -> 0%
where the time goes in v10:
time: 317 us; the launch traced here: 316 us
  waiting for transfers between devices  87.2 us (28%)
  local copies, waits for them, and re-layouts  56.7 us (18%)
  starting transfers between devices  54.6 us (17%)
  blocking collectives  49.3 us (16%)
  matrix products  38.7 us (12%)
  other arithmetic  15 us (5%)
  between operations  14.1 us (4%)
    ppermute x9, waiting for transfers between devices, swapped(): lax.ppermute(x, axis, [(i, i ^ 1 << stride) for i in range(lax.axis_size(...  62.2 us
    all_to_all x1, blocking collectives, exchange_first(): return jnp.sum(lax.all_to_all(g, 'dx', 2, 2), axis=2)  30.7 us
    all_to_all x1, starting transfers between devices, scatter_rest(): return jnp.sum(lax.all_to_all(g, 'dz', 0, 0), axis=0)  26.1 us
    ppermute x9, starting transfers between devices, swapped(): lax.ppermute(x, axis, [(i, i ^ 1 << stride) for i in range(lax.axis_size(...  23.4 us
    all_to_all x1, blocking collectives, scatter_rest(): b = jnp.sum(lax.all_to_all(on_tc, 'dy', 0, 0), axis=0)  18.6 us
    unnamed x48, local copies, waits for them, and re-layouts  18 us
    mul x2, local copies, waits for them, and re-layouts, shards(): jnp.einsum('tbc,tbd->cbd', joined, grad_pre, preferred_element_type=jnp.f...  10.9 us
    all_to_all x1, waiting for transfers between devices, scatter_rest(): a = jnp.sum(lax.all_to_all(a, 'dx', 2, 2), axis=2)  10.4 us
  transfers between devices with their start and end apart: 14, of which 7 were waited for; matrix products, arithmetic and copies ran while one was open for 27% of the time, Pallas kernels for 0%

profile of v10, /device:TPU:2, one launch (start us, length us, event | category | flops | bytes accessed | tf_op | source)
XLA Modules:
  0.0 315.5 jit_solution(14291913942892600892)
XLA Ops:
  7.2 1.5 copy.155
  9.1 5.2 %fusion.54 = (bf16[1,256,8,256]{3,2,1,0:T(8,128)(2,1)}, bf16[1,256,8,256]{3,2,1,0:T(8,128)(2,1)}, bf16[1,256,8,256]{3,2,1,0:T(8,128)(2,1)}, bf16[1,256,8,256]{3,...) fusion(bf16[3,512,8,256]{3,2,1,0:T(8,128)(2,1)} %param.4), kind=kLoop, calls=%fused_computation.80 | loop fusion | bytes 12582912 | tf_op jit(solution)/shard_map/slice | solution.py:85
  14.3 1.6 copy.219
  16.0 7.3 %collective-permute-start.1 = (f32[256]{0:T(256)S(1)}, f32[256]{0:T(256)S(1)}, u32[]{:S(2)}, u32[]{:S(2)}) collective-permute-start(f32[256]{0:T(256)S(1)} %add.78), channel_id=1, source_target_pairs={{0,2},{1,3},{2,0},{3,1},{4,6},{5,7},{6,4},{7,5},{8,10},{9,11},{10,... | collective-permute-start | bytes 3080 | tf_op jit(solution)/shard_map/ppermute | solution.py:19
  23.3 1.0 constant_dynamic-slice_fusion
  24.3 1.2 copy.172
  25.6 2.4 copy.216
  28.0 1.6 copy.215
  29.8 1.3 copy.158
  31.1 1.3 rev.8
  32.4 1.9 collective-permute-done.5
  34.4 0.6 copy-done.19
  35.1 1.8 fusion.46
  36.9 2.3 fusion.38
  39.2 1.0 copy.232
  40.3 4.1 %collective-permute-start.3 = (bf16[256,8,256]{2,0,1:T(8,128)(2,1)}, bf16[256,8,256]{2,0,1:T(8,128)(2,1)}, u32[]{:S(2)}, u32[]{:S(2)}) collective-permute-start(bf16[256,8,256]{2,0,1:T(8,128)(2,1)} %bitcast.121), channel_id=1, source_target_pairs={{0,2},{1,3},{2,0},{3,1},{4,6},{5,7},{6,4},{7,5},{8,10},{9,11},{10,... | collective-permute-start | bytes 3145736 | tf_op jit(solution)/shard_map/ppermute | solution.py:19
  44.3 1.6 copy.214
  46.0 1.8 fusion.41
  48.0 1.8 fusion.50
  49.8 3.7 %fusion.34 = (bf16[256,8,256]{0,2,1:T(8,128)(2,1)}, f32[8,256,256]{1,2,0:T(8,128)}) fusion(f32[8,256,256]{1,2,0:T(8,128)S(1)} %fusion.50, bf16[256,8,256]{0,2,1:T(8,128)(2,1)} %collective-permute-done.2, bf16[1,256,8,256]{3,2,1,0:T(8,128)(2,1)S(1)} %copy-done.3), kind=kOutput, calls=%fused_computation.47 | convolution fusion | flops 271581184 | bytes 7340032 | tf_op jit(solution)/shard_map/tbc,cbd->tbd/dot_general | solution.py:84
  53.5 24.6 %collective-permute-done.3 = bf16[256,8,256]{2,0,1:T(8,128)(2,1)} collective-permute-done((bf16[256,8,256]{2,0,1:T(8,128)(2,1)}, bf16[256,8,256]{2,0,1:T(8,128)(2,1)}, u32[]{:S(2)}, u32[]{:S(2)}) %collective-permute-start.3) | collective-permute-done | bytes 1048608 | tf_op jit(solution)/shard_map/ppermute | solution.py:19
  78.1 5.0 %all-gather.2.cloned.1.call-done = bf16[256,8,256]{2,0,1:T(8,128)(2,1)} async-done(((bf16[16,8,256]{2,0,1:T(8,128)(2,1)}), bf16[256,8,256]{2,0,1:T(8,128)(2,1)}) %all-gather.2.cloned.1.call-update) | async-done | bytes 1048592 | tf_op jit(solution)/shard_map/all_gather | solution.py:61
  83.0 4.0 %fusion.15 = bf16[256,8,256]{0,2,1:T(8,128)(2,1)S(1)} fusion(f32[8,256,256]{1,2,0:T(8,128)} %get-tuple-element.36, f32[8,256,256]{2,1,0:T(8,128)} %fusion.41, bf16[256,8,256]{2,0,1:T(8,128)(2,1)} %all-gather.2.cloned.1.call-done, bf16[256,8,256]{2,0,1:T(8,128)(2,1)} %collective-permute-done.3), kind=kOutput, calls=%fused_computation.23 | convolution fusion | flops 274202624 | bytes 7340032 | tf_op jit(solution)/shard_map/tbd,cbd->tbc/dot_general | solution.py:123
  87.0 1.0 copy-done.15
  88.0 4.3 %multiply_bitcast_fusion.2 = f32[512,8,256]{0,2,1:T(8,128)} fusion(bf16[256,8,256]{0,2,1:T(8,128)(2,1)S(1)} %fusion.15, bf16[256,8,256]{0,2,1:T(8,128)(2,1)} %collective-permute-done.2, bf16[256,8,256]{0,2,1:T(8,128)(2,1)} %get-tuple-element.33), kind=kOutput, calls=%fused_computation.2 | convolution fusion | flops 542113792 | bytes 7340032 | tf_op jit(solution)/shard_map/tbc,tbd->cbd/dot_general | solution.py:137
  92.3 5.4 %copy.185 = f32[512,8,256]{2,1,0:T(8,128)} copy(f32[512,8,256]{0,2,1:T(8,128)} %multiply_bitcast_fusion.2) | data formatting | bytes 8388608 | tf_op jit(solution)/shard_map/mul | solution.py:137
  97.8 1.8 convolution_bitcast_fusion
  99.9 5.8 %collective-permute-start.4 = (bf16[256,8,256]{0,2,1:T(8,128)(2,1)}, bf16[256,8,256]{0,2,1:T(8,128)(2,1)}, u32[]{:S(2)}, u32[]{:S(2)}) collective-permute-start(bf16[256,8,256]{0,2,1:T(8,128)(2,1)} %get-tuple-element.8), channel_id=1, source_target_pairs={{0,2},{1,3},{2,0},{3,1},{4,6},{5,7},{6,4},{7,5},{8,10},{9,11},{10,... | collective-permute-start | bytes 3145736 | tf_op jit(solution)/shard_map/ppermute | solution.py:19
  105.8 1.4 fusion.21
  107.2 0.5 fusion.44
  107.7 0.5 copy-done.6
  108.1 1.9 copy.181
  110.0 3.1 rev.9
  113.1 2.8 bitcast_add_fusion
  115.9 35.7 %collective-permute-done.4 = bf16[256,8,256]{0,2,1:T(8,128)(2,1)} collective-permute-done((bf16[256,8,256]{0,2,1:T(8,128)(2,1)}, bf16[256,8,256]{0,2,1:T(8,128)(2,1)}, u32[]{:S(2)}, u32[]{:S(2)}) %collective-permute-start.4) | collective-permute-done | bytes 1048608 | tf_op jit(solution)/shard_map/ppermute | solution.py:19
  151.6 2.3 multiply_bitcast_fusion.1
  153.8 4.4 %copy.187 = f32[512,8,256]{2,1,0:T(8,128)} copy(f32[512,8,256]{2,0,1:T(8,128)S(1)} %multiply_bitcast_fusion.1) | data formatting | bytes 8388608 | tf_op jit(solution)/shard_map/mul | solution.py:160
  158.3 2.3 copy.190
  160.5 4.5 %multiply_bitcast_fusion = f32[512,8,256]{0,2,1:T(8,128)} fusion(bf16[256,8,256]{0,2,1:T(8,128)(2,1)} %copy-done.6, bf16[256,8,256]{2,0,1:T(8,128)(2,1)} %bitcast.132, bf16[256,8,256]{2,0,1:T(8,128)(2,1)} %copy.190), kind=kOutput, calls=%fused_computation | convolution fusion | flops 542113792 | bytes 7340032 | tf_op jit(solution)/shard_map/tbc,tbd->cbd/dot_general | solution.py:137
  165.1 5.4 %copy.191 = f32[512,8,256]{2,1,0:T(8,128)} copy(f32[512,8,256]{0,2,1:T(8,128)} %multiply_bitcast_fusion) | data formatting | bytes 8388608 | tf_op jit(solution)/shard_map/mul | solution.py:137
  170.5 2.7 copy.192
  173.2 30.7 %all_to_all.20 = f32[4,4,4,8,8,256]{5,4,3,1,0,2:T(8,128)} all-to-all(f32[4,4,4,8,8,256]{5,4,3,1,0,2:T(8,128)S(1)} %copy.192), channel_id=1, replica_groups=mesh['dy'=4,'dz'=4,'dx'=4,'tensor'=4] {'dx'}, dimensions={2} | all-to-all | bytes 8388608 | tf_op jit(solution)/shard_map/all_to_all | solution.py:42
  203.9 3.7 %reduce_sum.56 = f32[4,4,8,8,256]{4,3,2,1,0:T(8,128)} reduce(f32[4,4,4,8,8,256]{5,4,3,1,0,2:T(8,128)} %all_to_all.20, f32[]{:T(128)} %constant.7.clone.1), dimensions={2}, to_apply=%region_4.5 | reduce | flops 786432 | bytes 5242884 | tf_op jit(solution)/shard_map/reduce_sum | solution.py:42
  207.5 0.7 reduce-scatter.5.cloned.1.call-done
  208.3 1.7 pad_maximum_fusion
  210.0 1.4 copy.213
  211.6 18.6 %all_to_all.21 = f32[4,4,8,8,256]{4,3,2,1,0:T(8,128)} all-to-all(f32[4,4,8,8,256]{4,3,2,1,0:T(8,128)S(1)} %copy-done.17), channel_id=1, replica_groups=mesh['dy'=4,'dz'=4,'dx'=4,'tensor'=4] {'dy'}, dimensions={0} | all-to-all | bytes 2097152 | tf_op jit(solution)/shard_map/all_to_all | solution.py:50
  230.1 5.0 %all-to-all-start.2 = ((f32[2,4,4,8,8,256]{5,4,3,1,0,2:T(8,128)}), f32[2,4,4,8,8,256]{5,4,3,1,0,2:T(8,128)}, u32[]{:S(2)}, u32[]{:S(2)}) async-start(f32[2,4,4,8,8,256]{5,4,3,1,0,2:T(8,128)} %copy.213), calls=%async_computation.4 | async-start | bytes 4194304 | tf_op jit(solution)/shard_map/all_to_all | solution.py:49
  235.1 2.3 copy.183
  237.8 0.8 copy-done.10
  238.6 3.0 fusion.39
  241.6 5.7 %collective-permute-start.8 = (f32[256]{0:T(256)S(1)}, f32[256]{0:T(256)S(1)}, u32[]{:S(2)}, u32[]{:S(2)}) collective-permute-start(f32[256]{0:T(256)S(1)} %add.99), channel_id=1, source_target_pairs={{0,2},{1,3},{2,0},{3,1},{4,6},{5,7},{6,4},{7,5},{8,10},{9,11},{10,... | collective-permute-start | bytes 3080 | tf_op jit(solution)/shard_map/ppermute | solution.py:19
  247.3 1.3 reduce_sum.57
  248.6 10.4 %all-to-all-done.2 = f32[2,4,4,8,8,256]{5,4,3,1,0,2:T(8,128)} async-done(((f32[2,4,4,8,8,256]{5,4,3,1,0,2:T(8,128)}), f32[2,4,4,8,8,256]{5,4,3,1,0,2:T(8,128)}, u32[]{:S(2)}, u32[]{:S(2)}) %all-to-all-start.2) | async-done | bytes 2097184 | tf_op jit(solution)/shard_map/all_to_all | solution.py:49
  259.0 2.6 reduce_sum.58
  261.6 1.1 maximum_bitcast_fusion
  262.7 0.9 copy.193
  263.7 26.1 %all-to-all-start.3 = ((f32[4,3,8,8,256]{4,3,2,1,0:T(8,128)}), f32[4,3,8,8,256]{4,3,2,1,0:T(8,128)}, u32[]{:S(2)}, u32[]{:S(2)}) async-start(f32[4,3,8,8,256]{4,3,2,1,0:T(8,128)} %copy.193), calls=%async_computation.5 | async-start | bytes 1572864 | tf_op jit(solution)/shard_map/all_to_all | solution.py:52
  289.7 2.8 convolution_add_fusion
  292.5 1.9 fusion.7
  294.5 2.4 copy.194
  296.8 1.4 copy.195
  298.2 8.9 %all-to-all-done.3 = f32[4,3,8,8,256]{4,3,2,1,0:T(8,128)} async-done(((f32[4,3,8,8,256]{4,3,2,1,0:T(8,128)}), f32[4,3,8,8,256]{4,3,2,1,0:T(8,128)}, u32[]{:S(2)}, u32[]{:S(2)}) %all-to-all-start.3) | async-done | bytes 786464 | tf_op jit(solution)/shard_map/all_to_all | solution.py:52
  307.1 1.9 reduce_sum.59
  (61 shorter events, 2.0 us)
Async XLA Ops:
  7.2 75.9 %all-gather.2.cloned.1.call-start = ((), (), s32[]{:S(2)}) async-start(), calls=%async_computation.6 | async-start | bytes 1114112 | tf_op jit(solution)/shard_map/all_gather | solution.py:61
  9.0 7.0 %collective-permute-start = (f32[256]{0:T(256)S(1)}, f32[256]{0:T(256)S(1)}, u32[]{:S(2)}, u32[]{:S(2)}) collective-permute-start(f32[256]{0:T(256)S(1)} %fusion.8), channel_id=1, source_target_pairs={{0,1},{1,0},{2,3},{3,2},{4,5},{5,4},{6,7},{7,6},{8,9},{9,8},{10,11... | collective-permute-start | bytes 3080 | tf_op jit(solution)/shard_map/ppermute | solution.py:19
  16.0 13.6 %copy-start.9 = (bf16[1,256,8,256]{1,3,2,0:T(8,128)(2,1)}, bf16[1,256,8,256]{1,3,2,0:T(8,128)(2,1)S(1)}, u32[]{:S(2)}) copy-start(bf16[1,256,8,256]{1,3,2,0:T(8,128)(2,1)S(1)} %copy.219) | copy-start | bytes 3145732
  16.0 13.6 %collective-permute-start.1 = (f32[256]{0:T(256)S(1)}, f32[256]{0:T(256)S(1)}, u32[]{:S(2)}, u32[]{:S(2)}) collective-permute-start(f32[256]{0:T(256)S(1)} %add.78), channel_id=1, source_target_pairs={{0,2},{1,3},{2,0},{3,1},{4,6},{5,7},{6,4},{7,5},{8,10},{9,11},{10,... | collective-permute-start | bytes 3080 | tf_op jit(solution)/shard_map/ppermute | solution.py:19
  25.5 8.9 %collective-permute-start.5 = (bf16[16,8,256]{2,0,1:T(8,128)(2,1)S(1)}, bf16[16,8,256]{2,0,1:T(8,128)(2,1)S(1)}, u32[]{:S(2)}, u32[]{:S(2)}) collective-permute-start(bf16[16,8,256]{2,0,1:T(8,128)(2,1)S(1)} %bitcast.137), channel_id=1, source_target_pairs={{0,2},{1,3},{2,0},{3,1},{4,6},{5,7},{6,4},{7,5},{8,10},{9,11},{10,... | collective-permute-start | bytes 196616 | tf_op jit(solution)/shard_map/ppermute | solution.py:19
  29.8 7.1 %copy-start = (bf16[256,2048]{0,1:T(8,128)(2,1)}, bf16[256,2048]{0,1:T(8,128)(2,1)S(1)}, u32[]{:S(2)}) copy-start(bf16[256,2048]{0,1:T(8,128)(2,1)S(1)} %fusion.2) | copy-start | bytes 3145732
  32.4 4.5 %copy-start.4 = (bf16[256,1,2,4,256]{4,0,3,2,1:T(8,128)(2,1)}, bf16[256,1,2,4,256]{4,0,3,2,1:T(8,128)(2,1)S(1)}, u32[]{:S(2)}) copy-start(bf16[256,1,2,4,256]{4,0,3,2,1:T(8,128)(2,1)S(1)} %rev.8) | copy-start | bytes 3145732
  34.4 0.6 copy-start.19
  35.0 172.5 %reduce-scatter.3.cloned.1.call-start = ((), (), s32[]{:S(2)}) async-start(), calls=%async_computation.7 | async-start | bytes 5242880 | tf_op jit(solution)/shard_map/reduce_scatter | solution.py:33
  35.1 1.8 copy-start.5
  36.9 2.3 copy-start.1
  39.2 10.6 %collective-permute-start.2 = (bf16[256,8,256]{0,2,1:T(8,128)(2,1)}, bf16[256,8,256]{0,2,1:T(8,128)(2,1)}, u32[]{:S(2)}, u32[]{:S(2)}) collective-permute-start(bf16[256,8,256]{0,2,1:T(8,128)(2,1)} %get-tuple-element.33), channel_id=1, source_target_pairs={{0,1},{1,0},{2,3},{3,2},{4,5},{5,4},{6,7},{7,6},{8,9},{9,8},{10,11... | collective-permute-start | bytes 3145736 | tf_op jit(solution)/shard_map/ppermute | solution.py:19
  40.3 37.8 %collective-permute-start.3 = (bf16[256,8,256]{2,0,1:T(8,128)(2,1)}, bf16[256,8,256]{2,0,1:T(8,128)(2,1)}, u32[]{:S(2)}, u32[]{:S(2)}) collective-permute-start(bf16[256,8,256]{2,0,1:T(8,128)(2,1)} %bitcast.121), channel_id=1, source_target_pairs={{0,2},{1,3},{2,0},{3,1},{4,6},{5,7},{6,4},{7,5},{8,10},{9,11},{10,... | collective-permute-start | bytes 3145736 | tf_op jit(solution)/shard_map/ppermute | solution.py:19
  46.0 1.8 copy-start.7
  46.0 2.0 copy-start.13
  48.0 1.8 copy-start.3
  87.0 1.0 copy-start.15
  97.7 8.0 %copy-start.14 = (bf16[1,256,8,256]{3,2,1,0:T(8,128)(2,1)S(1)}, bf16[1,256,8,256]{3,2,1,0:T(8,128)(2,1)}, u32[]{:S(2)}) copy-start(bf16[1,256,8,256]{3,2,1,0:T(8,128)(2,1)} %get-tuple-element.26) | copy-start | bytes 3145732
  97.7 110.5 %reduce-scatter.5.cloned.1.call-start = ((), (), s32[]{:S(2)}) async-start(), calls=%async_computation.8 | async-start | bytes 5242880 | tf_op jit(solution)/shard_map/reduce_scatter | solution.py:33
  97.8 8.0 %copy-start.16 = (bf16[256,8,256]{0,2,1:T(8,128)(2,1)S(1)}, bf16[256,8,256]{0,2,1:T(8,128)(2,1)}, u32[]{:S(2)}) copy-start(bf16[256,8,256]{0,2,1:T(8,128)(2,1)} %copy-done.15) | copy-start | bytes 3145732
  97.8 8.0 %copy-start.18 = (f32[8,256,256]{1,2,0:T(8,128)S(1)}, f32[8,256,256]{1,2,0:T(8,128)}, u32[]{:S(2)}) copy-start(f32[8,256,256]{1,2,0:T(8,128)} %get-tuple-element.34) | copy-start | bytes 6291460
  99.6 6.1 %collective-permute-start.6 = (f32[256,8,256]{0,2,1:T(8,128)S(1)}, f32[256,8,256]{0,2,1:T(8,128)S(1)}, u32[]{:S(2)}, u32[]{:S(2)}) collective-permute-start(f32[256,8,256]{0,2,1:T(8,128)S(1)} %convolution_bitcast_fusion), channel_id=1, source_target_pairs={{0,1},{1,0},{2,3},{3,2},{4,5},{5,4},{6,7},{7,6},{8,9},{9,8},{10,11... | collective-permute-start | bytes 6291464 | tf_op jit(solution)/shard_map/ppermute | solution.py:19
  99.9 51.7 %collective-permute-start.4 = (bf16[256,8,256]{0,2,1:T(8,128)(2,1)}, bf16[256,8,256]{0,2,1:T(8,128)(2,1)}, u32[]{:S(2)}, u32[]{:S(2)}) collective-permute-start(bf16[256,8,256]{0,2,1:T(8,128)(2,1)} %get-tuple-element.8), channel_id=1, source_target_pairs={{0,2},{1,3},{2,0},{3,1},{4,6},{5,7},{6,4},{7,5},{8,10},{9,11},{10,... | collective-permute-start | bytes 3145736 | tf_op jit(solution)/shard_map/ppermute | solution.py:19
  105.8 1.4 copy-start.8
  107.1 1.0 copy-start.6
  113.1 38.5 %copy-start.2 = (bf16[256,2048]{1,0:T(8,128)(2,1)S(1)}, bf16[256,2048]{1,0:T(8,128)(2,1)}, u32[]{:S(2)}) copy-start(bf16[256,2048]{1,0:T(8,128)(2,1)} %param.5) | copy-start | bytes 3145732
  209.9 1.6 copy-start.17
  230.1 28.9 %all-to-all-start.2 = ((f32[2,4,4,8,8,256]{5,4,3,1,0,2:T(8,128)}), f32[2,4,4,8,8,256]{5,4,3,1,0,2:T(8,128)}, u32[]{:S(2)}, u32[]{:S(2)}) async-start(f32[2,4,4,8,8,256]{5,4,3,1,0,2:T(8,128)} %copy.213), calls=%async_computation.4 | async-start | bytes 4194304 | tf_op jit(solution)/shard_map/all_to_all | solution.py:49
  237.4 1.2 copy-start.10
  237.7 3.9 %collective-permute-start.7 = (f32[256]{0:T(256)S(1)}, f32[256]{0:T(256)S(1)}, u32[]{:S(2)}, u32[]{:S(2)}) collective-permute-start(f32[256]{0:T(256)S(1)} %fusion.3), channel_id=1, source_target_pairs={{0,1},{1,0},{2,3},{3,2},{4,5},{5,4},{6,7},{7,6},{8,9},{9,8},{10,11... | collective-permute-start | bytes 3080 | tf_op jit(solution)/shard_map/ppermute | solution.py:19
  241.6 50.9 %collective-permute-start.8 = (f32[256]{0:T(256)S(1)}, f32[256]{0:T(256)S(1)}, u32[]{:S(2)}, u32[]{:S(2)}) collective-permute-start(f32[256]{0:T(256)S(1)} %add.99), channel_id=1, source_target_pairs={{0,2},{1,3},{2,0},{3,1},{4,6},{5,7},{6,4},{7,5},{8,10},{9,11},{10,... | collective-permute-start | bytes 3080 | tf_op jit(solution)/shard_map/ppermute | solution.py:19
  263.7 43.4 %all-to-all-start.3 = ((f32[4,3,8,8,256]{4,3,2,1,0:T(8,128)}), f32[4,3,8,8,256]{4,3,2,1,0:T(8,128)}, u32[]{:S(2)}, u32[]{:S(2)}) async-start(f32[4,3,8,8,256]{4,3,2,1,0:T(8,128)} %copy.193), calls=%async_computation.5 | async-start | bytes 1572864 | tf_op jit(solution)/shard_map/all_to_all | solution.py:52
  289.7 2.8 copy-start.11
  294.5 2.4 copy-start.12
Sparse Core Ops, SparseCore 0:
  35.1 47.8 all-gather.1
  97.8 58.2 reduce-scatter.2
  158.9 49.3 reduce-scatter.4

commit v11 on v9

--- a/solution.py
+++ b/solution.py
@@ -154,7 +154,9 @@
         if factor > 0:
             previous = stored_preact[factor - 1]
             grad_pre = (grad_hidden * gelu_slope(previous)).astype(jnp.bfloat16)
-    partner_top, _ = lax.optimization_barrier((partner_top, grad_hidden))
+    partner_top, _, grad_terms[0] = lax.optimization_barrier(
+        (partner_top, grad_hidden, grad_terms[0])
+    )
     preact = apply_factor(hidden, partner_top, top_weights)
     mixed = (tokens_f32 + preact.reshape(tok_rows, local_width)).astype(jnp.bfloat16)
     joined = jnp.concatenate([hidden, partner_top], axis=2)

time: 302 us -> 316 us (1.046)
  waiting for transfers between devices: 114 us -> 152 us
  blocking collectives: 30.7 us -> 0 us
  starting transfers between devices: 32.7 us -> 38 us
    reduce_scatter x2, waiting for transfers between devices: 0.68 us -> 56.8 us  [scatter_first(): lax.psum_scatter(grads.reshape(ny, -1, rest[-1]), 'dy', scatter_dimension...]
    all_to_all x0 -> x1, waiting for transfers between devices: none -> 34.1 us  [exchange_first(): return jnp.sum(lax.all_to_all(g, 'dx', 2, 2), axis=2)]
    ppermute x9, waiting for transfers between devices: 61.9 us -> 29.5 us  [swapped(): lax.ppermute(x, axis, [(i, i ^ 1 << stride) for i in range(lax.axis_size(...]
    all_to_all x1 -> x0, blocking collectives: 30.7 us -> none  [exchange_first(): return jnp.sum(lax.all_to_all(g, 'dx', 2, 2), axis=2)]
    reduce_scatter x1, waiting for transfers between devices: 31.2 us -> 9.78 us  [scatter_rest(): lax.psum_scatter(a.reshape(nx, -1, rest[-1]), 'dx', scatter_dimension=0,...]
    all_to_all x0 -> x1, starting transfers between devices: none -> 5.89 us  [exchange_first(): return jnp.sum(lax.all_to_all(g, 'dx', 2, 2), axis=2)]
    unnamed x46 -> x36, local copies, waits for them, and re-layouts: 17.9 us -> 17.2 us
  transfers between devices with their start and end apart: 15 -> 16, of which waited for: 8 -> 10; matrix products, arithmetic and copies ran while one was open for 28% -> 27% of each run, Pallas kernels for 0% -> 0%
where the time goes in v11:
time: 316 us; the launch traced here: 314 us
  waiting for transfers between devices  152 us (48%)
  local copies, waits for them, and re-layouts  54.4 us (17%)
  matrix products  41.8 us (13%)
  starting transfers between devices  38 us (12%)
  between operations  14 us (4%)
  other arithmetic  13.3 us (4%)
    reduce_scatter x2, waiting for transfers between devices, scatter_first(): lax.psum_scatter(grads.reshape(ny, -1, rest[-1]), 'dy', scatter_dimension...  56.8 us
    all_to_all x1, waiting for transfers between devices, exchange_first(): return jnp.sum(lax.all_to_all(g, 'dx', 2, 2), axis=2)  34.1 us
    ppermute x9, waiting for transfers between devices, swapped(): lax.ppermute(x, axis, [(i, i ^ 1 << stride) for i in range(lax.axis_size(...  29.5 us
    ppermute x9, starting transfers between devices, swapped(): lax.ppermute(x, axis, [(i, i ^ 1 << stride) for i in range(lax.axis_size(...  23 us
    unnamed x36, local copies, waits for them, and re-layouts  17.2 us
    mul x2, local copies, waits for them, and re-layouts, shards(): jnp.einsum('tbc,tbd->cbd', joined, grad_pre, preferred_element_type=jnp.f...  10.9 us
    all_to_all x1, waiting for transfers between devices, scatter_rest(): return jnp.sum(lax.all_to_all(g, 'dz', 0, 0), axis=0)  10.7 us
    reduce_scatter x1, waiting for transfers between devices, scatter_rest(): lax.psum_scatter(a.reshape(nx, -1, rest[-1]), 'dx', scatter_dimension=0,...  9.78 us
  transfers between devices with their start and end apart: 16, of which 10 were waited for; matrix products, arithmetic and copies ran while one was open for 27% of the time, Pallas kernels for 0%

profile of v11, /device:TPU:2, one launch (start us, length us, event | category | flops | bytes accessed | tf_op | source)
XLA Modules:
  0.0 313.6 jit_solution(13144303240102357673)
XLA Ops:
  7.2 1.5 copy.117
  8.7 0.3 fusion.8
  9.1 5.3 %fusion.54 = (bf16[1,256,8,256]{3,2,1,0:T(8,128)(2,1)}, bf16[1,256,8,256]{3,2,1,0:T(8,128)(2,1)}, bf16[1,256,8,256]{3,2,1,0:T(8,128)(2,1)}, bf16[1,256,8,256]{3,...) fusion(bf16[3,512,8,256]{3,2,1,0:T(8,128)(2,1)} %param.4), kind=kLoop, calls=%fused_computation.80 | loop fusion | bytes 12582912 | tf_op jit(solution)/shard_map/slice | solution.py:87
  14.4 1.6 copy.182
  16.0 7.3 %collective-permute-start.1 = (f32[256]{0:T(256)S(1)}, f32[256]{0:T(256)S(1)}, u32[]{:S(2)}, u32[]{:S(2)}) collective-permute-start(f32[256]{0:T(256)S(1)} %add.80), channel_id=1, source_target_pairs={{0,2},{1,3},{2,0},{3,1},{4,6},{5,7},{6,4},{7,5},{8,10},{9,11},{10,... | collective-permute-start | bytes 3080 | tf_op jit(solution)/shard_map/ppermute | solution.py:19
  23.3 1.0 constant_dynamic-slice_fusion
  24.3 1.2 copy.134
  25.6 2.4 copy.179
  28.1 1.6 copy.178
  29.9 1.3 copy.120
  31.2 1.3 rev.8
  32.5 1.9 collective-permute-done.5
  34.4 0.6 copy-done.13
  35.1 1.8 fusion.46
  36.9 2.3 fusion.38
  39.2 1.0 copy.197
  40.3 4.0 %collective-permute-start.3 = (bf16[256,8,256]{2,0,1:T(8,128)(2,1)}, bf16[256,8,256]{2,0,1:T(8,128)(2,1)}, u32[]{:S(2)}, u32[]{:S(2)}) collective-permute-start(bf16[256,8,256]{2,0,1:T(8,128)(2,1)} %bitcast.127), channel_id=1, source_target_pairs={{0,2},{1,3},{2,0},{3,1},{4,6},{5,7},{6,4},{7,5},{8,10},{9,11},{10,... | collective-permute-start | bytes 3145736 | tf_op jit(solution)/shard_map/ppermute | solution.py:19
  44.3 2.4 copy.177
  46.7 3.2 %fusion.41 = f32[8,256,256]{2,1,0:T(8,128)} fusion(bf16[1,256,8,256]{1,3,2,0:T(8,128)(2,1)} %copy.177, bf16[32,8,8,256]{3,2,1,0:T(8,128)(2,1)S(1)} %bitcast.136), kind=kOutput, calls=%fused_computation.63 | convolution fusion | flops 268435456 | bytes 4194304 | tf_op jit(solution)/shard_map/tbd,cbd->tbc/dot_general | solution.py:123
  49.9 1.8 fusion.50
  51.7 3.6 %fusion.34 = (bf16[256,8,256]{0,2,1:T(8,128)(2,1)}, f32[8,256,256]{1,2,0:T(8,128)}) fusion(f32[8,256,256]{1,2,0:T(8,128)S(1)} %fusion.50, bf16[256,8,256]{0,2,1:T(8,128)(2,1)} %collective-permute-done.2, bf16[1,256,8,256]{3,2,1,0:T(8,128)(2,1)S(1)} %copy-done.1), kind=kOutput, calls=%fused_computation.47 | convolution fusion | flops 271581184 | bytes 7340032 | tf_op jit(solution)/shard_map/tbc,cbd->tbd/dot_general | solution.py:86
  55.4 22.4 %collective-permute-done.3 = bf16[256,8,256]{2,0,1:T(8,128)(2,1)} collective-permute-done((bf16[256,8,256]{2,0,1:T(8,128)(2,1)}, bf16[256,8,256]{2,0,1:T(8,128)(2,1)}, u32[]{:S(2)}, u32[]{:S(2)}) %collective-permute-start.3) | collective-permute-done | bytes 1048608 | tf_op jit(solution)/shard_map/ppermute | solution.py:19
  77.8 5.2 %all-gather.2.cloned.1.call-done = bf16[256,8,256]{2,0,1:T(8,128)(2,1)} async-done(((bf16[16,8,256]{2,0,1:T(8,128)(2,1)}), bf16[256,8,256]{2,0,1:T(8,128)(2,1)}) %all-gather.2.cloned.1.call-update) | async-done | bytes 1048592 | tf_op jit(solution)/shard_map/all_gather | solution.py:63
  83.0 4.0 %fusion.15 = bf16[256,8,256]{0,2,1:T(8,128)(2,1)S(1)} fusion(f32[8,256,256]{1,2,0:T(8,128)} %get-tuple-element.35, f32[8,256,256]{2,1,0:T(8,128)} %fusion.41, bf16[256,8,256]{2,0,1:T(8,128)(2,1)} %all-gather.2.cloned.1.call-done, bf16[256,8,256]{2,0,1:T(8,128)(2,1)} %collective-permute-done.3), kind=kOutput, calls=%fused_computation.23 | convolution fusion | flops 274202624 | bytes 7340032 | tf_op jit(solution)/shard_map/tbd,cbd->tbc/dot_general | solution.py:125
  87.0 1.0 copy-done.12
  88.0 4.3 %multiply_bitcast_fusion.1 = f32[512,8,256]{0,2,1:T(8,128)} fusion(bf16[256,8,256]{0,2,1:T(8,128)(2,1)S(1)} %fusion.15, bf16[256,8,256]{0,2,1:T(8,128)(2,1)} %collective-permute-done.2, bf16[256,8,256]{0,2,1:T(8,128)(2,1)} %get-tuple-element.32), kind=kOutput, calls=%fused_computation.1 | convolution fusion | flops 542113792 | bytes 7340032 | tf_op jit(solution)/shard_map/tbc,tbd->cbd/dot_general | solution.py:139
  92.3 5.4 %copy.150 = f32[512,8,256]{2,1,0:T(8,128)} copy(f32[512,8,256]{0,2,1:T(8,128)} %multiply_bitcast_fusion.1) | data formatting | bytes 8388608 | tf_op jit(solution)/shard_map/mul | solution.py:139
  97.7 3.0 convolution_bitcast_fusion
  100.8 0.5 copy.144
  101.3 4.0 %collective-permute-done.6 = f32[256,8,256]{0,2,1:T(8,128)} collective-permute-done((f32[256,8,256]{0,2,1:T(8,128)}, f32[256,8,256]{0,2,1:T(8,128)}, u32[]{:S(2)}, u32[]{:S(2)}) %collective-permute-start.6) | collective-permute-done | bytes 2097184 | tf_op jit(solution)/shard_map/ppermute | solution.py:19
  105.3 4.1 %fusion.21 = bf16[256,8,256]{0,2,1:T(8,128)(2,1)S(1)} fusion(f32[256,8,256]{0,2,1:T(8,128)} %collective-permute-done.6, f32[8,256,256]{1,2,0:T(8,128)} %get-tuple-element.33, bf16[256,8,256]{0,2,1:T(8,128)(2,1)} %copy-done.12, bf16[1,256,8,256]{3,2,1,0:T(8,128)(2,1)} %get-tuple-element.25), kind=kOutput, calls=%fused_computation.29 | convolution fusion | flops 274202624 | bytes 7340032 | tf_op jit(solution)/shard_map/tbd,cbd->tbc/dot_general | solution.py:143
  109.4 2.7 multiply_bitcast_fusion.2
  112.1 5.5 %copy.145 = f32[512,8,256]{2,1,0:T(8,128)} copy(f32[512,8,256]{0,2,1:T(8,128)} %multiply_bitcast_fusion.2) | data formatting | bytes 8388608 | tf_op jit(solution)/shard_map/mul | solution.py:139
  117.6 5.2 %copy.146 = f32[4,4,4,8,8,256]{5,4,3,1,0,2:T(8,128)} copy(f32[4,4,4,8,8,256]{5,4,3,2,1,0:T(8,128)} %bitcast.133) | data formatting | bytes 8388608 | tf_op jit(solution)/shard_map/reshape | solution.py:41
  122.8 5.9 %all-to-all-start = ((f32[4,4,4,8,8,256]{5,4,3,1,0,2:T(8,128)}), f32[4,4,4,8,8,256]{5,4,3,1,0,2:T(8,128)}, u32[]{:S(2)}, u32[]{:S(2)}) async-start(f32[4,4,4,8,8,256]{5,4,3,1,0,2:T(8,128)} %copy.146), calls=%async_computation | async-start | bytes 8388608 | tf_op jit(solution)/shard_map/all_to_all | solution.py:42
  128.7 5.6 %collective-permute-start.4 = (bf16[256,8,256]{0,2,1:T(8,128)(2,1)}, bf16[256,8,256]{0,2,1:T(8,128)(2,1)}, u32[]{:S(2)}, u32[]{:S(2)}) collective-permute-start(bf16[256,8,256]{0,2,1:T(8,128)(2,1)} %get-tuple-element.9), channel_id=1, source_target_pairs={{0,2},{1,3},{2,0},{3,1},{4,6},{5,7},{6,4},{7,5},{8,10},{9,11},{10,... | collective-permute-start | bytes 3145736 | tf_op jit(solution)/shard_map/ppermute | solution.py:19
  134.3 1.8 fusion.44
  136.2 2.0 copy.143
  138.1 1.6 rev.9
  139.7 2.7 bitcast_add_fusion
  142.4 34.1 %all-to-all-done = f32[4,4,4,8,8,256]{5,4,3,1,0,2:T(8,128)} async-done(((f32[4,4,4,8,8,256]{5,4,3,1,0,2:T(8,128)}), f32[4,4,4,8,8,256]{5,4,3,1,0,2:T(8,128)}, u32[]{:S(2)}, u32[]{:S(2)}) %all-to-all-start) | async-done | bytes 4194336 | tf_op jit(solution)/shard_map/all_to_all | solution.py:42
  176.5 3.6 %reduce_sum.46 = f32[4,4,8,8,256]{4,3,2,1,0:T(8,128)} reduce(f32[4,4,4,8,8,256]{5,4,3,1,0,2:T(8,128)} %all-to-all-done, f32[]{:T(128)} %constant.7.clone.1), dimensions={2}, to_apply=%region_1.2 | reduce | flops 786432 | bytes 5242884 | tf_op jit(solution)/shard_map/reduce_sum | solution.py:42
  180.1 2.6 multiply_bitcast_fusion
  182.7 4.4 %copy.152 = f32[512,8,256]{2,1,0:T(8,128)} copy(f32[512,8,256]{2,0,1:T(8,128)S(1)} %multiply_bitcast_fusion) | data formatting | bytes 8388608 | tf_op jit(solution)/shard_map/mul | solution.py:164
  187.2 56.8 %reduce-scatter.6.cloned.1.call-done = f32[1,1024,256]{2,1,0:T(8,128)} async-done(((f32[4,1024,256]{2,1,0:T(8,128)}), f32[1,1024,256]{2,1,0:T(8,128)}) %reduce-scatter.6.cloned.1.call-update) | async-done | bytes 1048592 | tf_op jit(solution)/shard_map/reduce_scatter | solution.py:33
  244.0 1.7 pad_maximum_fusion
  245.7 1.5 copy.176
  247.2 4.3 %all-to-all-start.1 = ((f32[4,4,8,8,256]{4,3,2,1,0:T(8,128)}), f32[4,4,8,8,256]{4,3,2,1,0:T(8,128)}, u32[]{:S(2)}, u32[]{:S(2)}) async-start(f32[4,4,8,8,256]{4,3,2,1,0:T(8,128)} %reduce_sum.46), calls=%async_computation.3 | async-start | bytes 2097152 | tf_op jit(solution)/shard_map/all_to_all | solution.py:52
  251.4 0.3 fusion.3
  251.9 1.1 collective-permute-done.7
  253.0 5.7 %collective-permute-start.8 = (f32[256]{0:T(256)S(1)}, f32[256]{0:T(256)S(1)}, u32[]{:S(2)}, u32[]{:S(2)}) collective-permute-start(f32[256]{0:T(256)S(1)} %add.101), channel_id=1, source_target_pairs={{0,2},{1,3},{2,0},{3,1},{4,6},{5,7},{6,4},{7,5},{8,10},{9,11},{10,... | collective-permute-start | bytes 3080 | tf_op jit(solution)/shard_map/ppermute | solution.py:19
  258.7 2.3 copy.148
  261.0 5.9 %all-to-all-done.1 = f32[4,4,8,8,256]{4,3,2,1,0:T(8,128)} async-done(((f32[4,4,8,8,256]{4,3,2,1,0:T(8,128)}), f32[4,4,8,8,256]{4,3,2,1,0:T(8,128)}, u32[]{:S(2)}, u32[]{:S(2)}) %all-to-all-start.1) | async-done | bytes 1048608 | tf_op jit(solution)/shard_map/all_to_all | solution.py:52
  266.9 1.3 reduce_sum.48
  268.3 9.8 %reduce-scatter.8.cloned.1.call-done = f32[1,512,256]{2,1,0:T(8,128)} async-done(((f32[4,512,256]{2,1,0:T(8,128)}), f32[1,512,256]{2,1,0:T(8,128)}) %reduce-scatter.8.cloned.1.call-update) | async-done | bytes 524304 | tf_op jit(solution)/shard_map/reduce_scatter | solution.py:50
  278.0 2.0 maximum_bitcast_fusion
  280.1 4.8 %all-to-all-start.2 = ((f32[4,3,8,8,256]{4,3,2,1,0:T(8,128)}), f32[4,3,8,8,256]{4,3,2,1,0:T(8,128)}, u32[]{:S(2)}, u32[]{:S(2)}) async-start(f32[4,3,8,8,256]{4,3,2,1,0:T(8,128)} %maximum_bitcast_fusion), calls=%async_computation.5 | async-start | bytes 1572864 | tf_op jit(solution)/shard_map/all_to_all | solution.py:54
  284.9 2.1 fusion.39
  287.0 1.8 convolution_add_fusion
  288.8 1.9 fusion.7
  290.7 2.4 copy.157
  293.0 1.4 copy.158
  294.5 10.7 %all-to-all-done.2 = f32[4,3,8,8,256]{4,3,2,1,0:T(8,128)} async-done(((f32[4,3,8,8,256]{4,3,2,1,0:T(8,128)}), f32[4,3,8,8,256]{4,3,2,1,0:T(8,128)}, u32[]{:S(2)}, u32[]{:S(2)}) %all-to-all-start.2) | async-done | bytes 786464 | tf_op jit(solution)/shard_map/all_to_all | solution.py:54
  305.1 1.9 reduce_sum.49
  (50 shorter events, 0.8 us)
Async XLA Ops:
  7.2 75.9 %all-gather.2.cloned.1.call-start = ((), (), s32[]{:S(2)}) async-start(), calls=%async_computation.6 | async-start | bytes 1114112 | tf_op jit(solution)/shard_map/all_gather | solution.py:63
  9.0 7.0 %collective-permute-start = (f32[256]{0:T(256)S(1)}, f32[256]{0:T(256)S(1)}, u32[]{:S(2)}, u32[]{:S(2)}) collective-permute-start(f32[256]{0:T(256)S(1)} %fusion.8), channel_id=1, source_target_pairs={{0,1},{1,0},{2,3},{3,2},{4,5},{5,4},{6,7},{7,6},{8,9},{9,8},{10,11... | collective-permute-start | bytes 3080 | tf_op jit(solution)/shard_map/ppermute | solution.py:19
  16.0 13.6 %copy-start.8 = (bf16[1,256,8,256]{1,3,2,0:T(8,128)(2,1)}, bf16[1,256,8,256]{1,3,2,0:T(8,128)(2,1)S(1)}, u32[]{:S(2)}) copy-start(bf16[1,256,8,256]{1,3,2,0:T(8,128)(2,1)S(1)} %copy.182) | copy-start | bytes 3145732
  16.0 13.6 %collective-permute-start.1 = (f32[256]{0:T(256)S(1)}, f32[256]{0:T(256)S(1)}, u32[]{:S(2)}, u32[]{:S(2)}) collective-permute-start(f32[256]{0:T(256)S(1)} %add.80), channel_id=1, source_target_pairs={{0,2},{1,3},{2,0},{3,1},{4,6},{5,7},{6,4},{7,5},{8,10},{9,11},{10,... | collective-permute-start | bytes 3080 | tf_op jit(solution)/shard_map/ppermute | solution.py:19
  25.5 8.9 %collective-permute-start.5 = (bf16[16,8,256]{2,0,1:T(8,128)(2,1)S(1)}, bf16[16,8,256]{2,0,1:T(8,128)(2,1)S(1)}, u32[]{:S(2)}, u32[]{:S(2)}) collective-permute-start(bf16[16,8,256]{2,0,1:T(8,128)(2,1)S(1)} %bitcast.145), channel_id=1, source_target_pairs={{0,2},{1,3},{2,0},{3,1},{4,6},{5,7},{6,4},{7,5},{8,10},{9,11},{10,... | collective-permute-start | bytes 196616 | tf_op jit(solution)/shard_map/ppermute | solution.py:19
  32.5 4.4 %copy-start.3 = (bf16[256,1,2,4,256]{4,0,3,2,1:T(8,128)(2,1)}, bf16[256,1,2,4,256]{4,0,3,2,1:T(8,128)(2,1)S(1)}, u32[]{:S(2)}) copy-start(bf16[256,1,2,4,256]{4,0,3,2,1:T(8,128)(2,1)S(1)} %rev.8) | copy-start | bytes 3145732
  34.4 0.6 copy-start.13
  35.0 152.2 %reduce-scatter.4.cloned.1.call-start = ((), (), s32[]{:S(2)}) async-start(), calls=%async_computation.7 | async-start | bytes 5242880 | tf_op jit(solution)/shard_map/reduce_scatter | solution.py:33
  35.1 1.8 copy-start.2
  36.9 2.3 copy-start
  39.2 12.5 %collective-permute-start.2 = (bf16[256,8,256]{0,2,1:T(8,128)(2,1)}, bf16[256,8,256]{0,2,1:T(8,128)(2,1)}, u32[]{:S(2)}, u32[]{:S(2)}) collective-permute-start(bf16[256,8,256]{0,2,1:T(8,128)(2,1)} %get-tuple-element.32), channel_id=1, source_target_pairs={{0,1},{1,0},{2,3},{3,2},{4,5},{5,4},{6,7},{7,6},{8,9},{9,8},{10,11... | collective-permute-start | bytes 3145736 | tf_op jit(solution)/shard_map/ppermute | solution.py:19
  40.3 37.5 %collective-permute-start.3 = (bf16[256,8,256]{2,0,1:T(8,128)(2,1)}, bf16[256,8,256]{2,0,1:T(8,128)(2,1)}, u32[]{:S(2)}, u32[]{:S(2)}) collective-permute-start(bf16[256,8,256]{2,0,1:T(8,128)(2,1)} %bitcast.127), channel_id=1, source_target_pairs={{0,2},{1,3},{2,0},{3,1},{4,6},{5,7},{6,4},{7,5},{8,10},{9,11},{10,... | collective-permute-start | bytes 3145736 | tf_op jit(solution)/shard_map/ppermute | solution.py:19
  46.7 3.2 %copy-start.11 = (bf16[1,256,8,256]{3,2,1,0:T(8,128)(2,1)S(1)}, bf16[1,256,8,256]{3,2,1,0:T(8,128)(2,1)}, u32[]{:S(2)}) copy-start(bf16[1,256,8,256]{3,2,1,0:T(8,128)(2,1)} %get-tuple-element.25) | copy-start | bytes 3145732
  49.9 1.8 copy-start.1
  87.0 1.0 copy-start.12
  100.8 4.5 %collective-permute-start.6 = (f32[256,8,256]{0,2,1:T(8,128)}, f32[256,8,256]{0,2,1:T(8,128)}, u32[]{:S(2)}, u32[]{:S(2)}) collective-permute-start(f32[256,8,256]{0,2,1:T(8,128)} %convolution_bitcast_fusion), channel_id=1, source_target_pairs={{0,1},{1,0},{2,3},{3,2},{4,5},{5,4},{6,7},{7,6},{8,9},{9,8},{10,11... | collective-permute-start | bytes 6291464 | tf_op jit(solution)/shard_map/ppermute | solution.py:19
  105.3 4.1 %copy-start.4 = (bf16[256,1,2,4,256]{4,0,3,2,1:T(8,128)(2,1)S(1)}, bf16[256,1,2,4,256]{4,0,3,2,1:T(8,128)(2,1)}, u32[]{:S(2)}) copy-start(bf16[256,1,2,4,256]{4,0,3,2,1:T(8,128)(2,1)} %copy-done.3) | copy-start | bytes 3145732
  109.4 24.9 %copy-start.5 = (bf16[256,8,256]{0,2,1:T(8,128)(2,1)}, bf16[256,8,256]{0,2,1:T(8,128)(2,1)S(1)}, u32[]{:S(2)}) copy-start(bf16[256,8,256]{0,2,1:T(8,128)(2,1)S(1)} %fusion.21) | copy-start | bytes 3145732
  122.8 11.5 %copy-start.7 = (bf16[1,256,8,256]{1,3,2,0:T(8,128)(2,1)S(1)}, bf16[1,256,8,256]{1,3,2,0:T(8,128)(2,1)}, u32[]{:S(2)}) copy-start(bf16[1,256,8,256]{1,3,2,0:T(8,128)(2,1)} %copy.179) | copy-start | bytes 3145732
  122.8 53.7 %all-to-all-start = ((f32[4,4,4,8,8,256]{5,4,3,1,0,2:T(8,128)}), f32[4,4,4,8,8,256]{5,4,3,1,0,2:T(8,128)}, u32[]{:S(2)}, u32[]{:S(2)}) async-start(f32[4,4,4,8,8,256]{5,4,3,1,0,2:T(8,128)} %copy.146), calls=%async_computation | async-start | bytes 8388608 | tf_op jit(solution)/shard_map/all_to_all | solution.py:42
  128.7 115.3 %reduce-scatter.6.cloned.1.call-start = ((), (), s32[]{:S(2)}) async-start(), calls=%async_computation.8 | async-start | bytes 5242880 | tf_op jit(solution)/shard_map/reduce_scatter | solution.py:33
  128.7 51.4 %collective-permute-start.4 = (bf16[256,8,256]{0,2,1:T(8,128)(2,1)}, bf16[256,8,256]{0,2,1:T(8,128)(2,1)}, u32[]{:S(2)}, u32[]{:S(2)}) collective-permute-start(bf16[256,8,256]{0,2,1:T(8,128)(2,1)} %get-tuple-element.9), channel_id=1, source_target_pairs={{0,2},{1,3},{2,0},{3,1},{4,6},{5,7},{6,4},{7,5},{8,10},{9,11},{10,... | collective-permute-start | bytes 3145736 | tf_op jit(solution)/shard_map/ppermute | solution.py:19
  187.1 90.9 %reduce-scatter.8.cloned.1.call-start = ((), (), s32[]{:S(2)}) async-start(), calls=%async_computation.9 | async-start | bytes 2621440 | tf_op jit(solution)/shard_map/reduce_scatter | solution.py:50
  247.2 19.8 %all-to-all-start.1 = ((f32[4,4,8,8,256]{4,3,2,1,0:T(8,128)}), f32[4,4,8,8,256]{4,3,2,1,0:T(8,128)}, u32[]{:S(2)}, u32[]{:S(2)}) async-start(f32[4,4,8,8,256]{4,3,2,1,0:T(8,128)} %reduce_sum.46), calls=%async_computation.3 | async-start | bytes 2097152 | tf_op jit(solution)/shard_map/all_to_all | solution.py:52
  251.8 1.2 collective-permute-start.7
  253.0 8.0 %collective-permute-start.8 = (f32[256]{0:T(256)S(1)}, f32[256]{0:T(256)S(1)}, u32[]{:S(2)}, u32[]{:S(2)}) collective-permute-start(f32[256]{0:T(256)S(1)} %add.101), channel_id=1, source_target_pairs={{0,2},{1,3},{2,0},{3,1},{4,6},{5,7},{6,4},{7,5},{8,10},{9,11},{10,... | collective-permute-start | bytes 3080 | tf_op jit(solution)/shard_map/ppermute | solution.py:19
  280.1 25.1 %all-to-all-start.2 = ((f32[4,3,8,8,256]{4,3,2,1,0:T(8,128)}), f32[4,3,8,8,256]{4,3,2,1,0:T(8,128)}, u32[]{:S(2)}, u32[]{:S(2)}) async-start(f32[4,3,8,8,256]{4,3,2,1,0:T(8,128)} %maximum_bitcast_fusion), calls=%async_computation.5 | async-start | bytes 1572864 | tf_op jit(solution)/shard_map/all_to_all | solution.py:54
  284.9 2.1 copy-start.6
  287.0 1.8 copy-start.9
  290.7 2.4 copy-start.10
Sparse Core Ops, SparseCore 0:
  35.2 47.8 all-gather.1
  97.9 58.2 reduce-scatter.3
  187.2 56.6 reduce-scatter.5
  247.3 30.7 reduce-scatter.7
